TPU v7x, 256 devices: a whole 4x4x8 slice. The times are simulated.
256 devices in a mesh: ctx: 64 (over y, z, core), head: 4 (over x).
Axes of the slice: x: 4, y: 4, z: 8, core: 2. Of those that a mesh axis runs over, the one named last changes fastest.
Arguments:
- linear_query: bfloat16 [16384, 8192], P('ctx', 'head'), may hold values from -6 to 6
- linear_key: bfloat16 [16384, 8192], P('ctx', 'head'), may hold values from -6 to 6
- linear_value: bfloat16 [16384, 8192], P('ctx', 'head'), may hold values from -6 to 6
- log_decay: float32 [64, 16384], P('head', 'ctx'), may hold values from -1.2 to 0, as said below
- norm_gain: float32 [8192], P('head'), may hold values from 0.25 to 1.75
- soft_query: bfloat16 [16384, 8192], P('ctx', 'head'), may hold values from -4.5 to 4.5
- soft_key: bfloat16 [16384, 8192], P('ctx', 'head'), may hold values from -4.5 to 4.5
- soft_value: bfloat16 [16384, 8192], P('ctx', 'head'), may hold values from -6 to 6
- block_index: int32 [128, 5], P('ctx'), may hold values from 0 to 127, as said below
- block_count: int32 [128], P('ctx'), may hold values from 1 to 5, as said below
Outputs:
- linear_rows: bfloat16 [16384, 8192], P(('ctx', 'head'))
- softmax_rows: bfloat16 [16384, 8192], P(('ctx', 'head'))
Inputs may be any that keep to these rules, and one draw needn't show every extreme that they name: `block_index`: entry 0 of row r is r itself; entries 1 to block_count[r] - 1 are distinct blocks from r - 4 to r - 1, and the farthest of them, r - 4, is named in some row; the entries from block_count[r] on equal r. `block_count`: at most r + 1 for row r; 5 in some row. `log_decay`: strictly negative.
All inputs are finite; a program needn't handle non-finite values.
Results may differ from a plain program's by a relative error of at most 0.0057.
Values may be sent and summed in bfloat16 or wider, within the bound.
No kernel may reach another device: no remote copies, remote signals or barrier semaphores. Data moves between devices by JAX's collectives and lax.ppermute only.
A program may use at most 192 MiB of HBM per device.

v0:
```python
import math

import jax
import jax.numpy as jnp
from jax import lax
from jax.sharding import PartitionSpec as P

BLK = 128
WIN_SEC = 2


EPS = 1e-06


def carried_in(value, axis, join, neutral):
    count, mine = (lax.axis_size(axis), lax.axis_index(axis))
    pieces = jax.tree.map(lambda part: lax.all_gather(part, axis), value)
    subtotal = jax.tree.map(
        lambda part, zero: jnp.full_like(part, 0) + jnp.asarray(zero, part.dtype), value, neutral
    )

    def step(position, subtotal):
        longer = join(subtotal, jax.tree.map(lambda part: part[position], pieces))
        return jax.tree.map(lambda new, old: jnp.where(position < mine, new, old), longer, subtotal)

    return lax.fori_loop(0, count - 1, step, subtotal)


def passed_along(block, axis, distance):
    devices = range(lax.axis_size(axis))
    route = [(i - distance, i) for i in devices if i - distance in devices]
    return lax.ppermute(block, axis, route)


def causal_mask(length):
    rows_iota = lax.broadcasted_iota(jnp.int32, (length, length), 0)
    cols_iota = lax.broadcasted_iota(jnp.int32, (length, length), 1)
    return cols_iota <= rows_iota


def to_blocks(matrix, heads):
    length, columns = matrix.shape
    return matrix.reshape(length // BLK, BLK, heads, columns // heads)


def block_state(carried, keys_blk, values_blk, cumul_blk, total_blk):
    factor = jnp.exp(total_blk[:, None] - cumul_blk).T
    decayed = (keys_blk.astype(jnp.float32) * factor[:, :, None]).astype(jnp.bfloat16)
    update = jnp.einsum("jhd,jhe->hde", decayed, values_blk, preferred_element_type=jnp.float32)
    return jnp.exp(total_blk)[:, None, None] * carried + update


def block_output(carried, query_blk, keys_blk, values_blk, cumul_blk):
    scores = jnp.einsum("thd,jhd->htj", query_blk, keys_blk, preferred_element_type=jnp.float32)
    differ = cumul_blk[:, :, None] - cumul_blk[:, None, :]
    allowed = causal_mask(query_blk.shape[0])
    weights = jnp.where(allowed[None], jnp.exp(jnp.minimum(differ, 0.0)), 0.0)
    mixing = (scores * weights).astype(jnp.bfloat16)
    inside = jnp.einsum("htj,jhd->thd", mixing, values_blk, preferred_element_type=jnp.float32)
    decayed_query = (query_blk.astype(jnp.float32) * jnp.exp(cumul_blk).T[:, :, None]).astype(
        jnp.bfloat16
    )
    across = jnp.einsum(
        "thd,hde->the",
        decayed_query,
        carried.astype(jnp.bfloat16),
        preferred_element_type=jnp.float32,
    )
    return inside + across


def combine_states(earlier, later):
    return (earlier[0] * later[0], later[0][:, None, None] * earlier[1] + later[1])


def carry_in(final, section_total):
    identity = (jnp.ones(section_total.shape, jnp.float32), jnp.zeros_like(final))
    result = carried_in((jnp.exp(section_total), final), "ctx", combine_states, identity)
    return result[1]


def linear_layer(linear_query, linear_key, linear_value, log_decay, norm_gain):
    length, columns = linear_query.shape
    heads = log_decay.shape[0]
    width = columns // heads
    blocks_here = length // BLK
    query_blocks = to_blocks(linear_query, heads)
    keys_blocks = to_blocks(linear_key, heads)
    values_blocks = to_blocks(linear_value, heads)
    per_block = log_decay.reshape(heads, blocks_here, BLK).transpose(1, 0, 2)
    cumulative = jnp.cumsum(per_block, axis=2)
    totals = cumulative[:, :, -1]
    section_cum = jnp.cumsum(log_decay, axis=1)
    section_total = section_cum[:, -1]
    start = jnp.zeros((heads, width, width), jnp.float32)

    def advance_both(carried, pieces):
        query_blk, keys_blk, values_blk, cumul_blk, total_blk = pieces
        output = block_output(carried, query_blk, keys_blk, values_blk, cumul_blk)
        return (block_state(carried, keys_blk, values_blk, cumul_blk, total_blk), output)

    final, outputs = lax.scan(
        advance_both, start, (query_blocks, keys_blocks, values_blocks, cumulative, totals)
    )
    incoming = carry_in(final, section_total)
    queries_flat = linear_query.reshape(length, heads, width)
    scaled = (queries_flat.astype(jnp.float32) * jnp.exp(section_cum).T[:, :, None]).astype(
        jnp.bfloat16
    )
    raw = outputs.reshape(length, heads, width) + jnp.einsum(
        "thd,hde->the", scaled, incoming.astype(jnp.bfloat16), preferred_element_type=jnp.float32
    )
    square_mean = jnp.mean(raw * raw, axis=2, keepdims=True)
    normed = raw * lax.rsqrt(square_mean + EPS) * norm_gain.reshape(heads, width)
    return normed.astype(jnp.bfloat16).reshape(length, columns)


def attend(query_blk, keys_sel, values_sel, index_row, count_row, row_global):
    width = query_blk.shape[-1]
    inverse_root = 1.0 / math.sqrt(width)
    scores = (
        jnp.einsum("thd,kjhd->htkj", query_blk, keys_sel, preferred_element_type=jnp.float32)
        * inverse_root
    )
    slot_used = jnp.arange(index_row.shape[0], dtype=jnp.int32) < count_row
    off_diagonal = jnp.logical_not(index_row == row_global)
    allowed = slot_used[None, :, None] & (
        off_diagonal[None, :, None] | causal_mask(query_blk.shape[0])[:, None, :]
    )
    scores = jnp.where(allowed[None], scores, -jnp.inf)
    highest = jnp.max(scores, axis=(2, 3), keepdims=True)
    raised = jnp.exp(scores - highest)
    weights = (raised / jnp.sum(raised, axis=(2, 3), keepdims=True)).astype(jnp.bfloat16)
    output = jnp.einsum("htkj,kjhd->thd", weights, values_sel, preferred_element_type=jnp.float32)
    return output.astype(jnp.bfloat16)


def softmax_layer(soft_query, soft_key, soft_value, block_index, block_count, heads):
    length, columns = soft_query.shape
    per_section = length // BLK
    own_pair = (soft_key, soft_value)
    pieces = []
    for distance in range(WIN_SEC, 0, -1):
        pieces.append(passed_along((own_pair[0], own_pair[1]), "ctx", distance))
    window_key = jnp.concatenate([piece[0] for piece in pieces] + [soft_key], axis=0)
    window_value = jnp.concatenate([piece[1] for piece in pieces] + [soft_value], axis=0)
    key_blocks = to_blocks(window_key, heads)
    value_blocks = to_blocks(window_value, heads)
    section = lax.axis_index("ctx")
    first_block = (section - WIN_SEC) * per_section
    query_blocks = to_blocks(soft_query, heads)
    own_rows = section * per_section + jnp.arange(per_section, dtype=jnp.int32)

    def one_block(inputs):
        query_blk, index_row, count_row, row_global = inputs
        local_row = index_row - first_block
        keys_sel = jnp.take(key_blocks, local_row, axis=0)
        values_sel = jnp.take(value_blocks, local_row, axis=0)
        return attend(query_blk, keys_sel, values_sel, index_row, count_row, row_global)

    outputs = lax.map(one_block, (query_blocks, block_index, block_count, own_rows))
    return outputs.reshape(length, columns)


def local(
    linear_query,
    linear_key,
    linear_value,
    log_decay,
    norm_gain,
    soft_query,
    soft_key,
    soft_value,
    block_index,
    block_count,
):
    heads = log_decay.shape[0]
    linear_heads = linear_layer(linear_query, linear_key, linear_value, log_decay, norm_gain)
    softmax_heads = softmax_layer(soft_query, soft_key, soft_value, block_index, block_count, heads)
    result = (
        lax.all_to_all(linear_heads, "head", split_axis=0, concat_axis=1, tiled=True),
        lax.all_to_all(softmax_heads, "head", split_axis=0, concat_axis=1, tiled=True),
    )
    return (result[0], result[1])


def solution(mesh):
    in_specs = (
        P("ctx", "head"),
        P("ctx", "head"),
        P("ctx", "head"),
        P("head", "ctx"),
        P("head"),
        P("ctx", "head"),
        P("ctx", "head"),
        P("ctx", "head"),
        P("ctx", None),
        P("ctx"),
    )
    out_specs = (P(("ctx", "head"), None), P(("ctx", "head"), None))
    return jax.shard_map(local, mesh=mesh, in_specs=in_specs, out_specs=out_specs, check_vma=False)
```

profile of v0, /device:TPU:1, one launch (start us, length us, event | category | flops | bytes accessed | tf_op | source)
XLA Modules:
  0.0 513.5 jit_solution(12203310333632114149)
XLA Ops:
  8.6 2.4 copy.104
  11.1 2.4 copy.105
  14.7 68.9 %while.38 = (s32[]{:T(128)}, f32[16,128,128]{2,1,0:T(8,128)S(1)}, f32[2,128,16,128]{1,0,3,2:T(2,128)}, f32[2,16]{1,0:T(2,128)S(1)}, bf16[2,128,16,128]{3,2,1,0:T...) while((s32[]{:T(128)}, f32[16,128,128]{2,1,0:T(8,128)S(1)}, ...), condition=%wide.region_2.3_spmd.clone, body=%wide.region_1.2_spmd.clone.sunk | while | flops 272648192 | bytes 18973188 | solution.py:102
  19.3 2.0 fusion.61
  22.5 26.6 %dynamic_update_slice.13 = f32[2,128,16,128]{1,0,3,2:T(2,128)} dynamic-update-slice(f32[2,128,16,128]{1,0,3,2:T(2,128)} %get-tuple-element.512, f32[1,128,16,128]{1,0,3,2:T(1,128)S(1)} %bitcast.182, s32[]{:T(128)S(6)} %copy.170, s32[]{:T(128)} %constant.86.clone.1..sunk, s32[]{:T(128)} %constant.86.clone.1..sunk, s32[]{:T(128)} %constant.86.clone.1..sunk) | dynamic-update-slice | bytes 2097156 | tf_op jit(solution)/shard_map/while/body/jit(dynamic_update_index_in_dim)/dynamic_update_slice | solution.py:102
  51.8 1.9 convolution_bitcast_fusion.3
  53.8 2.0 fusion.61
  57.0 26.6 %dynamic_update_slice.13 = f32[2,128,16,128]{1,0,3,2:T(2,128)} dynamic-update-slice(f32[2,128,16,128]{1,0,3,2:T(2,128)} %get-tuple-element.512, f32[1,128,16,128]{1,0,3,2:T(1,128)S(1)} %bitcast.182, s32[]{:T(128)S(6)} %copy.170, s32[]{:T(128)} %constant.86.clone.1..sunk, s32[]{:T(128)} %constant.86.clone.1..sunk, s32[]{:T(128)} %constant.86.clone.1..sunk) | dynamic-update-slice | bytes 2097156 | tf_op jit(solution)/shard_map/while/body/jit(dynamic_update_index_in_dim)/dynamic_update_slice | solution.py:102
  84.6 4.9 collective-permute-start.1
  89.5 4.5 collective-permute-start
  94.0 1.9 collective-permute-start.3
  96.0 3.9 collective-permute-start.2
  99.8 4.1 reshape.126
  106.5 221.7 %all-reduce = f32[1024]{0:T(1024)S(1)} all-reduce(f32[1024]{0:T(1024)S(1)} %dynamic-update-slice), channel_id=2, replica_groups=mesh['ctx'=64,'head'=4] {'ctx'}, use_global_device_ids=true, to_apply=%add | all-reduce | flops 1024 | bytes 8192
  331.3 2.7 copy.107
  335.8 2.8 copy.109
  338.5 41.4 %while.37 = (s32[]{:T(128)}, bf16[2,128,16,128]{3,2,1,0:T(8,128)(2,1)}, s32[2,5]{1,0:T(2,128)S(1)}, s32[]{:T(128)}, bf16[6,128,16,128]{3,2,1,0:T(8,128)(2,1)}, /...) while((s32[]{:T(128)}, ...), condition=%wide.region_11.13_spmd, body=%wide.region_8.12_spmd.sunk | while | flops 689878016 | bytes 69611912 | solution.py:161
  338.6 3.0 gather_fusion
  341.6 4.4 gather_fusion.1
  346.0 2.3 broadcast_select_fusion.3
  354.9 2.6 fusion.59
  359.2 3.3 gather_fusion
  362.4 4.4 gather_fusion.1
  366.9 2.3 broadcast_select_fusion.3
  375.7 2.6 fusion.59
  380.0 2.4 all_to_all.32
  382.3 4.3 all-to-all-start.1
  386.6 94.8 %while.39 = (s32[]{:T(128)}, f32[16,128,128]{2,1,0:T(8,128)S(1)}, s32[]{:T(128)}, f32[64,16]{1,0:T(8,128)S(1)}, f32[64,16,128,128]{3,2,1,0:T(8,128)}, /*index=5*/s32[]{:T(128)}, s32[]{:T(128)}) while((s32[]{:T(128)}, f32[16,128,128]{2,1,0:T(8,128)S(1)}, s32[]{:T(128)}, f32[64,16]{1,0:T(8,128)S(1)}, f32[64,16,128,128]{3,2,1,0:T(8,128)}, ...), condition=%wide.region_6.7_spmd.clone, body=%wide.region_5.6_spmd.clone.sunk | while | flops 1048580 | bytes 3146033 | solution.py:26
  481.4 2.3 multiply_reduce_fusion
  486.5 4.3 all-to-all-start
  490.8 2.3 copy.103
  493.1 12.6 %all-to-all-done = bf16[4,64,2048]{2,1,0:T(8,128)(2,1)S(1)} async-done(((bf16[4,64,2048]{2,1,0:T(8,128)(2,1)}), bf16[4,64,2048]{2,1,0:T(8,128)(2,1)S(1)}, u32[]{:S(2)}, u32[]{:S(2)}) %all-to-all-start) | async-done | bytes 1048608 | tf_op jit(solution)/shard_map/all_to_all | solution.py:181
  (253 shorter events, 132.5 us)
Async XLA Ops:
  7.2 0.7 copy-start
  7.2 6.3 %copy-start.8 = (bf16[256,2048]{1,0:T(8,128)(2,1)S(1)}, bf16[256,2048]{1,0:T(8,128)(2,1)}, u32[]{:S(2)}) copy-start(bf16[256,2048]{1,0:T(8,128)(2,1)} %param.18) | copy-start | bytes 3145732
  7.2 379.4 %all-gather.4.cloned.1.call-start = ((), (), s32[]{:S(2)}) async-start(), calls=%async_computation.2 | async-start | bytes 68157440 | tf_op jit(solution)/shard_map/all_gather | solution.py:17
  15.8 3.5 copy-start.3
  19.3 2.1 copy-start.4
  50.2 3.5 copy-start.3
  53.8 2.1 copy-start.4
  83.6 1.0 copy-start.2
  83.6 21.1 %copy-start.17 = (u32[256]{0:T(256)S(1)}, u32[256]{0:T(256)}, u32[]{:S(2)}) copy-start(u32[256]{0:T(256)} %constant.99) | copy-start | bytes 3076
  83.6 244.7 %copy-start.9 = (bf16[256,2048]{1,0:T(8,128)(2,1)S(1)}, bf16[256,2048]{1,0:T(8,128)(2,1)}, u32[]{:S(2)}) copy-start(bf16[256,2048]{1,0:T(8,128)(2,1)} %param.23) | copy-start | bytes 3145732
  84.6 245.0 %collective-permute-start.1 = (bf16[256,2048]{1,0:T(8,128)(2,1)}, bf16[256,2048]{1,0:T(8,128)(2,1)}, u32[]{:S(2)}, u32[]{:S(2)}) collective-permute-start(bf16[256,2048]{1,0:T(8,128)(2,1)} %param.25), channel_id=1, source_target_pairs={{0,4},{4,8},{8,12},{12,16},{16,20},{20,24},{24,28},{28,32},{32,36}... | collective-permute-start | bytes 3145736 | tf_op jit(solution)/shard_map/ppermute | solution.py:32
  89.5 240.1 %collective-permute-start = (bf16[256,2048]{1,0:T(8,128)(2,1)}, bf16[256,2048]{1,0:T(8,128)(2,1)}, u32[]{:S(2)}, u32[]{:S(2)}) collective-permute-start(bf16[256,2048]{1,0:T(8,128)(2,1)} %param.25), channel_id=1, source_target_pairs={{0,8},{4,12},{8,16},{12,20},{16,24},{20,28},{24,32},{28,36},{32,40... | collective-permute-start | bytes 3145736 | tf_op jit(solution)/shard_map/ppermute | solution.py:32
  94.0 240.0 %collective-permute-start.3 = (bf16[256,2048]{1,0:T(8,128)(2,1)}, bf16[256,2048]{1,0:T(8,128)(2,1)S(1)}, u32[]{:S(2)}, u32[]{:S(2)}) collective-permute-start(bf16[256,2048]{1,0:T(8,128)(2,1)} %param.24), channel_id=1, source_target_pairs={{0,4},{4,8},{8,12},{12,16},{16,20},{20,24},{24,28},{28,32},{32,36}... | collective-permute-start | bytes 3145736 | tf_op jit(solution)/shard_map/ppermute | solution.py:32
  96.0 238.1 %collective-permute-start.2 = (bf16[256,2048]{1,0:T(8,128)(2,1)}, bf16[256,2048]{1,0:T(8,128)(2,1)}, u32[]{:S(2)}, u32[]{:S(2)}) collective-permute-start(bf16[256,2048]{1,0:T(8,128)(2,1)} %param.24), channel_id=1, source_target_pairs={{0,8},{4,12},{8,16},{12,20},{16,24},{20,28},{24,32},{28,36},{32,40... | collective-permute-start | bytes 3145736 | tf_op jit(solution)/shard_map/ppermute | solution.py:32
  99.8 229.8 %copy-start.12 = (bf16[256,2048]{1,0:T(8,128)(2,1)S(1)}, bf16[256,2048]{1,0:T(8,128)(2,1)}, u32[]{:S(2)}) copy-start(bf16[256,2048]{1,0:T(8,128)(2,1)} %param.25) | copy-start | bytes 3145732
  331.3 2.7 copy-start.13
  335.8 2.8 copy-start.14
  335.8 2.8 copy-start.16
  348.3 1.3 copy-start.6
  354.9 3.1 copy-start.10
  358.1 1.0 copy-start.11
  369.1 1.2 copy-start.6
  375.7 3.1 copy-start.10
  378.9 1.0 copy-start.11
  379.9 6.7 %copy-start.5 = (f32[16,128,128]{2,1,0:T(8,128)S(1)}, f32[16,128,128]{2,1,0:T(8,128)}, u32[]{:S(2)}) copy-start(f32[16,128,128]{2,1,0:T(8,128)} %custom-call.1) | copy-start | bytes 3145732
  382.3 104.1 %all-to-all-start.1 = ((bf16[4,64,2048]{2,1,0:T(8,128)(2,1)}), bf16[4,64,2048]{2,1,0:T(8,128)(2,1)}, u32[]{:S(2)}, u32[]{:S(2)}) async-start(bf16[4,64,2048]{2,1,0:T(8,128)(2,1)} %all_to_all.32), calls=%async_computation.1 | async-start | bytes 2097152 | tf_op jit(solution)/shard_map/all_to_all | solution.py:182
  386.6 94.8 %copy-start.7 = (f32[256,16,128]{0,2,1:T(8,128)S(1)}, f32[256,16,128]{0,2,1:T(8,128)}, u32[]{:S(2)}) copy-start(f32[256,16,128]{0,2,1:T(8,128)} %reshape.126) | copy-start | bytes 6291460
  481.4 2.3 copy-start.15
  485.2 21.5 %copy-start.1 = (f32[16,256]{1,0:T(8,128)S(1)}, f32[16,256]{1,0:T(8,128)}, u32[]{:S(2)}) copy-start(f32[16,256]{1,0:T(8,128)} %param.21) | copy-start | bytes 49156
  486.5 19.2 %all-to-all-start = ((bf16[4,64,2048]{2,1,0:T(8,128)(2,1)}), bf16[4,64,2048]{2,1,0:T(8,128)(2,1)S(1)}, u32[]{:S(2)}, u32[]{:S(2)}) async-start(bf16[4,64,2048]{2,1,0:T(8,128)(2,1)} %all_to_all.28), calls=%async_computation | async-start | bytes 2097152 | tf_op jit(solution)/shard_map/all_to_all | solution.py:181
Sparse Core Ops, SparseCore 0:
  84.7 279.2 all-gather.3
where the time goes:
time: 521 us; the launch traced here: 514 us
  blocking collectives  222 us (43%)
  local copies, waits for them, and re-layouts  111 us (21%)
  other arithmetic  108 us (21%)
  starting transfers between devices  23.8 us (5%)
  matrix products  19.3 us (4%)
  between operations  14.9 us (3%)
  waiting for transfers between devices  12.6 us (2%)
    unnamed x1, blocking collectives  222 us
    select_n x63, other arithmetic, step(): jnp.where(position < mine, new, old)  92 us
    dynamic_update_slice x2, local copies, waits for them, and re-layouts, linear_layer(): lax.scan(advance_both, start, (query_blocks, keys_blocks, values_blocks,...  53.2 us
    unnamed x35, local copies, waits for them, and re-layouts  15.2 us
    ppermute x4, starting transfers between devices, passed_along(): return lax.ppermute(block, axis, route)  15.2 us
    all_to_all x1, waiting for transfers between devices, local(): lax.all_to_all(linear_heads, 'head', split_axis=0, concat_axis=1, tiled=T...  12.6 us
  transfers between devices with their start and end apart: 7, of which 1 were waited for; matrix products, arithmetic and copies ran while one was open for 30% of the time, Pallas kernels for 0%

commit v1 on v0

--- a/solution.py
+++ b/solution.py
@@ -10,20 +10,6 @@
 
 
 EPS = 1e-06
-
-
-def carried_in(value, axis, join, neutral):
-    count, mine = (lax.axis_size(axis), lax.axis_index(axis))
-    pieces = jax.tree.map(lambda part: lax.all_gather(part, axis), value)
-    subtotal = jax.tree.map(
-        lambda part, zero: jnp.full_like(part, 0) + jnp.asarray(zero, part.dtype), value, neutral
-    )
-
-    def step(position, subtotal):
-        longer = join(subtotal, jax.tree.map(lambda part: part[position], pieces))
-        return jax.tree.map(lambda new, old: jnp.where(position < mine, new, old), longer, subtotal)
-
-    return lax.fori_loop(0, count - 1, step, subtotal)
 
 
 def passed_along(block, axis, distance):
@@ -74,9 +60,19 @@
 
 
 def carry_in(final, section_total):
-    identity = (jnp.ones(section_total.shape, jnp.float32), jnp.zeros_like(final))
-    result = carried_in((jnp.exp(section_total), final), "ctx", combine_states, identity)
-    return result[1]
+    count, mine = (lax.axis_size("ctx"), lax.axis_index("ctx"))
+    factor = jnp.exp(section_total)
+    shifted = passed_along((factor, final), "ctx", 1)
+    first = mine < 1
+    running = (jnp.where(first, 1.0, shifted[0]), jnp.where(first, 0.0, shifted[1]))
+    distance = 1
+    while distance < count:
+        earlier = passed_along(running, "ctx", distance)
+        joined = combine_states(earlier, running)
+        reached = mine >= distance
+        running = jax.tree.map(lambda new, old: jnp.where(reached, new, old), joined, running)
+        distance *= 2
+    return running[1]
 
 
 def linear_layer(linear_query, linear_key, linear_value, log_decay, norm_gain):
@@ -92,22 +88,21 @@
     totals = cumulative[:, :, -1]
     section_cum = jnp.cumsum(log_decay, axis=1)
     section_total = section_cum[:, -1]
-    start = jnp.zeros((heads, width, width), jnp.float32)
-
-    def advance_both(carried, pieces):
-        query_blk, keys_blk, values_blk, cumul_blk, total_blk = pieces
-        output = block_output(carried, query_blk, keys_blk, values_blk, cumul_blk)
-        return (block_state(carried, keys_blk, values_blk, cumul_blk, total_blk), output)
-
-    final, outputs = lax.scan(
-        advance_both, start, (query_blocks, keys_blocks, values_blocks, cumulative, totals)
-    )
-    incoming = carry_in(final, section_total)
+    carried = jnp.zeros((heads, width, width), jnp.float32)
+    before = []
+    for b in range(blocks_here):
+        before.append(carried)
+        carried = block_state(carried, keys_blocks[b], values_blocks[b], cumulative[b], totals[b])
+    incoming = carry_in(carried, section_total)
+    outputs = [
+        block_output(before[b], query_blocks[b], keys_blocks[b], values_blocks[b], cumulative[b])
+        for b in range(blocks_here)
+    ]
     queries_flat = linear_query.reshape(length, heads, width)
     scaled = (queries_flat.astype(jnp.float32) * jnp.exp(section_cum).T[:, :, None]).astype(
         jnp.bfloat16
     )
-    raw = outputs.reshape(length, heads, width) + jnp.einsum(
+    raw = jnp.concatenate(outputs, axis=0) + jnp.einsum(
         "thd,hde->the", scaled, incoming.astype(jnp.bfloat16), preferred_element_type=jnp.float32
     )
     square_mean = jnp.mean(raw * raw, axis=2, keepdims=True)

time: 521 us -> 376 us (0.72)
  the two profiles are of different devices: /device:TPU:1 before, /device:TPU:8 now
where the time goes in v1:
time: 376 us; the launch traced here: 374 us
  waiting for transfers between devices  219 us (58%)
  starting transfers between devices  58.4 us (16%)
  local copies, waits for them, and re-layouts  47.9 us (13%)
  other arithmetic  25 us (7%)
  matrix products  22.2 us (6%)
    ppermute x17, waiting for transfers between devices, passed_along(): return lax.ppermute(block, axis, route)  197 us
    ppermute x17, starting transfers between devices, passed_along(): return lax.ppermute(block, axis, route)  50.6 us
    unnamed x39, local copies, waits for them, and re-layouts  13 us
    all_to_all x1, waiting for transfers between devices, local(): lax.all_to_all(linear_heads, 'head', split_axis=0, concat_axis=1, tiled=T...  13 us
    gather x2, local copies, waits for them, and re-layouts, one_block(): keys_sel = jnp.take(key_blocks, local_row, axis=0)  8.96 us
    all_to_all x1, waiting for transfers between devices, local(): lax.all_to_all(softmax_heads, 'head', split_axis=0, concat_axis=1, tiled=...  8.84 us
  transfers between devices with their start and end apart: 19, of which 10 were waited for; matrix products, arithmetic and copies ran while one was open for 20% of the time, Pallas kernels for 0%

profile of v1, /device:TPU:8, one launch (start us, length us, event | category | flops | bytes accessed | tf_op | source)
XLA Modules:
  0.0 374.1 jit_solution(3439596358003893778)
XLA Ops:
  10.0 17.8 %collective-permute-done.6 = f32[16,128,128]{2,1,0:T(8,128)S(1)} collective-permute-done((f32[16,128,128]{2,1,0:T(8,128)}, f32[16,128,128]{2,1,0:T(8,128)S(1)}, u32[]{:S(2)}, u32[]{:S(2)}) %collective-permute-start.6) | collective-permute-done | bytes 1048608 | tf_op jit(solution)/shard_map/ppermute | solution.py:18
  33.8 13.6 %collective-permute-done = f32[16]{0:T(128)S(1)} collective-permute-done((f32[16]{0:T(128)S(1)}, f32[16]{0:T(128)S(1)}, u32[]{:S(2)}, u32[]{:S(2)}) %collective-permute-start) | collective-permute-done | bytes 96 | tf_op jit(solution)/shard_map/ppermute | solution.py:18
  54.6 3.5 collective-permute-start.15
  58.1 5.9 %collective-permute-start.1 = (f32[16]{0:T(128)S(1)}, f32[16]{0:T(128)S(1)}, u32[]{:S(2)}, u32[]{:S(2)}) collective-permute-start(f32[16]{0:T(128)S(1)} %broadcast_select_fusion.3), channel_id=1, source_target_pairs={{0,4},{4,8},{8,12},{12,16},{16,20},{20,24},{24,28},{28,32},{32,36}... | collective-permute-start | bytes 200 | tf_op jit(solution)/shard_map/ppermute | solution.py:18
  64.0 65.9 %collective-permute-done.1 = f32[16]{0:T(128)S(1)} collective-permute-done((f32[16]{0:T(128)S(1)}, f32[16]{0:T(128)S(1)}, u32[]{:S(2)}, u32[]{:S(2)}) %collective-permute-start.1) | collective-permute-done | bytes 96 | tf_op jit(solution)/shard_map/ppermute | solution.py:18
  138.0 2.8 convolution_bitcast_fusion.3
  140.9 4.6 %collective-permute-start.2 = (f32[16]{0:T(128)S(1)}, f32[16]{0:T(128)S(1)}, u32[]{:S(2)}, u32[]{:S(2)}) collective-permute-start(f32[16]{0:T(128)S(1)} %broadcast_select_fusion.4), channel_id=1, source_target_pairs={{0,8},{4,12},{8,16},{12,20},{16,24},{20,28},{24,32},{28,36},{32,40... | collective-permute-start | bytes 200 | tf_op jit(solution)/shard_map/ppermute | solution.py:18
  145.4 34.9 %collective-permute-done.2 = f32[16]{0:T(128)S(1)} collective-permute-done((f32[16]{0:T(128)S(1)}, f32[16]{0:T(128)S(1)}, u32[]{:S(2)}, u32[]{:S(2)}) %collective-permute-start.2) | collective-permute-done | bytes 96 | tf_op jit(solution)/shard_map/ppermute | solution.py:18
  181.8 5.5 %collective-permute-start.10 = (f32[16,128,128]{2,1,0:T(8,128)S(1)}, f32[16,128,128]{2,1,0:T(8,128)}, u32[]{:S(2)}, u32[]{:S(2)}) collective-permute-start(f32[16,128,128]{2,1,0:T(8,128)S(1)} %add_select_fusion.3), channel_id=1, source_target_pairs={{0,32},{4,36},{8,40},{12,44},{16,48},{20,52},{24,56},{28,60},{32,6... | collective-permute-start | bytes 3145736 | tf_op jit(solution)/shard_map/ppermute | solution.py:18
  188.7 2.7 fusion.19
  191.4 3.0 convolution_bitcast_fusion.1
  199.1 36.1 %collective-permute-done.3 = f32[16]{0:T(128)S(1)} collective-permute-done((f32[16]{0:T(128)S(1)}, f32[16]{0:T(128)S(1)}, u32[]{:S(2)}, u32[]{:S(2)}) %collective-permute-start.3) | collective-permute-done | bytes 96 | tf_op jit(solution)/shard_map/ppermute | solution.py:18
  237.1 8.3 %collective-permute-done.4 = f32[16]{0:T(128)S(1)} collective-permute-done((f32[16]{0:T(128)S(1)}, f32[16]{0:T(128)S(1)}, u32[]{:S(2)}, u32[]{:S(2)}) %collective-permute-start.4) | collective-permute-done | bytes 96 | tf_op jit(solution)/shard_map/ppermute | solution.py:18
  247.4 3.2 collective-permute-start.5
  252.0 12.0 %collective-permute-done.5 = f32[16]{0:T(128)S(1)} collective-permute-done((f32[16]{0:T(128)S(1)}, f32[16]{0:T(128)S(1)}, u32[]{:S(2)}, u32[]{:S(2)}) %collective-permute-start.5) | collective-permute-done | bytes 96 | tf_op jit(solution)/shard_map/ppermute | solution.py:18
  269.3 2.7 copy.127
  273.8 2.7 copy.129
  276.5 8.7 %collective-permute-done.11 = f32[16,128,128]{2,1,0:T(8,128)S(1)} collective-permute-done((f32[16,128,128]{2,1,0:T(8,128)S(1)}, f32[16,128,128]{2,1,0:T(8,128)S(1)}, u32[]{:S(2)}, u32[]{:S(2)}) %collective-permute-start.11) | collective-permute-done | bytes 1048608 | tf_op jit(solution)/shard_map/ppermute | solution.py:18
  286.3 6.6 %collective-permute-start.12 = (f32[16,128,128]{2,1,0:T(8,128)}, f32[16,128,128]{2,1,0:T(8,128)}, u32[]{:S(2)}, u32[]{:S(2)}) collective-permute-start(f32[16,128,128]{2,1,0:T(8,128)} %add_select_fusion.1), channel_id=1, source_target_pairs={{0,128},{4,132},{8,136},{12,140},{16,144},{20,148},{24,152},{28,15... | collective-permute-start | bytes 3145736 | tf_op jit(solution)/shard_map/ppermute | solution.py:18
  292.9 40.9 %while.10 = (s32[]{:T(128)}, bf16[2,128,16,128]{3,2,1,0:T(8,128)(2,1)}, s32[2,5]{1,0:T(2,128)S(1)}, s32[]{:T(128)}, bf16[6,128,16,128]{3,2,1,0:T(8,128)(2,1)}, /...) while((s32[]{:T(128)}, ...), condition=%wide.region_7.9_spmd, body=%wide.region_4.8_spmd.sunk | while | flops 689878016 | bytes 69611904 | solution.py:156
  292.9 2.9 gather_fusion
  295.8 4.5 %gather_fusion.1 = bf16[5,128,16,128]{3,2,1,0:T(8,128)(2,1)} fusion(bf16[6,128,16,128]{3,2,1,0:T(8,128)(2,1)} %get-tuple-element.209, s32[1024]{0:T(1024)S(1)} %pad_clamp_fusion.2), kind=kCustom, calls=%fused_computation.1.clone.clone.1 | custom fusion | bytes 5242900 | tf_op jit(solution)/shard_map/while/body/eval_jaxpr/jit(_take)/gather | solution.py:152
  309.1 2.6 fusion.79
  313.4 2.9 gather_fusion
  316.3 4.5 %gather_fusion.1 = bf16[5,128,16,128]{3,2,1,0:T(8,128)(2,1)} fusion(bf16[6,128,16,128]{3,2,1,0:T(8,128)(2,1)} %get-tuple-element.209, s32[1024]{0:T(1024)S(1)} %pad_clamp_fusion.2), kind=kCustom, calls=%fused_computation.1.clone.clone.1 | custom fusion | bytes 5242900 | tf_op jit(solution)/shard_map/while/body/eval_jaxpr/jit(_take)/gather | solution.py:152
  329.6 2.6 fusion.79
  333.8 2.4 all_to_all.32
  336.2 4.3 %all-to-all-start.1 = ((bf16[4,64,2048]{2,1,0:T(8,128)(2,1)}), bf16[4,64,2048]{2,1,0:T(8,128)(2,1)S(1)}, u32[]{:S(2)}, u32[]{:S(2)}) async-start(bf16[4,64,2048]{2,1,0:T(8,128)(2,1)} %all_to_all.32), calls=%async_computation.1 | async-start | bytes 2097152 | tf_op jit(solution)/shard_map/all_to_all | solution.py:177
  340.5 3.4 multiply_reduce_fusion
  346.7 8.8 %all-to-all-done.1 = bf16[4,64,2048]{2,1,0:T(8,128)(2,1)S(1)} async-done(((bf16[4,64,2048]{2,1,0:T(8,128)(2,1)}), bf16[4,64,2048]{2,1,0:T(8,128)(2,1)S(1)}, u32[]{:S(2)}, u32[]{:S(2)}) %all-to-all-start.1) | async-done | bytes 1048608 | tf_op jit(solution)/shard_map/all_to_all | solution.py:177
  355.5 3.5 all-to-all-start
  360.1 13.0 %all-to-all-done = bf16[4,64,2048]{2,1,0:T(8,128)(2,1)S(1)} async-done(((bf16[4,64,2048]{2,1,0:T(8,128)(2,1)}), bf16[4,64,2048]{2,1,0:T(8,128)(2,1)S(1)}, u32[]{:S(2)}, u32[]{:S(2)}) %all-to-all-start) | async-done | bytes 1048608 | tf_op jit(solution)/shard_map/all_to_all | solution.py:176
  (144 shorter events, 76.7 us)
Async XLA Ops:
  6.1 22.8 %copy-start.11 = (bf16[128,2048]{0,1:T(8,128)(2,1)}, bf16[128,2048]{0,1:T(8,128)(2,1)S(1)}, u32[]{:S(2)}) copy-start(bf16[128,2048]{0,1:T(8,128)(2,1)S(1)} %copy.121) | copy-start | bytes 1572868
  8.1 19.8 %collective-permute-start.6 = (f32[16,128,128]{2,1,0:T(8,128)}, f32[16,128,128]{2,1,0:T(8,128)S(1)}, u32[]{:S(2)}, u32[]{:S(2)}) collective-permute-start(f32[16,128,128]{2,1,0:T(8,128)} %convolution_add_fusion), channel_id=1, source_target_pairs={{0,4},{4,8},{8,12},{12,16},{16,20},{20,24},{24,28},{28,32},{32,36}... | collective-permute-start | bytes 3145736 | tf_op jit(solution)/shard_map/ppermute | solution.py:18
  28.9 18.5 %collective-permute-start.7 = (f32[16,128,128]{2,1,0:T(8,128)}, f32[16,128,128]{2,1,0:T(8,128)}, u32[]{:S(2)}, u32[]{:S(2)}) collective-permute-start(f32[16,128,128]{2,1,0:T(8,128)} %broadcast_select_fusion.2), channel_id=1, source_target_pairs={{0,4},{4,8},{8,12},{12,16},{16,20},{20,24},{24,28},{28,32},{32,36}... | collective-permute-start | bytes 3145736 | tf_op jit(solution)/shard_map/ppermute | solution.py:18
  31.9 15.6 %collective-permute-start = (f32[16]{0:T(128)S(1)}, f32[16]{0:T(128)S(1)}, u32[]{:S(2)}, u32[]{:S(2)}) collective-permute-start(f32[16]{0:T(128)S(1)} %fusion.50), channel_id=1, source_target_pairs={{0,4},{4,8},{8,12},{12,16},{16,20},{20,24},{24,28},{28,32},{32,36}... | collective-permute-start | bytes 200 | tf_op jit(solution)/shard_map/ppermute | solution.py:18
  48.8 81.1 %copy-start.4 = (f32[16,128,128]{2,1,0:T(8,128)}, f32[16,128,128]{2,1,0:T(8,128)S(1)}, u32[]{:S(2)}) copy-start(f32[16,128,128]{2,1,0:T(8,128)S(1)} %add_select_fusion.5) | copy-start | bytes 3145732
  48.9 81.1 %collective-permute-start.8 = (f32[16,128,128]{2,1,0:T(8,128)S(1)}, f32[16,128,128]{2,1,0:T(8,128)}, u32[]{:S(2)}, u32[]{:S(2)}) collective-permute-start(f32[16,128,128]{2,1,0:T(8,128)S(1)} %add_select_fusion.5), channel_id=1, source_target_pairs={{0,8},{4,12},{8,16},{12,20},{16,24},{20,28},{24,32},{28,36},{32,40... | collective-permute-start | bytes 3145736 | tf_op jit(solution)/shard_map/ppermute | solution.py:18
  50.8 216.5 %collective-permute-start.13 = (bf16[256,2048]{1,0:T(8,128)(2,1)}, bf16[256,2048]{1,0:T(8,128)(2,1)}, u32[]{:S(2)}, u32[]{:S(2)}) collective-permute-start(bf16[256,2048]{1,0:T(8,128)(2,1)} %param.21), channel_id=1, source_target_pairs={{0,8},{4,12},{8,16},{12,20},{16,24},{20,28},{24,32},{28,36},{32,40... | collective-permute-start | bytes 3145736 | tf_op jit(solution)/shard_map/ppermute | solution.py:18
  52.7 214.6 %collective-permute-start.14 = (bf16[256,2048]{1,0:T(8,128)(2,1)}, bf16[256,2048]{1,0:T(8,128)(2,1)}, u32[]{:S(2)}, u32[]{:S(2)}) collective-permute-start(bf16[256,2048]{1,0:T(8,128)(2,1)} %param.21), channel_id=1, source_target_pairs={{0,4},{4,8},{8,12},{12,16},{16,20},{20,24},{24,28},{28,32},{32,36}... | collective-permute-start | bytes 3145736 | tf_op jit(solution)/shard_map/ppermute | solution.py:18
  54.6 217.4 %collective-permute-start.15 = (bf16[256,2048]{1,0:T(8,128)(2,1)}, bf16[256,2048]{1,0:T(8,128)(2,1)}, u32[]{:S(2)}, u32[]{:S(2)}) collective-permute-start(bf16[256,2048]{1,0:T(8,128)(2,1)} %param.20), channel_id=1, source_target_pairs={{0,8},{4,12},{8,16},{12,20},{16,24},{20,28},{24,32},{28,36},{32,40... | collective-permute-start | bytes 3145736 | tf_op jit(solution)/shard_map/ppermute | solution.py:18
  58.1 71.8 %collective-permute-start.1 = (f32[16]{0:T(128)S(1)}, f32[16]{0:T(128)S(1)}, u32[]{:S(2)}, u32[]{:S(2)}) collective-permute-start(f32[16]{0:T(128)S(1)} %broadcast_select_fusion.3), channel_id=1, source_target_pairs={{0,4},{4,8},{8,12},{12,16},{16,20},{20,24},{24,28},{28,32},{32,36}... | collective-permute-start | bytes 200 | tf_op jit(solution)/shard_map/ppermute | solution.py:18
  129.9 8.1 %copy-start.7 = (bf16[128,2048]{0,1:T(8,128)(2,1)S(1)}, bf16[128,2048]{0,1:T(8,128)(2,1)}, u32[]{:S(2)}) copy-start(bf16[128,2048]{0,1:T(8,128)(2,1)} %copy-done.6) | copy-start | bytes 1572868
  129.9 8.1 %copy-start.9 = (bf16[128,2048]{0,1:T(8,128)(2,1)S(1)}, bf16[128,2048]{0,1:T(8,128)(2,1)}, u32[]{:S(2)}) copy-start(bf16[128,2048]{0,1:T(8,128)(2,1)} %copy-done.8) | copy-start | bytes 1572868
  131.7 48.6 %collective-permute-start.9 = (f32[16,128,128]{2,1,0:T(8,128)S(1)}, f32[16,128,128]{2,1,0:T(8,128)}, u32[]{:S(2)}, u32[]{:S(2)}) collective-permute-start(f32[16,128,128]{2,1,0:T(8,128)S(1)} %add_select_fusion.4), channel_id=1, source_target_pairs={{0,16},{4,20},{8,24},{12,28},{16,32},{20,36},{24,40},{28,44},{32,4... | collective-permute-start | bytes 3145736 | tf_op jit(solution)/shard_map/ppermute | solution.py:18
  140.9 39.5 %collective-permute-start.2 = (f32[16]{0:T(128)S(1)}, f32[16]{0:T(128)S(1)}, u32[]{:S(2)}, u32[]{:S(2)}) collective-permute-start(f32[16]{0:T(128)S(1)} %broadcast_select_fusion.4), channel_id=1, source_target_pairs={{0,8},{4,12},{8,16},{12,20},{16,24},{20,28},{24,32},{28,36},{32,40... | collective-permute-start | bytes 200 | tf_op jit(solution)/shard_map/ppermute | solution.py:18
  181.8 65.6 %collective-permute-start.10 = (f32[16,128,128]{2,1,0:T(8,128)S(1)}, f32[16,128,128]{2,1,0:T(8,128)}, u32[]{:S(2)}, u32[]{:S(2)}) collective-permute-start(f32[16,128,128]{2,1,0:T(8,128)S(1)} %add_select_fusion.3), channel_id=1, source_target_pairs={{0,32},{4,36},{8,40},{12,44},{16,48},{20,52},{24,56},{28,60},{32,6... | collective-permute-start | bytes 3145736 | tf_op jit(solution)/shard_map/ppermute | solution.py:18
  194.4 40.8 %collective-permute-start.3 = (f32[16]{0:T(128)S(1)}, f32[16]{0:T(128)S(1)}, u32[]{:S(2)}, u32[]{:S(2)}) collective-permute-start(f32[16]{0:T(128)S(1)} %broadcast_select_fusion.5), channel_id=1, source_target_pairs={{0,16},{4,20},{8,24},{12,28},{16,32},{20,36},{24,40},{28,44},{32,4... | collective-permute-start | bytes 200 | tf_op jit(solution)/shard_map/ppermute | solution.py:18
  235.2 10.2 %collective-permute-start.4 = (f32[16]{0:T(128)S(1)}, f32[16]{0:T(128)S(1)}, u32[]{:S(2)}, u32[]{:S(2)}) collective-permute-start(f32[16]{0:T(128)S(1)} %broadcast_select_fusion.6), channel_id=1, source_target_pairs={{0,32},{4,36},{8,40},{12,44},{16,48},{20,52},{24,56},{28,60},{32,6... | collective-permute-start | bytes 200 | tf_op jit(solution)/shard_map/ppermute | solution.py:18
  237.1 28.8 %copy-start.12 = (f32[128,16,128]{2,0,1:T(8,128)S(1)}, f32[128,16,128]{2,0,1:T(8,128)}, u32[]{:S(2)}) copy-start(f32[128,16,128]{2,0,1:T(8,128)} %convolution_bitcast_fusion.1) | copy-start | bytes 3145732
  245.4 26.6 %collective-permute-start.16 = (bf16[256,2048]{1,0:T(8,128)(2,1)}, bf16[256,2048]{1,0:T(8,128)(2,1)S(1)}, u32[]{:S(2)}, u32[]{:S(2)}) collective-permute-start(bf16[256,2048]{1,0:T(8,128)(2,1)} %param.20), channel_id=1, source_target_pairs={{0,4},{4,8},{8,12},{12,16},{16,20},{20,24},{24,28},{28,32},{32,36}... | collective-permute-start | bytes 3145736 | tf_op jit(solution)/shard_map/ppermute | solution.py:18
  247.4 16.6 %collective-permute-start.5 = (f32[16]{0:T(128)S(1)}, f32[16]{0:T(128)S(1)}, u32[]{:S(2)}, u32[]{:S(2)}) collective-permute-start(f32[16]{0:T(128)S(1)} %broadcast_select_fusion.7), channel_id=1, source_target_pairs={{0,64},{4,68},{8,72},{12,76},{16,80},{20,84},{24,88},{28,92},{32,9... | collective-permute-start | bytes 200 | tf_op jit(solution)/shard_map/ppermute | solution.py:18
  264.0 21.1 %collective-permute-start.11 = (f32[16,128,128]{2,1,0:T(8,128)S(1)}, f32[16,128,128]{2,1,0:T(8,128)S(1)}, u32[]{:S(2)}, u32[]{:S(2)}) collective-permute-start(f32[16,128,128]{2,1,0:T(8,128)S(1)} %add_select_fusion.2), channel_id=1, source_target_pairs={{0,64},{4,68},{8,72},{12,76},{16,80},{20,84},{24,88},{28,92},{32,9... | collective-permute-start | bytes 3145736 | tf_op jit(solution)/shard_map/ppermute | solution.py:18
  276.5 16.4 %copy-start.15 = (s32[2,5]{1,0:T(2,128)S(1)}, s32[2,5]{1,0:T(2,128)}, u32[]{:S(2)}) copy-start(s32[2,5]{1,0:T(2,128)} %param.22) | copy-start | bytes 124
  276.5 16.4 %copy-start.17 = (s32[2]{0:T(128)S(1)}, s32[2]{0:T(128)}, u32[]{:S(2)}) copy-start(s32[2]{0:T(128)} %param.23) | copy-start | bytes 28
  286.3 54.2 %collective-permute-start.12 = (f32[16,128,128]{2,1,0:T(8,128)}, f32[16,128,128]{2,1,0:T(8,128)}, u32[]{:S(2)}, u32[]{:S(2)}) collective-permute-start(f32[16,128,128]{2,1,0:T(8,128)} %add_select_fusion.1), channel_id=1, source_target_pairs={{0,128},{4,132},{8,136},{12,140},{16,144},{20,148},{24,152},{28,15... | collective-permute-start | bytes 3145736 | tf_op jit(solution)/shard_map/ppermute | solution.py:18
  309.1 3.1 copy-start.13
  329.6 3.1 copy-start.13
  333.8 6.7 %copy-start.3 = (f32[128,16,128]{2,0,1:T(8,128)S(1)}, f32[128,16,128]{2,0,1:T(8,128)}, u32[]{:S(2)}) copy-start(f32[128,16,128]{2,0,1:T(8,128)} %fusion.18) | copy-start | bytes 3145732
  333.8 6.8 %copy-start.5 = (bf16[256,2048]{1,0:T(8,128)(2,1)S(1)}, bf16[256,2048]{1,0:T(8,128)(2,1)}, u32[]{:S(2)}) copy-start(bf16[256,2048]{1,0:T(8,128)(2,1)} %param.14) | copy-start | bytes 3145732
  336.2 19.3 %all-to-all-start.1 = ((bf16[4,64,2048]{2,1,0:T(8,128)(2,1)}), bf16[4,64,2048]{2,1,0:T(8,128)(2,1)S(1)}, u32[]{:S(2)}, u32[]{:S(2)}) async-start(bf16[4,64,2048]{2,1,0:T(8,128)(2,1)} %all_to_all.32), calls=%async_computation.1 | async-start | bytes 2097152 | tf_op jit(solution)/shard_map/all_to_all | solution.py:177
  340.5 3.4 copy-start.16
  345.4 28.7 %copy-start.1 = (f32[16,256]{1,0:T(8,128)S(1)}, f32[16,256]{1,0:T(8,128)}, u32[]{:S(2)}) copy-start(f32[16,256]{1,0:T(8,128)} %param.17) | copy-start | bytes 49156
  355.5 17.6 %all-to-all-start = ((bf16[4,64,2048]{2,1,0:T(8,128)(2,1)}), bf16[4,64,2048]{2,1,0:T(8,128)(2,1)S(1)}, u32[]{:S(2)}, u32[]{:S(2)}) async-start(bf16[4,64,2048]{2,1,0:T(8,128)(2,1)} %all_to_all.28), calls=%async_computation | async-start | bytes 2097152 | tf_op jit(solution)/shard_map/all_to_all | solution.py:176
  (8 other events, 11.4 us)

commit v2 on v1

--- a/solution.py
+++ b/solution.py
@@ -12,8 +12,11 @@
 EPS = 1e-06
 
 
-def passed_along(block, axis, distance):
-    devices = range(lax.axis_size(axis))
+CTX = ("cy", "cz", "cc")
+
+
+def passed_along(block, axis, distance, count):
+    devices = range(count)
     route = [(i - distance, i) for i in devices if i - distance in devices]
     return lax.ppermute(block, axis, route)
 
@@ -55,24 +58,53 @@
     return inside + across
 
 
-def combine_states(earlier, later):
-    return (earlier[0] * later[0], later[0][:, None, None] * earlier[1] + later[1])
+def packed(state, factor):
+    heads, width, _ = state.shape
+    return jnp.concatenate([state, jnp.broadcast_to(factor[:, None, None], (heads, 8, width))], axis=1)
+
+
+def unpacked(both, width):
+    return both[..., :width, :], both[..., width, 0]
 
 
 def carry_in(final, section_total):
-    count, mine = (lax.axis_size("ctx"), lax.axis_index("ctx"))
-    factor = jnp.exp(section_total)
-    shifted = passed_along((factor, final), "ctx", 1)
-    first = mine < 1
-    running = (jnp.where(first, 1.0, shifted[0]), jnp.where(first, 0.0, shifted[1]))
-    distance = 1
-    while distance < count:
-        earlier = passed_along(running, "ctx", distance)
-        joined = combine_states(earlier, running)
-        reached = mine >= distance
-        running = jax.tree.map(lambda new, old: jnp.where(reached, new, old), joined, running)
-        distance *= 2
-    return running[1]
+    heads, width, _ = final.shape
+    half = heads // 2
+    core, row, column = (lax.axis_index("cc"), lax.axis_index("cz"), lax.axis_index("cy"))
+    pair_states, pair_factors = unpacked(
+        lax.all_gather(packed(final, jnp.exp(section_total)), "cc"), width
+    )
+    low = core * half
+    first = lax.dynamic_slice_in_dim(pair_states[0], low, half, 0)
+    second = lax.dynamic_slice_in_dim(pair_states[1], low, half, 0)
+    first_factor = lax.dynamic_slice_in_dim(pair_factors[0], low, half, 0)
+    second_factor = lax.dynamic_slice_in_dim(pair_factors[1], low, half, 0)
+    chip_state = second_factor[:, None, None] * first + second
+    chip_factor = first_factor * second_factor
+    row_states, row_factors = unpacked(
+        lax.all_gather(packed(chip_state, chip_factor), "cz"), width
+    )
+    total = jnp.zeros_like(chip_state)
+    total_factor = jnp.ones_like(chip_factor)
+    before = total
+    before_factor = total_factor
+    for z in range(row_states.shape[0]):
+        here = z == row
+        before = jnp.where(here, total, before)
+        before_factor = jnp.where(here, total_factor, before_factor)
+        total = row_factors[z][:, None, None] * total + row_states[z]
+        total_factor = total_factor * row_factors[z]
+    column_states, column_factors = unpacked(
+        lax.all_gather(packed(total, total_factor), "cy"), width
+    )
+    above = jnp.zeros_like(chip_state)
+    for y in range(column_states.shape[0]):
+        joined = column_factors[y][:, None, None] * above + column_states[y]
+        above = jnp.where(y < column, joined, above)
+    prefix_half = before_factor[:, None, None] * above + before
+    prefix = lax.all_gather(prefix_half, "cc", axis=0, tiled=True)
+    later = pair_factors[0][:, None, None] * prefix + pair_states[0]
+    return jnp.where(core == 0, prefix, later)
 
 
 def linear_layer(linear_query, linear_key, linear_value, log_decay, norm_gain):
@@ -130,18 +162,18 @@
     return output.astype(jnp.bfloat16)
 
 
-def softmax_layer(soft_query, soft_key, soft_value, block_index, block_count, heads):
+def softmax_layer(soft_query, soft_key, soft_value, block_index, block_count, heads, sections):
     length, columns = soft_query.shape
     per_section = length // BLK
     own_pair = (soft_key, soft_value)
     pieces = []
     for distance in range(WIN_SEC, 0, -1):
-        pieces.append(passed_along((own_pair[0], own_pair[1]), "ctx", distance))
+        pieces.append(passed_along((own_pair[0], own_pair[1]), CTX, distance, sections))
     window_key = jnp.concatenate([piece[0] for piece in pieces] + [soft_key], axis=0)
     window_value = jnp.concatenate([piece[1] for piece in pieces] + [soft_value], axis=0)
     key_blocks = to_blocks(window_key, heads)
     value_blocks = to_blocks(window_value, heads)
-    section = lax.axis_index("ctx")
+    section = lax.axis_index(CTX)
     first_block = (section - WIN_SEC) * per_section
     query_blocks = to_blocks(soft_query, heads)
     own_rows = section * per_section + jnp.arange(per_section, dtype=jnp.int32)
@@ -171,7 +203,10 @@
 ):
     heads = log_decay.shape[0]
     linear_heads = linear_layer(linear_query, linear_key, linear_value, log_decay, norm_gain)
-    softmax_heads = softmax_layer(soft_query, soft_key, soft_value, block_index, block_count, heads)
+    sections = lax.psum(1, CTX)
+    softmax_heads = softmax_layer(
+        soft_query, soft_key, soft_value, block_index, block_count, heads, sections
+    )
     result = (
         lax.all_to_all(linear_heads, "head", split_axis=0, concat_axis=1, tiled=True),
         lax.all_to_all(softmax_heads, "head", split_axis=0, concat_axis=1, tiled=True),
@@ -180,17 +215,21 @@
 
 
 def solution(mesh):
+    ctx, head = mesh.devices.shape
+    split = mesh.devices.reshape(ctx // 16, 8, 2, head)
+    mesh = jax.sharding.Mesh(split, CTX + ("head",))
+    rows = P(CTX, "head")
     in_specs = (
-        P("ctx", "head"),
-        P("ctx", "head"),
-        P("ctx", "head"),
-        P("head", "ctx"),
+        rows,
+        rows,
+        rows,
+        P("head", CTX),
         P("head"),
-        P("ctx", "head"),
-        P("ctx", "head"),
-        P("ctx", "head"),
-        P("ctx", None),
-        P("ctx"),
-    )
-    out_specs = (P(("ctx", "head"), None), P(("ctx", "head"), None))
+        rows,
+        rows,
+        rows,
+        P(CTX, None),
+        P(CTX),
+    )
+    out_specs = (P(CTX + ("head",), None), P(CTX + ("head",), None))
     return jax.shard_map(local, mesh=mesh, in_specs=in_specs, out_specs=out_specs, check_vma=False)

time: 376 us -> 288 us (0.77)
  waiting for transfers between devices: 219 us -> 156 us
  starting transfers between devices: 58.4 us -> 19.5 us
  between operations: 1.13 us -> 14.2 us
    ppermute x17 -> x4, waiting for transfers between devices: 197 us -> 42.1 us  [passed_along(): return lax.ppermute(block, axis, route)]
    all_gather x0 -> x4, waiting for transfers between devices: none -> 91.4 us  [the longest x1 58.7 us: carry_in(): lax.all_gather(packed(chip_state, chip_factor), 'cz')]
    ppermute x17 -> x4, starting transfers between devices: 50.6 us -> 11.6 us  [passed_along(): return lax.ppermute(block, axis, route)]
    select_n x12 -> x1, other arithmetic: 8.28 us -> 0.02 us  [carry_in(): before_factor = jnp.where(here, total_factor, before_factor)]
    add x0 -> x3, other arithmetic: none -> 7.13 us  [the longest x1 4.37 us: carry_in(): prefix_half = before_factor[:, None, None] * above + before]
    slice x1 -> x4, local copies, waits for them, and re-layouts: 0.16 us -> 3.97 us  [the longest x1 1.68 us: carry_in(): first = lax.dynamic_slice_in_dim(pair_states[0], low, half, 0)]
    unnamed x39 -> x41, local copies, waits for them, and re-layouts: 13 us -> 12.4 us
  transfers between devices with their start and end apart: 19 -> 10, of which waited for: 10 -> 8; matrix products, arithmetic and copies ran while one was open for 20% -> 24% of each run, Pallas kernels for 0% -> 0%
where the time goes in v2:
time: 288 us; the launch traced here: 287 us
  waiting for transfers between devices  156 us (54%)
  local copies, waits for them, and re-layouts  48.6 us (17%)
  other arithmetic  27.2 us (9%)
  matrix products  21.2 us (7%)
  starting transfers between devices  19.5 us (7%)
  between operations  14.2 us (5%)
    all_gather x1, waiting for transfers between devices, carry_in(): lax.all_gather(packed(chip_state, chip_factor), 'cz')  58.7 us
    ppermute x4, waiting for transfers between devices, passed_along(): return lax.ppermute(block, axis, route)  42.1 us
    all_gather x1, waiting for transfers between devices, carry_in(): lax.all_gather(packed(final, jnp.exp(section_total)), 'cc')  19.1 us
    all_gather x1, waiting for transfers between devices, carry_in(): lax.all_gather(packed(total, total_factor), 'cy')  13.6 us
    all_to_all x1, waiting for transfers between devices, local(): lax.all_to_all(linear_heads, 'head', split_axis=0, concat_axis=1, tiled=T...  13.3 us
    unnamed x41, local copies, waits for them, and re-layouts  12.4 us
    ppermute x4, starting transfers between devices, passed_along(): return lax.ppermute(block, axis, route)  11.6 us
    all_to_all x1, waiting for transfers between devices, local(): lax.all_to_all(softmax_heads, 'head', split_axis=0, concat_axis=1, tiled=...  9.16 us
  transfers between devices with their start and end apart: 10, of which 8 were waited for; matrix products, arithmetic and copies ran while one was open for 24% of the time, Pallas kernels for 0%

profile of v2, /device:TPU:8, one launch (start us, length us, event | category | flops | bytes accessed | tf_op | source)
XLA Modules:
  0.0 286.9 jit_solution(10776661430231851212)
XLA Ops:
  14.6 19.1 %all-gather.10.cloned.1.call-done = f32[32,136,128]{2,1,0:T(8,128)} async-done(((f32[16,136,128]{2,1,0:T(8,128)}), f32[32,136,128]{2,1,0:T(8,128)}) %all-gather.10.cloned.1.call-update) | async-done | bytes 2228240 | tf_op jit(solution)/shard_map/all_gather | solution.py:75
  37.7 58.7 %all-gather.12.cloned.1.call-done = f32[64,136,128]{2,1,0:T(8,128)} async-done(((f32[8,136,128]{2,1,0:T(8,128)}), f32[64,136,128]{2,1,0:T(8,128)}) %all-gather.12.cloned.1.call-update) | async-done | bytes 4456464 | tf_op jit(solution)/shard_map/all_gather | solution.py:85
  97.5 2.6 fusion.45
  101.1 1.9 collective-permute-start
  105.0 3.2 %collective-permute-start.2 = (bf16[256,2048]{1,0:T(8,128)(2,1)}, bf16[256,2048]{1,0:T(8,128)(2,1)}, u32[]{:S(2)}, u32[]{:S(2)}) collective-permute-start(bf16[256,2048]{1,0:T(8,128)(2,1)} %param.20), channel_id=1, source_target_pairs={{0,8},{4,12},{8,16},{12,20},{16,24},{20,28},{24,32},{28,36},{32,40... | collective-permute-start | bytes 3145736 | tf_op jit(solution)/shard_map/ppermute | solution.py:21
  108.2 4.5 %collective-permute-start.3 = (bf16[256,2048]{1,0:T(8,128)(2,1)}, bf16[256,2048]{1,0:T(8,128)(2,1)}, u32[]{:S(2)}, u32[]{:S(2)}) collective-permute-start(bf16[256,2048]{1,0:T(8,128)(2,1)} %param.20), channel_id=1, source_target_pairs={{0,4},{4,8},{8,12},{12,16},{16,20},{20,24},{24,28},{28,32},{32,36}... | collective-permute-start | bytes 3145736 | tf_op jit(solution)/shard_map/ppermute | solution.py:21
  115.1 2.8 convolution_bitcast_fusion.3
  118.0 2.6 fusion.19
  121.9 2.5 copy.161
  126.3 2.6 fusion.18
  128.9 2.7 collective-permute-done
  131.6 20.2 %collective-permute-done.1 = bf16[256,2048]{1,0:T(8,128)(2,1)} collective-permute-done((bf16[256,2048]{1,0:T(8,128)(2,1)}, bf16[256,2048]{1,0:T(8,128)(2,1)}, u32[]{:S(2)}, u32[]{:S(2)}) %collective-permute-start.1) | collective-permute-done | bytes 1048608 | tf_op jit(solution)/shard_map/ppermute | solution.py:21
  153.5 2.7 copy.160
  156.2 19.2 %collective-permute-done.3 = bf16[256,2048]{1,0:T(8,128)(2,1)} collective-permute-done((bf16[256,2048]{1,0:T(8,128)(2,1)}, bf16[256,2048]{1,0:T(8,128)(2,1)}, u32[]{:S(2)}, u32[]{:S(2)}) %collective-permute-start.3) | collective-permute-done | bytes 1048608 | tf_op jit(solution)/shard_map/ppermute | solution.py:21
  177.1 2.7 copy.162
  179.9 13.6 %all-gather.14.cloned.1.call-done = f32[32,136,128]{2,1,0:T(8,128)} async-done(((f32[8,136,128]{2,1,0:T(8,128)}), f32[32,136,128]{2,1,0:T(8,128)}) %all-gather.14.cloned.1.call-update) | async-done | bytes 2228240 | tf_op jit(solution)/shard_map/all_gather | solution.py:98
  194.5 4.4 %fusion.38 = f32[8,128,128]{2,1,0:T(8,128)} fusion(f32[4,8,136,128]{3,2,1,0:T(8,128)} %bitcast.290, f32[8,128,128]{2,1,0:T(8,128)S(1)} %get-tuple-element.122, f32[8,8,136,128]{3,2,1,0:T(8,128)} %bitcast.271, f32[8]{0:T(128)S(1)} %get-tuple-element.96, f32[8]{0:T(128)S(1)} %get-tuple-element.97, f32[8]{0:T(128)S(1)} %get-tuple-element.98, ...), kind=kLoop, calls=%fused_computation.72 | loop fusion | flops 4063232 | bytes 6291819 | tf_op jit(solution)/shard_map/add | solution.py:104
  198.9 40.5 %while.10 = (s32[]{:T(128)}, bf16[2,128,16,128]{3,2,1,0:T(8,128)(2,1)}, s32[2,5]{1,0:T(2,128)S(1)}, s32[]{:T(128)}, bf16[6,128,16,128]{3,2,1,0:T(8,128)(2,1)}, /...) while((s32[]{:T(128)}, ...), condition=%wide.region_7.9_spmd, body=%wide.region_4.8_spmd.sunk | while | flops 689878016 | bytes 69611904 | solution.py:188
  198.9 2.9 %gather_fusion = bf16[5,128,16,128]{3,2,1,0:T(8,128)(2,1)S(1)} fusion(bf16[6,128,16,128]{3,2,1,0:T(8,128)(2,1)} %get-tuple-element.238, s32[1024]{0:T(1024)S(1)} %pad_clamp_fusion.2), kind=kCustom, calls=%fused_computation.clone.clone.1 | custom fusion | bytes 5242900 | tf_op jit(solution)/shard_map/while/body/eval_jaxpr/jit(_take)/gather | solution.py:185
  201.9 4.4 %gather_fusion.1 = bf16[5,128,16,128]{3,2,1,0:T(8,128)(2,1)} fusion(bf16[6,128,16,128]{3,2,1,0:T(8,128)(2,1)} %get-tuple-element.242, s32[1024]{0:T(1024)S(1)} %pad_clamp_fusion.2), kind=kCustom, calls=%fused_computation.1.clone.clone.1 | custom fusion | bytes 5242900 | tf_op jit(solution)/shard_map/while/body/eval_jaxpr/jit(_take)/gather | solution.py:184
  206.3 2.4 broadcast_select_fusion.10
  215.1 2.6 fusion.102
  219.3 2.9 %gather_fusion = bf16[5,128,16,128]{3,2,1,0:T(8,128)(2,1)S(1)} fusion(bf16[6,128,16,128]{3,2,1,0:T(8,128)(2,1)} %get-tuple-element.238, s32[1024]{0:T(1024)S(1)} %pad_clamp_fusion.2), kind=kCustom, calls=%fused_computation.clone.clone.1 | custom fusion | bytes 5242900 | tf_op jit(solution)/shard_map/while/body/eval_jaxpr/jit(_take)/gather | solution.py:185
  222.2 4.4 %gather_fusion.1 = bf16[5,128,16,128]{3,2,1,0:T(8,128)(2,1)} fusion(bf16[6,128,16,128]{3,2,1,0:T(8,128)(2,1)} %get-tuple-element.242, s32[1024]{0:T(1024)S(1)} %pad_clamp_fusion.2), kind=kCustom, calls=%fused_computation.1.clone.clone.1 | custom fusion | bytes 5242900 | tf_op jit(solution)/shard_map/while/body/eval_jaxpr/jit(_take)/gather | solution.py:184
  226.7 2.3 broadcast_select_fusion.10
  235.2 2.6 fusion.102
  239.4 2.5 all_to_all.32
  241.9 4.2 %all-to-all-start.1 = ((bf16[4,64,2048]{2,1,0:T(8,128)(2,1)}), bf16[4,64,2048]{2,1,0:T(8,128)(2,1)S(1)}, u32[]{:S(2)}, u32[]{:S(2)}) async-start(bf16[4,64,2048]{2,1,0:T(8,128)(2,1)} %all_to_all.32), calls=%async_computation.1 | async-start | bytes 2097152 | tf_op jit(solution)/shard_map/all_to_all | solution.py:212
  246.2 3.4 %multiply_reduce_fusion = (f32[256,16]{0,1:T(8,128)S(1)}, f32[256,16,128]{2,0,1:T(8,128)S(1)}) fusion(f32[16,128,128]{2,1,0:T(8,128)} %all-gather.8.cloned.1.call-done, f32[16]{0:T(128)S(1)} %get-tuple-element.125, pred[]{:T(512)S(6)} %eq.36, f32[2,16,136,128]{3,2,1,0:T(8,128)} %bitcast.274, f32[256,16]{0,1:T(8,128)S(1)} %exponential_bitcast_fusion, ...), kind=kOutput, calls=%fused_computation.36 | convolution fusion | flops 138932224 | bytes 7372865 | tf_op jit(solution)/shard_map/thd,hde->the/dot_general | solution.py:137
  252.3 9.2 %all-to-all-done.1 = bf16[4,64,2048]{2,1,0:T(8,128)(2,1)S(1)} async-done(((bf16[4,64,2048]{2,1,0:T(8,128)(2,1)}), bf16[4,64,2048]{2,1,0:T(8,128)(2,1)S(1)}, u32[]{:S(2)}, u32[]{:S(2)}) %all-to-all-start.1) | async-done | bytes 1048608 | tf_op jit(solution)/shard_map/all_to_all | solution.py:212
  261.4 3.5 %all-to-all-start = ((bf16[4,64,2048]{2,1,0:T(8,128)(2,1)}), bf16[4,64,2048]{2,1,0:T(8,128)(2,1)S(1)}, u32[]{:S(2)}, u32[]{:S(2)}) async-start(bf16[4,64,2048]{2,1,0:T(8,128)(2,1)} %all_to_all.28), calls=%async_computation | async-start | bytes 2097152 | tf_op jit(solution)/shard_map/all_to_all | solution.py:211
  266.0 13.3 %all-to-all-done = bf16[4,64,2048]{2,1,0:T(8,128)(2,1)S(1)} async-done(((bf16[4,64,2048]{2,1,0:T(8,128)(2,1)}), bf16[4,64,2048]{2,1,0:T(8,128)(2,1)S(1)}, u32[]{:S(2)}, u32[]{:S(2)}) %all-to-all-start) | async-done | bytes 1048608 | tf_op jit(solution)/shard_map/all_to_all | solution.py:211
  (136 shorter events, 45.5 us)
Async XLA Ops:
  7.2 0.7 copy-start
  7.2 3.1 %copy-start.11 = (bf16[256,2048]{1,0:T(8,128)(2,1)S(1)}, bf16[256,2048]{1,0:T(8,128)(2,1)}, u32[]{:S(2)}) copy-start(bf16[256,2048]{1,0:T(8,128)(2,1)} %param.16) | copy-start | bytes 3145732
  7.2 26.5 %all-gather.10.cloned.1.call-start = ((), (), s32[]{:S(2)}) async-start(), calls=%async_computation.3 | async-start | bytes 3342336 | tf_op jit(solution)/shard_map/all_gather | solution.py:75
  10.7 2.6 copy-start.6
  11.0 2.3 copy-start.7
  11.3 2.1 copy-start.9
  14.5 81.9 %all-gather.12.cloned.1.call-start = ((), (), s32[]{:S(2)}) async-start(), calls=%async_computation.4 | async-start | bytes 5013504 | tf_op jit(solution)/shard_map/all_gather | solution.py:85
  37.7 155.8 %all-gather.14.cloned.1.call-start = ((), (), s32[]{:S(2)}) async-start(), calls=%async_computation.5 | async-start | bytes 2785280 | tf_op jit(solution)/shard_map/all_gather | solution.py:98
  97.5 15.3 %copy-start.4 = (bf16[256,2048]{1,0:T(8,128)(2,1)S(1)}, bf16[256,2048]{1,0:T(8,128)(2,1)}, u32[]{:S(2)}) copy-start(bf16[256,2048]{1,0:T(8,128)(2,1)} %param.14) | copy-start | bytes 3145732
  101.1 145.1 %all-gather.8.cloned.1.call-start = ((), (), s32[]{:S(2)}) async-start(), calls=%async_computation.2 | async-start | bytes 1572864 | tf_op jit(solution)/shard_map/all_gather | solution.py:105
  101.1 30.5 %collective-permute-start = (bf16[256,2048]{1,0:T(8,128)(2,1)}, bf16[256,2048]{1,0:T(8,128)(2,1)}, u32[]{:S(2)}, u32[]{:S(2)}) collective-permute-start(bf16[256,2048]{1,0:T(8,128)(2,1)} %param.21), channel_id=1, source_target_pairs={{0,8},{4,12},{8,16},{12,20},{16,24},{20,28},{24,32},{28,36},{32,40... | collective-permute-start | bytes 3145736 | tf_op jit(solution)/shard_map/ppermute | solution.py:21
  103.1 48.7 %collective-permute-start.1 = (bf16[256,2048]{1,0:T(8,128)(2,1)}, bf16[256,2048]{1,0:T(8,128)(2,1)}, u32[]{:S(2)}, u32[]{:S(2)}) collective-permute-start(bf16[256,2048]{1,0:T(8,128)(2,1)} %param.21), channel_id=1, source_target_pairs={{0,4},{4,8},{8,12},{12,16},{16,20},{20,24},{24,28},{28,32},{32,36}... | collective-permute-start | bytes 3145736 | tf_op jit(solution)/shard_map/ppermute | solution.py:21
  105.0 51.2 %collective-permute-start.2 = (bf16[256,2048]{1,0:T(8,128)(2,1)}, bf16[256,2048]{1,0:T(8,128)(2,1)}, u32[]{:S(2)}, u32[]{:S(2)}) collective-permute-start(bf16[256,2048]{1,0:T(8,128)(2,1)} %param.20), channel_id=1, source_target_pairs={{0,8},{4,12},{8,16},{12,20},{16,24},{20,28},{24,32},{28,36},{32,40... | collective-permute-start | bytes 3145736 | tf_op jit(solution)/shard_map/ppermute | solution.py:21
  108.2 67.2 %collective-permute-start.3 = (bf16[256,2048]{1,0:T(8,128)(2,1)}, bf16[256,2048]{1,0:T(8,128)(2,1)}, u32[]{:S(2)}, u32[]{:S(2)}) collective-permute-start(bf16[256,2048]{1,0:T(8,128)(2,1)} %param.20), channel_id=1, source_target_pairs={{0,4},{4,8},{8,12},{12,16},{16,20},{20,24},{24,28},{28,32},{32,36}... | collective-permute-start | bytes 3145736 | tf_op jit(solution)/shard_map/ppermute | solution.py:21
  117.9 6.5 %copy-start.8 = (bf16[128,2048]{0,1:T(8,128)(2,1)S(1)}, bf16[128,2048]{0,1:T(8,128)(2,1)}, u32[]{:S(2)}) copy-start(bf16[128,2048]{0,1:T(8,128)(2,1)} %copy-done.7) | copy-start | bytes 1572868
  118.0 6.5 %copy-start.10 = (bf16[128,2048]{0,1:T(8,128)(2,1)S(1)}, bf16[128,2048]{0,1:T(8,128)(2,1)}, u32[]{:S(2)}) copy-start(bf16[128,2048]{0,1:T(8,128)(2,1)} %copy-done.9) | copy-start | bytes 1572868
  126.3 25.5 %copy-start.14 = (bf16[256,2048]{1,0:T(8,128)(2,1)S(1)}, bf16[256,2048]{1,0:T(8,128)(2,1)}, u32[]{:S(2)}) copy-start(bf16[256,2048]{1,0:T(8,128)(2,1)} %param.21) | copy-start | bytes 3145732
  153.5 21.9 %copy-start.15 = (bf16[256,2048]{1,0:T(8,128)(2,1)S(1)}, bf16[256,2048]{1,0:T(8,128)(2,1)}, u32[]{:S(2)}) copy-start(bf16[256,2048]{1,0:T(8,128)(2,1)} %param.20) | copy-start | bytes 3145732
  194.4 4.4 %copy-start.16 = (s32[2,5]{1,0:T(2,128)S(1)}, s32[2,5]{1,0:T(2,128)}, u32[]{:S(2)}) copy-start(s32[2,5]{1,0:T(2,128)} %param.22) | copy-start | bytes 124
  194.4 4.4 %copy-start.18 = (s32[2]{0:T(128)S(1)}, s32[2]{0:T(128)}, u32[]{:S(2)}) copy-start(s32[2]{0:T(128)} %param.23) | copy-start | bytes 28
  208.7 1.2 copy-start.2
  215.1 3.1 %copy-start.12 = (bf16[2,128,16,128]{3,2,1,0:T(8,128)(2,1)S(1)}, bf16[2,128,16,128]{3,2,1,0:T(8,128)(2,1)}, u32[]{:S(2)}) copy-start(bf16[2,128,16,128]{3,2,1,0:T(8,128)(2,1)} %get-tuple-element.225) | copy-start | bytes 3145732 | tf_op jit(solution)/shard_map/while
  218.3 1.0 copy-start.13
  228.9 1.2 copy-start.2
  235.2 3.1 %copy-start.12 = (bf16[2,128,16,128]{3,2,1,0:T(8,128)(2,1)S(1)}, bf16[2,128,16,128]{3,2,1,0:T(8,128)(2,1)}, u32[]{:S(2)}) copy-start(bf16[2,128,16,128]{3,2,1,0:T(8,128)(2,1)} %get-tuple-element.225) | copy-start | bytes 3145732 | tf_op jit(solution)/shard_map/while
  238.4 1.0 copy-start.13
  239.4 6.7 %copy-start.3 = (f32[128,16,128]{2,0,1:T(8,128)S(1)}, f32[128,16,128]{2,0,1:T(8,128)}, u32[]{:S(2)}) copy-start(f32[128,16,128]{2,0,1:T(8,128)} %fusion.18) | copy-start | bytes 3145732
  239.4 6.7 %copy-start.5 = (bf16[256,2048]{1,0:T(8,128)(2,1)S(1)}, bf16[256,2048]{1,0:T(8,128)(2,1)}, u32[]{:S(2)}) copy-start(bf16[256,2048]{1,0:T(8,128)(2,1)} %param.14) | copy-start | bytes 3145732
  241.9 19.6 %all-to-all-start.1 = ((bf16[4,64,2048]{2,1,0:T(8,128)(2,1)}), bf16[4,64,2048]{2,1,0:T(8,128)(2,1)S(1)}, u32[]{:S(2)}, u32[]{:S(2)}) async-start(bf16[4,64,2048]{2,1,0:T(8,128)(2,1)} %all_to_all.32), calls=%async_computation.1 | async-start | bytes 2097152 | tf_op jit(solution)/shard_map/all_to_all | solution.py:212
  246.1 3.4 %copy-start.17 = (f32[2048]{0:T(1024)S(1)}, f32[2048]{0:T(1024)}, u32[]{:S(2)}) copy-start(f32[2048]{0:T(1024)} %param.18) | copy-start | bytes 24580
  261.4 17.9 %all-to-all-start = ((bf16[4,64,2048]{2,1,0:T(8,128)(2,1)}), bf16[4,64,2048]{2,1,0:T(8,128)(2,1)S(1)}, u32[]{:S(2)}, u32[]{:S(2)}) async-start(bf16[4,64,2048]{2,1,0:T(8,128)(2,1)} %all_to_all.28), calls=%async_computation | async-start | bytes 2097152 | tf_op jit(solution)/shard_map/all_to_all | solution.py:211
  265.0 15.4 %copy-start.1 = (f32[16,256]{1,0:T(8,128)S(1)}, f32[16,256]{1,0:T(8,128)}, u32[]{:S(2)}) copy-start(f32[16,256]{1,0:T(8,128)} %param.17) | copy-start | bytes 49156
Sparse Core Ops, SparseCore 0:
  14.7 18.9 all-gather.9
  37.8 58.5 all-gather.11
  101.2 92.2 all-gather.13
  199.0 10.4 all-gather.7

commit v3 on v2

--- a/solution.py
+++ b/solution.py
@@ -67,18 +67,26 @@
     return both[..., :width, :], both[..., width, 0]
 
 
+def swapped(block):
+    return lax.ppermute(block, "cc", [(0, 1), (1, 0)])
+
+
 def carry_in(final, section_total):
     heads, width, _ = final.shape
     half = heads // 2
     core, row, column = (lax.axis_index("cc"), lax.axis_index("cz"), lax.axis_index("cy"))
-    pair_states, pair_factors = unpacked(
-        lax.all_gather(packed(final, jnp.exp(section_total)), "cc"), width
-    )
+    factor = jnp.exp(section_total)
+    other_state, other_factor = unpacked(swapped(packed(final, factor)), width)
+    on_first = core == 0
+    first_state = jnp.where(on_first, final, other_state)
+    first_all = jnp.where(on_first, factor, other_factor)
+    second_state = jnp.where(on_first, other_state, final)
+    second_all = jnp.where(on_first, other_factor, factor)
     low = core * half
-    first = lax.dynamic_slice_in_dim(pair_states[0], low, half, 0)
-    second = lax.dynamic_slice_in_dim(pair_states[1], low, half, 0)
-    first_factor = lax.dynamic_slice_in_dim(pair_factors[0], low, half, 0)
-    second_factor = lax.dynamic_slice_in_dim(pair_factors[1], low, half, 0)
+    first = lax.dynamic_slice_in_dim(first_state, low, half, 0)
+    second = lax.dynamic_slice_in_dim(second_state, low, half, 0)
+    first_factor = lax.dynamic_slice_in_dim(first_all, low, half, 0)
+    second_factor = lax.dynamic_slice_in_dim(second_all, low, half, 0)
     chip_state = second_factor[:, None, None] * first + second
     chip_factor = first_factor * second_factor
     row_states, row_factors = unpacked(
@@ -102,9 +110,14 @@
         joined = column_factors[y][:, None, None] * above + column_states[y]
         above = jnp.where(y < column, joined, above)
     prefix_half = before_factor[:, None, None] * above + before
-    prefix = lax.all_gather(prefix_half, "cc", axis=0, tiled=True)
-    later = pair_factors[0][:, None, None] * prefix + pair_states[0]
-    return jnp.where(core == 0, prefix, later)
+    other_half = swapped(prefix_half)
+    prefix = jnp.where(
+        on_first,
+        jnp.concatenate([prefix_half, other_half], axis=0),
+        jnp.concatenate([other_half, prefix_half], axis=0),
+    )
+    later = first_all[:, None, None] * prefix + first_state
+    return jnp.where(on_first, prefix, later)
 
 
 def linear_layer(linear_query, linear_key, linear_value, log_decay, norm_gain):
@@ -142,17 +155,12 @@
     return normed.astype(jnp.bfloat16).reshape(length, columns)
 
 
-def attend(query_blk, keys_sel, values_sel, index_row, count_row, row_global):
+def attend(query_blk, keys_sel, values_sel, allowed):
     width = query_blk.shape[-1]
     inverse_root = 1.0 / math.sqrt(width)
     scores = (
         jnp.einsum("thd,kjhd->htkj", query_blk, keys_sel, preferred_element_type=jnp.float32)
         * inverse_root
-    )
-    slot_used = jnp.arange(index_row.shape[0], dtype=jnp.int32) < count_row
-    off_diagonal = jnp.logical_not(index_row == row_global)
-    allowed = slot_used[None, :, None] & (
-        off_diagonal[None, :, None] | causal_mask(query_blk.shape[0])[:, None, :]
     )
     scores = jnp.where(allowed[None], scores, -jnp.inf)
     highest = jnp.max(scores, axis=(2, 3), keepdims=True)
@@ -165,6 +173,7 @@
 def softmax_layer(soft_query, soft_key, soft_value, block_index, block_count, heads, sections):
     length, columns = soft_query.shape
     per_section = length // BLK
+    slots = block_index.shape[1]
     own_pair = (soft_key, soft_value)
     pieces = []
     for distance in range(WIN_SEC, 0, -1):
@@ -176,17 +185,27 @@
     section = lax.axis_index(CTX)
     first_block = (section - WIN_SEC) * per_section
     query_blocks = to_blocks(soft_query, heads)
-    own_rows = section * per_section + jnp.arange(per_section, dtype=jnp.int32)
-
-    def one_block(inputs):
-        query_blk, index_row, count_row, row_global = inputs
-        local_row = index_row - first_block
-        keys_sel = jnp.take(key_blocks, local_row, axis=0)
-        values_sel = jnp.take(value_blocks, local_row, axis=0)
-        return attend(query_blk, keys_sel, values_sel, index_row, count_row, row_global)
-
-    outputs = lax.map(one_block, (query_blocks, block_index, block_count, own_rows))
-    return outputs.reshape(length, columns)
+    causal = causal_mask(BLK)
+    slot_ids = jnp.arange(slots, dtype=jnp.int32)
+    outputs = []
+    for b in range(per_section):
+        row_global = section * per_section + b
+        low = b + WIN_SEC * per_section - (slots - 1)
+        candidates = first_block + low + jnp.arange(slots, dtype=jnp.int32)
+        used = slot_ids < block_count[b]
+        matches = (block_index[b][None, :] == candidates[:, None]) & used[None, :]
+        named = jnp.any(matches, axis=1)
+        off_diagonal = candidates != row_global
+        allowed = named[None, :, None] & (off_diagonal[None, :, None] | causal[:, None, :])
+        outputs.append(
+            attend(
+                query_blocks[b],
+                key_blocks[low : low + slots],
+                value_blocks[low : low + slots],
+                allowed,
+            )
+        )
+    return jnp.concatenate(outputs, axis=0).reshape(length, columns)
 
 
 def local(

time: 288 us -> 247 us (0.86)
  waiting for transfers between devices: 156 us -> 124 us
  local copies, waits for them, and re-layouts: 48.6 us -> 39.2 us
  other arithmetic: 27.2 us -> 20.6 us
  matrix products: 21.2 us -> 24.9 us
    all_gather x1, waiting for transfers between devices: 58.7 us -> 0.01 us  [carry_in(): lax.all_gather(packed(chip_state, chip_factor), 'cz')]
    ppermute x4, waiting for transfers between devices: 42.1 us -> 81.1 us  [passed_along(): return lax.ppermute(block, axis, route)]
    all_gather x2 -> x0, waiting for transfers between devices: 19.1 us -> none  [the longest x1 19.1 us: carry_in(): lax.all_gather(packed(final, jnp.exp(section_total)), 'cc')]
    gather x4 -> x0, local copies, waits for them, and re-layouts: 14.7 us -> none  [the longest x2 8.86 us: one_block(): keys_sel = jnp.take(key_blocks, local_row, axis=0)]
    unnamed x41 -> x50, local copies, waits for them, and re-layouts: 12.4 us -> 23.3 us
    select_n x2, other arithmetic: 4.72 us -> 1.05 us  [the longest x1 1.05 us: carry_in(): first_all = jnp.where(on_first, factor, other_factor)]
    unnamed x2 -> x0, other arithmetic: 3.42 us -> none
    all_gather x1, waiting for transfers between devices: 13.6 us -> 17 us  [carry_in(): lax.all_gather(packed(total, total_factor), 'cy')]
  transfers between devices with their start and end apart: 10 -> 10, of which waited for: 8 -> 8; matrix products, arithmetic and copies ran while one was open for 24% -> 22% of each run, Pallas kernels for 0% -> 0%
where the time goes in v3:
time: 247 us; the launch traced here: 245 us
  waiting for transfers between devices  124 us (50%)
  local copies, waits for them, and re-layouts  39.2 us (16%)
  matrix products  24.9 us (10%)
  starting transfers between devices  21.3 us (9%)
  other arithmetic  20.6 us (8%)
  between operations  14.6 us (6%)
    ppermute x4, waiting for transfers between devices, passed_along(): return lax.ppermute(block, axis, route)  81.1 us
    unnamed x50, local copies, waits for them, and re-layouts  23.3 us
    all_gather x1, waiting for transfers between devices, carry_in(): lax.all_gather(packed(total, total_factor), 'cy')  17 us
    all_to_all x1, waiting for transfers between devices, local(): lax.all_to_all(linear_heads, 'head', split_axis=0, concat_axis=1, tiled=T...  13.9 us
    ppermute x4, starting transfers between devices, passed_along(): return lax.ppermute(block, axis, route)  13.4 us
    all_to_all x1, waiting for transfers between devices, local(): lax.all_to_all(softmax_heads, 'head', split_axis=0, concat_axis=1, tiled=...  9.18 us
    dot_general x2, matrix products, attend(): jnp.einsum('htkj,kjhd->thd', weights, values_sel, preferred_element_type=...  6.39 us
    dot_general x2, matrix products, block_output(): jnp.einsum('thd,hde->the', decayed_query, carried.astype(jnp.bfloat16), p...  5.12 us
  transfers between devices with their start and end apart: 10, of which 8 were waited for; matrix products, arithmetic and copies ran while one was open for 22% of the time, Pallas kernels for 0%

profile of v3, /device:TPU:8, one launch (start us, length us, event | category | flops | bytes accessed | tf_op | source)
XLA Modules:
  0.0 244.8 jit_solution(3519546591789854583)
XLA Ops:
  15.4 1.7 convolution_add_fusion
  18.2 3.1 %collective-permute-done = f32[16,136,128]{2,1,0:T(8,128)} collective-permute-done((f32[16,136,128]{2,1,0:T(8,128)}, f32[16,136,128]{2,1,0:T(8,128)}, u32[]{:S(2)}, u32[]{:S(2)}) %collective-permute-start) | collective-permute-done | bytes 1114144 | tf_op jit(solution)/shard_map/ppermute | solution.py:71
  22.5 1.4 fusion.95
  25.9 3.8 %collective-permute-start.4 = (bf16[256,2048]{1,0:T(8,128)(2,1)}, bf16[256,2048]{1,0:T(8,128)(2,1)}, u32[]{:S(2)}, u32[]{:S(2)}) collective-permute-start(bf16[256,2048]{1,0:T(8,128)(2,1)} %param.16), channel_id=1, source_target_pairs={{0,8},{4,12},{8,16},{12,20},{16,24},{20,28},{24,32},{28,36},{32,40... | collective-permute-start | bytes 3145736 | tf_op jit(solution)/shard_map/ppermute | solution.py:21
  29.8 1.9 collective-permute-start.5
  31.7 3.8 %collective-permute-start.2 = (bf16[256,2048]{1,0:T(8,128)(2,1)}, bf16[256,2048]{1,0:T(8,128)(2,1)}, u32[]{:S(2)}, u32[]{:S(2)}) collective-permute-start(bf16[256,2048]{1,0:T(8,128)(2,1)} %param.17), channel_id=1, source_target_pairs={{0,8},{4,12},{8,16},{12,20},{16,24},{20,28},{24,32},{28,36},{32,40... | collective-permute-start | bytes 3145736 | tf_op jit(solution)/shard_map/ppermute | solution.py:21
  35.5 3.8 %collective-permute-start.3 = (bf16[256,2048]{1,0:T(8,128)(2,1)}, bf16[256,2048]{1,0:T(8,128)(2,1)}, u32[]{:S(2)}, u32[]{:S(2)}) collective-permute-start(bf16[256,2048]{1,0:T(8,128)(2,1)} %param.17), channel_id=1, source_target_pairs={{0,4},{4,8},{8,12},{12,16},{16,20},{20,24},{24,28},{28,32},{32,36}... | collective-permute-start | bytes 3145736 | tf_op jit(solution)/shard_map/ppermute | solution.py:21
  39.4 2.2 fusion.97
  41.8 1.3 copy.222
  44.5 1.8 convolution_bitcast_fusion.3
  46.3 2.6 %fusion.22 = f32[128,16,128]{2,0,1:T(8,128)} fusion(f32[128,16,128]{2,0,1:T(8,128)} %convolution_bitcast_fusion.3, bf16[128,16,128]{0,2,1:T(8,128)(2,1)S(1)} %bitcast.288, f32[128,16]{0,1:T(8,128)S(1)} %get-tuple-element.43), kind=kOutput, calls=%fused_computation.39 | convolution fusion | flops 68157440 | bytes 2629632 | tf_op jit(solution)/shard_map/thd,hde->the/dot_general | solution.py:52
  48.8 3.0 %convolution_bitcast_fusion.1 = f32[128,16,128]{2,0,1:T(8,128)} fusion(bf16[128,16,128]{0,2,1:T(8,128)(2,1)} %bitcast.290, bf16[128,16,128]{0,2,1:T(8,128)(2,1)S(1)} %bitcast.285, bf16[128,16,128]{0,2,1:T(8,128)(2,1)} %bitcast.292, f32[16,128]{1,0:T(8,128)S(1)} %get-tuple-element.47, pred[128,128]{1,0:T(8,128)(4,1)S(1)} %iota_compare_fusion), kind=kOutput, calls=%fused_computation.36 | convolution fusion | flops 135528448 | bytes 2646016 | tf_op jit(solution)/shard_map/htj,jhd->thd/dot_general | solution.py:48
  54.1 2.6 %fusion.21 = f32[128,16,128]{2,0,1:T(8,128)} fusion(f32[128,16,128]{2,0,1:T(8,128)} %convolution_bitcast_fusion.1, bf16[128,16,128]{0,2,1:T(8,128)(2,1)S(1)} %bitcast.286, f32[128,16]{0,1:T(8,128)S(1)} %get-tuple-element.41, f32[16,128,128]{2,1,0:T(8,128)S(1)} %convolution_add_fusion.1), kind=kOutput, calls=%fused_computation.34 | convolution fusion | flops 68419584 | bytes 3678208 | tf_op jit(solution)/shard_map/thd,hde->the/dot_general | solution.py:52
  58.9 12.8 %collective-permute-done.4 = bf16[256,2048]{1,0:T(8,128)(2,1)} collective-permute-done((bf16[256,2048]{1,0:T(8,128)(2,1)}, bf16[256,2048]{1,0:T(8,128)(2,1)}, u32[]{:S(2)}, u32[]{:S(2)}) %collective-permute-start.4) | collective-permute-done | bytes 1048608 | tf_op jit(solution)/shard_map/ppermute | solution.py:21
  71.7 1.3 constant_dynamic-update-slice_fusion.5
  73.0 41.6 %collective-permute-done.5 = bf16[256,2048]{1,0:T(8,128)(2,1)} collective-permute-done((bf16[256,2048]{1,0:T(8,128)(2,1)}, bf16[256,2048]{1,0:T(8,128)(2,1)}, u32[]{:S(2)}, u32[]{:S(2)}) %collective-permute-start.5) | collective-permute-done | bytes 1048608 | tf_op jit(solution)/shard_map/ppermute | solution.py:21
  114.7 1.3 constant_dynamic-update-slice_fusion.4
  117.9 26.1 %collective-permute-done.3 = bf16[256,2048]{1,0:T(8,128)(2,1)} collective-permute-done((bf16[256,2048]{1,0:T(8,128)(2,1)}, bf16[256,2048]{1,0:T(8,128)(2,1)}, u32[]{:S(2)}, u32[]{:S(2)}) %collective-permute-start.3) | collective-permute-done | bytes 1048608 | tf_op jit(solution)/shard_map/ppermute | solution.py:21
  145.4 3.5 %slice_bitcast_fusion.2 = (bf16[80,8,16,128]{3,1,2,0:T(8,128)(2,1)}, bf16[80,8,16,128]{3,1,2,0:T(8,128)(2,1)}) fusion(bf16[768,2048]{1,0:T(8,128)(2,1)S(1)} %constant_dynamic-update-slice_fusion.3), kind=kLoop, calls=%fused_computation.12 | loop fusion | bytes 10485760
  150.0 3.3 %fusion.57 = (f32[8,128,128]{2,1,0:T(8,128)S(1)}, f32[8,128,128]{2,1,0:T(8,128)}) fusion(f32[8,8,136,128]{3,2,1,0:T(8,128)} %bitcast.273, f32[8]{0:T(128)S(1)} %get-tuple-element.4, f32[8]{0:T(128)S(1)} %get-tuple-element.3, f32[8]{0:T(128)S(1)} %get-tuple-element.6, f32[8]{0:T(128)S(1)} %get-tuple-element.5, f32[8]{0:T(128)S(1)} %get-tuple-element.56, ...), kind=kLoop, calls=%fused_computation.82 | loop fusion | flops 1966080 | bytes 5243136 | tf_op jit(solution)/shard_map/add | solution.py:103
  155.5 2.5 %copy.236 = bf16[80,8,16,128]{3,2,1,0:T(8,128)(2,1)S(1)} copy(bf16[80,8,16,128]{3,1,2,0:T(8,128)(2,1)} %get-tuple-element.24) | data formatting | bytes 5242880
  162.4 1.3 fusion.2
  163.7 1.3 fusion.3
  167.4 3.6 %fusion.31 = bf16[128,16,128]{2,0,1:T(8,128)(2,1)} fusion(f32[16,5,128,128]{3,2,1,0:T(8,128)S(1)} %get-tuple-element.62, f32[16,128]{1,0:T(8,128)S(1)} %fusion, f32[16,128]{1,0:T(8,128)S(1)} %get-tuple-element.61, pred[128,5,128]{0,2,1:T(8,128)(4,1)S(1)} %get-tuple-element.36, bf16[5,128,16,128]{3,2,1,0:T(8,128)(2,1)S(1)} %bitcast.278), kind=kOutput, calls=%fused_computation.46 | convolution fusion | flops 342360064 | bytes 8486912 | tf_op jit(solution)/shard_map/htkj,kjhd->thd/dot_general | solution.py:169
  171.0 17.0 %all-gather.7.cloned.1.call-done = f32[32,136,128]{2,1,0:T(8,128)} async-done(((f32[8,136,128]{2,1,0:T(8,128)}), f32[32,136,128]{2,1,0:T(8,128)}) %all-gather.7.cloned.1.call-update) | async-done | bytes 2228240 | tf_op jit(solution)/shard_map/all_gather | solution.py:106
  189.0 4.6 %fusion.50 = f32[8,128,128]{2,1,0:T(8,128)} fusion(f32[4,8,136,128]{3,2,1,0:T(8,128)} %bitcast.294, f32[8,128,128]{2,1,0:T(8,128)S(1)} %copy-done.7, f32[8,8,136,128]{3,2,1,0:T(8,128)} %bitcast.274, f32[8]{0:T(128)S(1)} %get-tuple-element.11, f32[8]{0:T(128)S(1)} %get-tuple-element.12, f32[8]{0:T(128)S(1)} %get-tuple-element.13, f32[8]{0:T(128)S(1)} %get-tuple-element.10, ...), kind=kLoop, calls=%fused_computation.71 | loop fusion | flops 4063232 | bytes 6291819 | tf_op jit(solution)/shard_map/add | solution.py:112
  193.6 2.8 %fusion.34 = bf16[128,16,128]{2,0,1:T(8,128)(2,1)S(1)} fusion(f32[16,5,128,128]{3,2,1,0:T(8,128)S(1)} %copy-done.4, f32[16,128]{1,0:T(8,128)S(1)} %fusion.1, f32[16,128]{1,0:T(8,128)S(1)} %get-tuple-element.59, pred[128,5,128]{0,2,1:T(8,128)(4,1)S(1)} %get-tuple-element.37, bf16[5,128,16,128]{3,2,1,0:T(8,128)(2,1)S(1)} %bitcast.277), kind=kOutput, calls=%fused_computation.47 | convolution fusion | flops 342360064 | bytes 8486912 | tf_op jit(solution)/shard_map/htkj,kjhd->thd/dot_general | solution.py:169
  198.5 4.2 %all-to-all-start.1 = ((bf16[4,64,2048]{2,1,0:T(8,128)(2,1)}), bf16[4,64,2048]{2,1,0:T(8,128)(2,1)S(1)}, u32[]{:S(2)}, u32[]{:S(2)}) async-start(bf16[4,64,2048]{2,1,0:T(8,128)(2,1)} %all_to_all.32), calls=%async_computation.1 | async-start | bytes 2097152 | tf_op jit(solution)/shard_map/all_to_all | solution.py:231
  202.8 3.8 %multiply_reduce_fusion = (f32[256,16]{0,1:T(8,128)S(1)}, f32[256,16,128]{2,0,1:T(8,128)S(1)}) fusion(f32[16,128,128]{2,1,0:T(8,128)S(1)} %copy-done.6, f32[8,128,128]{2,1,0:T(8,128)} %fusion.50, f32[8,128,128]{2,1,0:T(8,128)} %collective-permute-done.1, f32[16]{0:T(128)S(1)} %get-tuple-element.14, pred[]{:T(512)S(6)} %eq.55, ...), kind=kOutput, calls=%fused_computation.29 | convolution fusion | flops 139718656 | bytes 7372865 | tf_op jit(solution)/shard_map/thd,hde->the/dot_general | solution.py:150
  209.3 9.2 %all-to-all-done.1 = bf16[4,64,2048]{2,1,0:T(8,128)(2,1)S(1)} async-done(((bf16[4,64,2048]{2,1,0:T(8,128)(2,1)}), bf16[4,64,2048]{2,1,0:T(8,128)(2,1)S(1)}, u32[]{:S(2)}, u32[]{:S(2)}) %all-to-all-start.1) | async-done | bytes 1048608 | tf_op jit(solution)/shard_map/all_to_all | solution.py:231
  218.5 3.5 %all-to-all-start = ((bf16[4,64,2048]{2,1,0:T(8,128)(2,1)}), bf16[4,64,2048]{2,1,0:T(8,128)(2,1)S(1)}, u32[]{:S(2)}, u32[]{:S(2)}) async-start(bf16[4,64,2048]{2,1,0:T(8,128)(2,1)} %all_to_all.28), calls=%async_computation | async-start | bytes 2097152 | tf_op jit(solution)/shard_map/all_to_all | solution.py:230
  223.0 13.9 %all-to-all-done = bf16[4,64,2048]{2,1,0:T(8,128)(2,1)S(1)} async-done(((bf16[4,64,2048]{2,1,0:T(8,128)(2,1)}), bf16[4,64,2048]{2,1,0:T(8,128)(2,1)S(1)}, u32[]{:S(2)}, u32[]{:S(2)}) %all-to-all-start) | async-done | bytes 1048608 | tf_op jit(solution)/shard_map/all_to_all | solution.py:230
  (109 shorter events, 39.5 us)
Async XLA Ops:
  7.2 0.7 copy-start
  7.2 141.7 %all-gather.5.cloned.1.call-start = ((), (), s32[]{:S(2)}) async-start(), calls=%async_computation.2 | async-start | bytes 5013504 | tf_op jit(solution)/shard_map/all_gather | solution.py:93
  18.2 3.1 %collective-permute-start = (f32[16,136,128]{2,1,0:T(8,128)}, f32[16,136,128]{2,1,0:T(8,128)}, u32[]{:S(2)}, u32[]{:S(2)}) collective-permute-start(f32[16,136,128]{2,1,0:T(8,128)} %pad_maximum_fusion), channel_id=1, source_target_pairs={{0,4},{4,0},{1,5},{5,1},{2,6},{6,2},{3,7},{7,3},{8,12},{12,8},{9,1... | collective-permute-start | bytes 3342344 | tf_op jit(solution)/shard_map/ppermute | solution.py:71
  23.9 1.0 copy-start.5
  24.9 18.3 %copy-start.14 = (s32[2]{0:T(128)S(1)}, s32[2]{0:T(128)}, u32[]{:S(2)}) copy-start(s32[2]{0:T(128)} %param.19) | copy-start | bytes 28
  24.9 19.6 %copy-start.15 = (s32[2,5]{1,0:T(2,128)S(1)}, s32[2,5]{1,0:T(2,128)}, u32[]{:S(2)}) copy-start(s32[2,5]{1,0:T(2,128)} %param.18) | copy-start | bytes 124
  25.9 162.2 %all-gather.7.cloned.1.call-start = ((), (), s32[]{:S(2)}) async-start(), calls=%async_computation.3 | async-start | bytes 2785280 | tf_op jit(solution)/shard_map/all_gather | solution.py:106
  25.9 45.8 %collective-permute-start.4 = (bf16[256,2048]{1,0:T(8,128)(2,1)}, bf16[256,2048]{1,0:T(8,128)(2,1)}, u32[]{:S(2)}, u32[]{:S(2)}) collective-permute-start(bf16[256,2048]{1,0:T(8,128)(2,1)} %param.16), channel_id=1, source_target_pairs={{0,8},{4,12},{8,16},{12,20},{16,24},{20,28},{24,32},{28,36},{32,40... | collective-permute-start | bytes 3145736 | tf_op jit(solution)/shard_map/ppermute | solution.py:21
  29.8 84.9 %collective-permute-start.5 = (bf16[256,2048]{1,0:T(8,128)(2,1)}, bf16[256,2048]{1,0:T(8,128)(2,1)}, u32[]{:S(2)}, u32[]{:S(2)}) collective-permute-start(bf16[256,2048]{1,0:T(8,128)(2,1)} %param.16), channel_id=1, source_target_pairs={{0,4},{4,8},{8,12},{12,16},{16,20},{20,24},{24,28},{28,32},{32,36}... | collective-permute-start | bytes 3145736 | tf_op jit(solution)/shard_map/ppermute | solution.py:21
  31.7 84.9 %collective-permute-start.2 = (bf16[256,2048]{1,0:T(8,128)(2,1)}, bf16[256,2048]{1,0:T(8,128)(2,1)}, u32[]{:S(2)}, u32[]{:S(2)}) collective-permute-start(bf16[256,2048]{1,0:T(8,128)(2,1)} %param.17), channel_id=1, source_target_pairs={{0,8},{4,12},{8,16},{12,20},{16,24},{20,28},{24,32},{28,36},{32,40... | collective-permute-start | bytes 3145736 | tf_op jit(solution)/shard_map/ppermute | solution.py:21
  35.5 108.5 %collective-permute-start.3 = (bf16[256,2048]{1,0:T(8,128)(2,1)}, bf16[256,2048]{1,0:T(8,128)(2,1)}, u32[]{:S(2)}, u32[]{:S(2)}) collective-permute-start(bf16[256,2048]{1,0:T(8,128)(2,1)} %param.17), channel_id=1, source_target_pairs={{0,4},{4,8},{8,12},{12,16},{16,20},{20,24},{24,28},{28,32},{32,36}... | collective-permute-start | bytes 3145736 | tf_op jit(solution)/shard_map/ppermute | solution.py:21
  56.9 59.1 %copy-start.9 = (bf16[256,2048]{1,0:T(8,128)(2,1)S(1)}, bf16[256,2048]{1,0:T(8,128)(2,1)}, u32[]{:S(2)}) copy-start(bf16[256,2048]{1,0:T(8,128)(2,1)} %param.16) | copy-start | bytes 3145732
  158.8 1.7 copy-start.2
  161.4 1.0 copy-start.11
  162.4 1.3 copy-start.10
  165.0 2.4 copy-start.3
  167.4 21.6 %copy-start.7 = (f32[8,128,128]{2,1,0:T(8,128)S(1)}, f32[8,128,128]{2,1,0:T(8,128)}, u32[]{:S(2)}) copy-start(f32[8,128,128]{2,1,0:T(8,128)} %get-tuple-element.19) | copy-start | bytes 1572868
  189.0 4.6 %copy-start.4 = (f32[16,5,128,128]{3,2,1,0:T(8,128)S(1)}, f32[16,5,128,128]{3,2,1,0:T(8,128)}, u32[]{:S(2)}) copy-start(f32[16,5,128,128]{3,2,1,0:T(8,128)} %copy-done.3) | copy-start | bytes 15728644
  193.6 9.2 %collective-permute-start.1 = (f32[8,128,128]{2,1,0:T(8,128)}, f32[8,128,128]{2,1,0:T(8,128)}, u32[]{:S(2)}, u32[]{:S(2)}) collective-permute-start(f32[8,128,128]{2,1,0:T(8,128)} %fusion.50), channel_id=1, source_target_pairs={{0,4},{4,0},{1,5},{5,1},{2,6},{6,2},{3,7},{7,3},{8,12},{12,8},{9,1... | collective-permute-start | bytes 1572872 | tf_op jit(solution)/shard_map/ppermute | solution.py:71
  193.6 2.8 %copy-start.12 = (bf16[128,16,128]{2,0,1:T(8,128)(2,1)S(1)}, bf16[128,16,128]{2,0,1:T(8,128)(2,1)}, u32[]{:S(2)}) copy-start(bf16[128,16,128]{2,0,1:T(8,128)(2,1)} %fusion.31) | copy-start | bytes 1572868
  196.5 6.3 %copy-start.6 = (f32[16,128,128]{2,1,0:T(8,128)S(1)}, f32[16,128,128]{2,1,0:T(8,128)}, u32[]{:S(2)}) copy-start(f32[16,128,128]{2,1,0:T(8,128)} %copy-done.5) | copy-start | bytes 3145732
  196.5 6.2 %copy-start.8 = (f32[128,16,128]{2,0,1:T(8,128)S(1)}, f32[128,16,128]{2,0,1:T(8,128)}, u32[]{:S(2)}) copy-start(f32[128,16,128]{2,0,1:T(8,128)} %fusion.21) | copy-start | bytes 3145732
  198.5 20.0 %all-to-all-start.1 = ((bf16[4,64,2048]{2,1,0:T(8,128)(2,1)}), bf16[4,64,2048]{2,1,0:T(8,128)(2,1)S(1)}, u32[]{:S(2)}, u32[]{:S(2)}) async-start(bf16[4,64,2048]{2,1,0:T(8,128)(2,1)} %all_to_all.32), calls=%async_computation.1 | async-start | bytes 2097152 | tf_op jit(solution)/shard_map/all_to_all | solution.py:231
  202.7 3.8 %copy-start.13 = (f32[2048]{0:T(1024)S(1)}, f32[2048]{0:T(1024)}, u32[]{:S(2)}) copy-start(f32[2048]{0:T(1024)} %param.14) | copy-start | bytes 24580
  208.0 29.9 %copy-start.1 = (f32[16,256]{1,0:T(8,128)S(1)}, f32[16,256]{1,0:T(8,128)}, u32[]{:S(2)}) copy-start(f32[16,256]{1,0:T(8,128)} %param.13) | copy-start | bytes 49156
  218.5 18.4 %all-to-all-start = ((bf16[4,64,2048]{2,1,0:T(8,128)(2,1)}), bf16[4,64,2048]{2,1,0:T(8,128)(2,1)S(1)}, u32[]{:S(2)}, u32[]{:S(2)}) async-start(bf16[4,64,2048]{2,1,0:T(8,128)(2,1)} %all_to_all.28), calls=%async_computation | async-start | bytes 2097152 | tf_op jit(solution)/shard_map/all_to_all | solution.py:230
Sparse Core Ops, SparseCore 0:
  26.0 99.3 all-gather.4
  154.4 33.6 all-gather.6

commit v4 on v3

--- a/solution.py
+++ b/solution.py
@@ -175,9 +175,11 @@
     per_section = length // BLK
     slots = block_index.shape[1]
     own_pair = (soft_key, soft_value)
-    pieces = []
-    for distance in range(WIN_SEC, 0, -1):
-        pieces.append(passed_along((own_pair[0], own_pair[1]), CTX, distance, sections))
+    farther = passed_along(own_pair, CTX, 2, sections)
+    on_first = lax.axis_index("cc") == 0
+    handed = jax.tree.map(lambda own, far: jnp.where(on_first, own, far), own_pair, farther)
+    nearer = swapped(handed)
+    pieces = [farther, nearer]
     window_key = jnp.concatenate([piece[0] for piece in pieces] + [soft_key], axis=0)
     window_value = jnp.concatenate([piece[1] for piece in pieces] + [soft_value], axis=0)
     key_blocks = to_blocks(window_key, heads)

time: 247 us -> 234 us (0.947)
  waiting for transfers between devices: 124 us -> 108 us
  starting transfers between devices: 21.3 us -> 15.5 us
  other arithmetic: 20.6 us -> 26.1 us
  local copies, waits for them, and re-layouts: 39.2 us -> 44 us
    ppermute x4 -> x2, waiting for transfers between devices: 81.1 us -> 64.7 us  [passed_along(): return lax.ppermute(block, axis, route)]
    select_n x0 -> x2, other arithmetic: none -> 6.52 us  [softmax_layer(): jnp.where(on_first, own, far)]
    ppermute x4 -> x2, starting transfers between devices: 13.4 us -> 7.66 us  [passed_along(): return lax.ppermute(block, axis, route)]
    unnamed x50 -> x58, local copies, waits for them, and re-layouts: 23.3 us -> 26.1 us
  transfers between devices with their start and end apart: 10 -> 10, of which waited for: 8 -> 6; matrix products, arithmetic and copies ran while one was open for 22% -> 27% of each run, Pallas kernels for 0% -> 0%
where the time goes in v4:
time: 234 us; the launch traced here: 232 us
  waiting for transfers between devices  108 us (46%)
  local copies, waits for them, and re-layouts  44 us (19%)
  other arithmetic  26.1 us (11%)
  matrix products  24.4 us (10%)
  starting transfers between devices  15.5 us (7%)
  between operations  14.6 us (6%)
    ppermute x2, waiting for transfers between devices, passed_along(): return lax.ppermute(block, axis, route)  64.7 us
    unnamed x58, local copies, waits for them, and re-layouts  26.1 us
    all_gather x1, waiting for transfers between devices, carry_in(): lax.all_gather(packed(total, total_factor), 'cy')  16.6 us
    all_to_all x1, waiting for transfers between devices, local(): lax.all_to_all(linear_heads, 'head', split_axis=0, concat_axis=1, tiled=T...  13.9 us
    all_to_all x1, waiting for transfers between devices, local(): lax.all_to_all(softmax_heads, 'head', split_axis=0, concat_axis=1, tiled=...  9.3 us
    ppermute x2, starting transfers between devices, passed_along(): return lax.ppermute(block, axis, route)  7.66 us
    dot_general x2, matrix products, attend(): jnp.einsum('htkj,kjhd->thd', weights, values_sel, preferred_element_type=...  6.6 us
    select_n x2, other arithmetic, softmax_layer(): jnp.where(on_first, own, far)  6.52 us
  transfers between devices with their start and end apart: 10, of which 6 were waited for; matrix products, arithmetic and copies ran while one was open for 27% of the time, Pallas kernels for 0%

profile of v4, /device:TPU:8, one launch (start us, length us, event | category | flops | bytes accessed | tf_op | source)
XLA Modules:
  0.0 232.2 jit_solution(3740708738520989533)
XLA Ops:
  16.4 1.7 convolution_add_fusion
  19.2 3.1 %collective-permute-done = f32[16,136,128]{2,1,0:T(8,128)} collective-permute-done((f32[16,136,128]{2,1,0:T(8,128)}, f32[16,136,128]{2,1,0:T(8,128)}, u32[]{:S(2)}, u32[]{:S(2)}) %collective-permute-start) | collective-permute-done | bytes 1114144 | tf_op jit(solution)/shard_map/ppermute | solution.py:71
  23.4 1.5 fusion.95
  26.9 3.8 %collective-permute-start.4 = (bf16[256,2048]{1,0:T(8,128)(2,1)S(1)}, bf16[256,2048]{1,0:T(8,128)(2,1)}, u32[]{:S(2)}, u32[]{:S(2)}) collective-permute-start(bf16[256,2048]{1,0:T(8,128)(2,1)S(1)} %copy-done.7), channel_id=1, source_target_pairs={{0,8},{4,12},{8,16},{12,20},{16,24},{20,28},{24,32},{28,36},{32,40... | collective-permute-start | bytes 3145736 | tf_op jit(solution)/shard_map/ppermute | solution.py:21
  30.8 3.8 %collective-permute-start.2 = (bf16[256,2048]{1,0:T(8,128)(2,1)}, bf16[256,2048]{1,0:T(8,128)(2,1)}, u32[]{:S(2)}, u32[]{:S(2)}) collective-permute-start(bf16[256,2048]{1,0:T(8,128)(2,1)} %param.17), channel_id=1, source_target_pairs={{0,8},{4,12},{8,16},{12,20},{16,24},{20,28},{24,32},{28,36},{32,40... | collective-permute-start | bytes 3145736 | tf_op jit(solution)/shard_map/ppermute | solution.py:21
  34.6 2.1 fusion.97
  37.8 1.8 convolution_bitcast_fusion.3
  39.5 2.6 %fusion.22 = f32[128,16,128]{2,0,1:T(8,128)} fusion(f32[128,16,128]{2,0,1:T(8,128)} %convolution_bitcast_fusion.3, bf16[128,16,128]{0,2,1:T(8,128)(2,1)S(1)} %bitcast.288, f32[128,16]{0,1:T(8,128)S(1)} %get-tuple-element.47), kind=kOutput, calls=%fused_computation.39 | convolution fusion | flops 68157440 | bytes 2629632 | tf_op jit(solution)/shard_map/thd,hde->the/dot_general | solution.py:52
  44.7 1.8 convolution_bitcast_fusion.1
  46.7 2.3 fusion.96
  49.0 23.3 %collective-permute-done.4 = bf16[256,2048]{1,0:T(8,128)(2,1)} collective-permute-done((bf16[256,2048]{1,0:T(8,128)(2,1)S(1)}, bf16[256,2048]{1,0:T(8,128)(2,1)}, u32[]{:S(2)}, u32[]{:S(2)}) %collective-permute-start.4) | collective-permute-done | bytes 1048608 | tf_op jit(solution)/shard_map/ppermute | solution.py:21
  72.3 3.1 %broadcast_select_fusion = (bf16[256,2048]{1,0:T(8,128)(2,1)}, bf16[768,2048]{1,0:T(8,128)(2,1)S(1)}) fusion(bf16[256,2048]{1,0:T(8,128)(2,1)} %param.16, bf16[256,2048]{1,0:T(8,128)(2,1)} %collective-permute-done.4, pred[]{:T(512)S(6)} %eq.56), kind=kLoop, calls=%fused_computation.65 | loop fusion | flops 524287 | bytes 4194305 | tf_op jit(solution)/shard_map/jit(_where)/select_n | solution.py:180
  75.3 41.4 %collective-permute-done.2 = bf16[256,2048]{1,0:T(8,128)(2,1)} collective-permute-done((bf16[256,2048]{1,0:T(8,128)(2,1)}, bf16[256,2048]{1,0:T(8,128)(2,1)}, u32[]{:S(2)}, u32[]{:S(2)}) %collective-permute-start.2) | collective-permute-done | bytes 1048608 | tf_op jit(solution)/shard_map/ppermute | solution.py:21
  116.7 3.5 %broadcast_select_fusion.1 = (bf16[256,2048]{1,0:T(8,128)(2,1)}, bf16[768,2048]{1,0:T(8,128)(2,1)}) fusion(bf16[256,2048]{1,0:T(8,128)(2,1)} %param.17, bf16[256,2048]{1,0:T(8,128)(2,1)} %collective-permute-done.2, pred[]{:T(512)S(6)} %eq.56), kind=kLoop, calls=%fused_computation.66 | loop fusion | flops 524287 | bytes 4194305 | tf_op jit(solution)/shard_map/jit(_where)/select_n | solution.py:180
  120.3 2.1 copy.228
  122.4 2.0 copy.229
  124.6 3.1 %fusion.21 = f32[128,16,128]{2,0,1:T(8,128)} fusion(f32[128,16,128]{2,0,1:T(8,128)} %convolution_bitcast_fusion.1, bf16[128,16,128]{0,2,1:T(8,128)(2,1)} %bitcast.286, f32[128,16]{0,1:T(8,128)S(1)} %get-tuple-element.45, f32[16,128,128]{2,1,0:T(8,128)} %copy-done.4), kind=kOutput, calls=%fused_computation.34 | convolution fusion | flops 68419584 | bytes 3678208 | tf_op jit(solution)/shard_map/thd,hde->the/dot_general | solution.py:52
  129.2 2.4 %constant_dynamic-update-slice_fusion.1 = bf16[768,2048]{1,0:T(8,128)(2,1)} fusion(bf16[768,2048]{1,0:T(8,128)(2,1)} %get-tuple-element.31, bf16[256,2048]{1,0:T(8,128)(2,1)} %collective-permute-done.3), kind=kLoop, calls=%fused_computation.129 | loop fusion | bytes 2097152
  131.5 3.5 %slice_bitcast_fusion.2 = (bf16[80,8,16,128]{3,1,2,0:T(8,128)(2,1)}, bf16[80,8,16,128]{3,1,2,0:T(8,128)(2,1)}) fusion(bf16[768,2048]{1,0:T(8,128)(2,1)S(1)} %constant_dynamic-update-slice_fusion.3), kind=kLoop, calls=%fused_computation.12 | loop fusion | bytes 10485760
  136.1 2.6 %fusion.57 = (f32[8,128,128]{2,1,0:T(8,128)S(1)}, f32[8,128,128]{2,1,0:T(8,128)S(1)}) fusion(f32[8,8,136,128]{3,2,1,0:T(8,128)} %bitcast.273, f32[8]{0:T(128)S(1)} %get-tuple-element.4, f32[8]{0:T(128)S(1)} %get-tuple-element.3, f32[8]{0:T(128)S(1)} %get-tuple-element.6, f32[8]{0:T(128)S(1)} %get-tuple-element.5, f32[8]{0:T(128)S(1)} %get-tuple-element.60, ...), kind=kLoop, calls=%fused_computation.84 | loop fusion | flops 1966080 | bytes 5243136 | tf_op jit(solution)/shard_map/add | solution.py:103
  139.7 2.3 constant_dynamic-update-slice_fusion
  142.8 3.6 %slice_bitcast_fusion.3 = (bf16[80,8,16,128]{3,1,2,0:T(8,128)(2,1)S(1)}, bf16[80,8,16,128]{3,1,2,0:T(8,128)(2,1)S(1)}) fusion(bf16[768,2048]{1,0:T(8,128)(2,1)} %constant_dynamic-update-slice_fusion), kind=kLoop, calls=%fused_computation.13 | loop fusion | bytes 10485760
  151.4 1.3 fusion.3
  155.1 3.8 %fusion.31 = bf16[128,16,128]{2,0,1:T(8,128)(2,1)} fusion(f32[16,5,128,128]{3,2,1,0:T(8,128)S(1)} %get-tuple-element.66, f32[16,128]{1,0:T(8,128)S(1)} %fusion, f32[16,128]{1,0:T(8,128)S(1)} %get-tuple-element.65, pred[128,5,128]{0,2,1:T(8,128)(4,1)S(1)} %get-tuple-element.40, bf16[5,128,16,128]{3,2,1,0:T(8,128)(2,1)S(1)} %bitcast.278), kind=kOutput, calls=%fused_computation.46 | convolution fusion | flops 342360064 | bytes 8486912 | tf_op jit(solution)/shard_map/htkj,kjhd->thd/dot_general | solution.py:169
  158.9 16.6 %all-gather.7.cloned.1.call-done = f32[32,136,128]{2,1,0:T(8,128)} async-done(((f32[8,136,128]{2,1,0:T(8,128)}), f32[32,136,128]{2,1,0:T(8,128)}) %all-gather.7.cloned.1.call-update) | async-done | bytes 2228240 | tf_op jit(solution)/shard_map/all_gather | solution.py:106
  176.5 4.5 %fusion.50 = f32[8,128,128]{2,1,0:T(8,128)} fusion(f32[4,8,136,128]{3,2,1,0:T(8,128)} %bitcast.294, f32[8,128,128]{2,1,0:T(8,128)S(1)} %get-tuple-element.19, f32[8,8,136,128]{3,2,1,0:T(8,128)} %bitcast.274, f32[8]{0:T(128)S(1)} %get-tuple-element.11, f32[8]{0:T(128)S(1)} %get-tuple-element.12, f32[8]{0:T(128)S(1)} %get-tuple-element.13, ...), kind=kLoop, calls=%fused_computation.73 | loop fusion | flops 4063232 | bytes 6291819 | tf_op jit(solution)/shard_map/add | solution.py:112
  181.0 2.8 %fusion.34 = bf16[128,16,128]{2,0,1:T(8,128)(2,1)S(1)} fusion(f32[16,5,128,128]{3,2,1,0:T(8,128)S(1)} %copy-done.6, f32[16,128]{1,0:T(8,128)S(1)} %fusion.1, f32[16,128]{1,0:T(8,128)S(1)} %get-tuple-element.63, pred[128,5,128]{0,2,1:T(8,128)(4,1)S(1)} %get-tuple-element.41, bf16[5,128,16,128]{3,2,1,0:T(8,128)(2,1)S(1)} %bitcast.277), kind=kOutput, calls=%fused_computation.47 | convolution fusion | flops 342360064 | bytes 8486912 | tf_op jit(solution)/shard_map/htkj,kjhd->thd/dot_general | solution.py:169
  185.9 4.2 %all-to-all-start.1 = ((bf16[4,64,2048]{2,1,0:T(8,128)(2,1)}), bf16[4,64,2048]{2,1,0:T(8,128)(2,1)S(1)}, u32[]{:S(2)}, u32[]{:S(2)}) async-start(bf16[4,64,2048]{2,1,0:T(8,128)(2,1)} %all_to_all.32), calls=%async_computation.1 | async-start | bytes 2097152 | tf_op jit(solution)/shard_map/all_to_all | solution.py:233
  190.2 3.7 %multiply_reduce_fusion = (f32[256,16]{0,1:T(8,128)S(1)}, f32[256,16,128]{2,0,1:T(8,128)S(1)}) fusion(f32[16,128,128]{2,1,0:T(8,128)S(1)} %copy-done.10, f32[8,128,128]{2,1,0:T(8,128)} %fusion.50, f32[8,128,128]{2,1,0:T(8,128)} %collective-permute-done.1, f32[16]{0:T(128)S(1)} %get-tuple-element.14, pred[]{:T(512)S(6)} %eq.56, ...), kind=kOutput, calls=%fused_computation.29 | convolution fusion | flops 139718656 | bytes 7372865 | tf_op jit(solution)/shard_map/thd,hde->the/dot_general | solution.py:150
  196.6 9.3 %all-to-all-done.1 = bf16[4,64,2048]{2,1,0:T(8,128)(2,1)S(1)} async-done(((bf16[4,64,2048]{2,1,0:T(8,128)(2,1)}), bf16[4,64,2048]{2,1,0:T(8,128)(2,1)S(1)}, u32[]{:S(2)}, u32[]{:S(2)}) %all-to-all-start.1) | async-done | bytes 1048608 | tf_op jit(solution)/shard_map/all_to_all | solution.py:233
  205.9 3.5 %all-to-all-start = ((bf16[4,64,2048]{2,1,0:T(8,128)(2,1)}), bf16[4,64,2048]{2,1,0:T(8,128)(2,1)S(1)}, u32[]{:S(2)}, u32[]{:S(2)}) async-start(bf16[4,64,2048]{2,1,0:T(8,128)(2,1)} %all_to_all.28), calls=%async_computation | async-start | bytes 2097152 | tf_op jit(solution)/shard_map/all_to_all | solution.py:232
  210.5 13.9 %all-to-all-done = bf16[4,64,2048]{2,1,0:T(8,128)(2,1)S(1)} async-done(((bf16[4,64,2048]{2,1,0:T(8,128)(2,1)}), bf16[4,64,2048]{2,1,0:T(8,128)(2,1)S(1)}, u32[]{:S(2)}, u32[]{:S(2)}) %all-to-all-start) | async-done | bytes 1048608 | tf_op jit(solution)/shard_map/all_to_all | solution.py:232
  (119 shorter events, 36.6 us)
Async XLA Ops:
  7.2 0.7 copy-start
  7.2 127.9 %all-gather.5.cloned.1.call-start = ((), (), s32[]{:S(2)}) async-start(), calls=%async_computation.2 | async-start | bytes 5013504 | tf_op jit(solution)/shard_map/all_gather | solution.py:93
  15.4 1.0 copy-start.4
  19.2 3.1 %collective-permute-start = (f32[16,136,128]{2,1,0:T(8,128)}, f32[16,136,128]{2,1,0:T(8,128)}, u32[]{:S(2)}, u32[]{:S(2)}) collective-permute-start(f32[16,136,128]{2,1,0:T(8,128)} %pad_maximum_fusion), channel_id=1, source_target_pairs={{0,4},{4,0},{1,5},{5,1},{2,6},{6,2},{3,7},{7,3},{8,12},{12,8},{9,1... | collective-permute-start | bytes 3342344 | tf_op jit(solution)/shard_map/ppermute | solution.py:71
  23.4 3.5 %copy-start.7 = (bf16[256,2048]{1,0:T(8,128)(2,1)S(1)}, bf16[256,2048]{1,0:T(8,128)(2,1)}, u32[]{:S(2)}) copy-start(bf16[256,2048]{1,0:T(8,128)(2,1)} %param.16) | copy-start | bytes 3145732
  24.9 1.0 copy-start.9
  24.9 12.1 %copy-start.19 = (s32[2]{0:T(128)S(1)}, s32[2]{0:T(128)}, u32[]{:S(2)}) copy-start(s32[2]{0:T(128)} %param.19) | copy-start | bytes 28
  24.9 12.7 %copy-start.20 = (s32[2,5]{1,0:T(2,128)S(1)}, s32[2,5]{1,0:T(2,128)}, u32[]{:S(2)}) copy-start(s32[2,5]{1,0:T(2,128)} %param.18) | copy-start | bytes 124
  26.9 148.6 %all-gather.7.cloned.1.call-start = ((), (), s32[]{:S(2)}) async-start(), calls=%async_computation.3 | async-start | bytes 2785280 | tf_op jit(solution)/shard_map/all_gather | solution.py:106
  26.9 45.3 %collective-permute-start.4 = (bf16[256,2048]{1,0:T(8,128)(2,1)S(1)}, bf16[256,2048]{1,0:T(8,128)(2,1)}, u32[]{:S(2)}, u32[]{:S(2)}) collective-permute-start(bf16[256,2048]{1,0:T(8,128)(2,1)S(1)} %copy-done.7), channel_id=1, source_target_pairs={{0,8},{4,12},{8,16},{12,20},{16,24},{20,28},{24,32},{28,36},{32,40... | collective-permute-start | bytes 3145736 | tf_op jit(solution)/shard_map/ppermute | solution.py:21
  30.8 86.0 %collective-permute-start.2 = (bf16[256,2048]{1,0:T(8,128)(2,1)}, bf16[256,2048]{1,0:T(8,128)(2,1)}, u32[]{:S(2)}, u32[]{:S(2)}) collective-permute-start(bf16[256,2048]{1,0:T(8,128)(2,1)} %param.17), channel_id=1, source_target_pairs={{0,8},{4,12},{8,16},{12,20},{16,24},{20,28},{24,32},{28,36},{32,40... | collective-permute-start | bytes 3145736 | tf_op jit(solution)/shard_map/ppermute | solution.py:21
  37.8 6.9 %copy-start.12 = (bf16[128,2048]{0,1:T(8,128)(2,1)S(1)}, bf16[128,2048]{0,1:T(8,128)(2,1)}, u32[]{:S(2)}) copy-start(bf16[128,2048]{0,1:T(8,128)(2,1)} %copy.227) | copy-start | bytes 1572868
  39.5 5.1 %copy-start.13 = (bf16[128,2048]{0,1:T(8,128)(2,1)S(1)}, bf16[128,2048]{0,1:T(8,128)(2,1)}, u32[]{:S(2)}) copy-start(bf16[128,2048]{0,1:T(8,128)(2,1)} %copy.226) | copy-start | bytes 1572868
  44.1 4.9 %copy-start.11 = (bf16[128,2048]{0,1:T(8,128)(2,1)}, bf16[128,2048]{0,1:T(8,128)(2,1)S(1)}, u32[]{:S(2)}) copy-start(bf16[128,2048]{0,1:T(8,128)(2,1)S(1)} %copy.225) | copy-start | bytes 1572868
  75.3 52.4 %collective-permute-start.5 = (bf16[256,2048]{1,0:T(8,128)(2,1)}, bf16[256,2048]{1,0:T(8,128)(2,1)}, u32[]{:S(2)}, u32[]{:S(2)}) collective-permute-start(bf16[256,2048]{1,0:T(8,128)(2,1)} %get-tuple-element.32), channel_id=1, source_target_pairs={{0,4},{4,0},{1,5},{5,1},{2,6},{6,2},{3,7},{7,3},{8,12},{12,8},{9,1... | collective-permute-start | bytes 3145736 | tf_op jit(solution)/shard_map/ppermute | solution.py:71
  120.2 9.0 %collective-permute-start.3 = (bf16[256,2048]{1,0:T(8,128)(2,1)}, bf16[256,2048]{1,0:T(8,128)(2,1)}, u32[]{:S(2)}, u32[]{:S(2)}) collective-permute-start(bf16[256,2048]{1,0:T(8,128)(2,1)} %get-tuple-element.30), channel_id=1, source_target_pairs={{0,4},{4,0},{1,5},{5,1},{2,6},{6,2},{3,7},{7,3},{8,12},{12,8},{9,1... | collective-permute-start | bytes 3145736 | tf_op jit(solution)/shard_map/ppermute | solution.py:71
  124.5 4.6 %copy-start.8 = (bf16[256,2048]{1,0:T(8,128)(2,1)S(1)}, bf16[256,2048]{1,0:T(8,128)(2,1)}, u32[]{:S(2)}) copy-start(bf16[256,2048]{1,0:T(8,128)(2,1)} %param.16) | copy-start | bytes 3145732
  138.7 3.3 %copy-start.3 = (bf16[80,8,16,128]{3,1,2,0:T(8,128)(2,1)S(1)}, bf16[80,8,16,128]{3,1,2,0:T(8,128)(2,1)}, u32[]{:S(2)}) copy-start(bf16[80,8,16,128]{3,1,2,0:T(8,128)(2,1)} %get-tuple-element.24) | copy-start | bytes 7864324
  146.4 1.7 copy-start.2
  149.0 1.0 copy-start.16
  150.1 1.3 copy-start.15
  152.7 2.4 %copy-start.5 = (f32[16,5,128,128]{3,2,1,0:T(8,128)}, f32[16,5,128,128]{3,2,1,0:T(8,128)S(1)}, u32[]{:S(2)}) copy-start(f32[16,5,128,128]{3,2,1,0:T(8,128)S(1)} %get-tuple-element.64) | copy-start | bytes 15728644
  176.5 4.5 %copy-start.6 = (f32[16,5,128,128]{3,2,1,0:T(8,128)S(1)}, f32[16,5,128,128]{3,2,1,0:T(8,128)}, u32[]{:S(2)}) copy-start(f32[16,5,128,128]{3,2,1,0:T(8,128)} %copy-done.5) | copy-start | bytes 15728644
  181.0 9.2 %collective-permute-start.1 = (f32[8,128,128]{2,1,0:T(8,128)}, f32[8,128,128]{2,1,0:T(8,128)}, u32[]{:S(2)}, u32[]{:S(2)}) collective-permute-start(f32[8,128,128]{2,1,0:T(8,128)} %fusion.50), channel_id=1, source_target_pairs={{0,4},{4,0},{1,5},{5,1},{2,6},{6,2},{3,7},{7,3},{8,12},{12,8},{9,1... | collective-permute-start | bytes 1572872 | tf_op jit(solution)/shard_map/ppermute | solution.py:71
  181.0 2.8 %copy-start.17 = (bf16[128,16,128]{2,0,1:T(8,128)(2,1)S(1)}, bf16[128,16,128]{2,0,1:T(8,128)(2,1)}, u32[]{:S(2)}) copy-start(bf16[128,16,128]{2,0,1:T(8,128)(2,1)} %fusion.31) | copy-start | bytes 1572868
  183.9 6.3 %copy-start.10 = (f32[16,128,128]{2,1,0:T(8,128)S(1)}, f32[16,128,128]{2,1,0:T(8,128)}, u32[]{:S(2)}) copy-start(f32[16,128,128]{2,1,0:T(8,128)} %copy-done.9) | copy-start | bytes 3145732
  183.9 6.2 %copy-start.14 = (f32[128,16,128]{2,0,1:T(8,128)S(1)}, f32[128,16,128]{2,0,1:T(8,128)}, u32[]{:S(2)}) copy-start(f32[128,16,128]{2,0,1:T(8,128)} %fusion.21) | copy-start | bytes 3145732
  185.9 20.0 %all-to-all-start.1 = ((bf16[4,64,2048]{2,1,0:T(8,128)(2,1)}), bf16[4,64,2048]{2,1,0:T(8,128)(2,1)S(1)}, u32[]{:S(2)}, u32[]{:S(2)}) async-start(bf16[4,64,2048]{2,1,0:T(8,128)(2,1)} %all_to_all.32), calls=%async_computation.1 | async-start | bytes 2097152 | tf_op jit(solution)/shard_map/all_to_all | solution.py:233
  190.2 3.7 %copy-start.18 = (f32[2048]{0:T(1024)S(1)}, f32[2048]{0:T(1024)}, u32[]{:S(2)}) copy-start(f32[2048]{0:T(1024)} %param.14) | copy-start | bytes 24580
  195.3 30.1 %copy-start.1 = (f32[16,256]{1,0:T(8,128)S(1)}, f32[16,256]{1,0:T(8,128)}, u32[]{:S(2)}) copy-start(f32[16,256]{1,0:T(8,128)} %param.13) | copy-start | bytes 49156
  205.9 18.4 %all-to-all-start = ((bf16[4,64,2048]{2,1,0:T(8,128)(2,1)}), bf16[4,64,2048]{2,1,0:T(8,128)(2,1)S(1)}, u32[]{:S(2)}, u32[]{:S(2)}) async-start(bf16[4,64,2048]{2,1,0:T(8,128)(2,1)} %all_to_all.28), calls=%async_computation | async-start | bytes 2097152 | tf_op jit(solution)/shard_map/all_to_all | solution.py:232
Sparse Core Ops, SparseCore 0:
  27.0 95.9 all-gather.4
  139.8 35.6 all-gather.6

commit v5 on v4

--- a/solution.py
+++ b/solution.py
@@ -71,7 +71,7 @@
     return lax.ppermute(block, "cc", [(0, 1), (1, 0)])
 
 
-def carry_in(final, section_total):
+def carry_in(final, section_total, held):
     heads, width, _ = final.shape
     half = heads // 2
     core, row, column = (lax.axis_index("cc"), lax.axis_index("cz"), lax.axis_index("cy"))
@@ -102,9 +102,9 @@
         before_factor = jnp.where(here, total_factor, before_factor)
         total = row_factors[z][:, None, None] * total + row_states[z]
         total_factor = total_factor * row_factors[z]
-    column_states, column_factors = unpacked(
-        lax.all_gather(packed(total, total_factor), "cy"), width
-    )
+    column_packed = lax.all_gather(packed(total, total_factor), "cy")
+    column_packed, held = lax.optimization_barrier((column_packed, held))
+    column_states, column_factors = unpacked(column_packed, width)
     above = jnp.zeros_like(chip_state)
     for y in range(column_states.shape[0]):
         joined = column_factors[y][:, None, None] * above + column_states[y]
@@ -117,10 +117,10 @@
         jnp.concatenate([other_half, prefix_half], axis=0),
     )
     later = first_all[:, None, None] * prefix + first_state
-    return jnp.where(on_first, prefix, later)
-
-
-def linear_layer(linear_query, linear_key, linear_value, log_decay, norm_gain):
+    return jnp.where(on_first, prefix, later), held
+
+
+def linear_layer(linear_query, linear_key, linear_value, log_decay, norm_gain, held):
     length, columns = linear_query.shape
     heads = log_decay.shape[0]
     width = columns // heads
@@ -138,7 +138,7 @@
     for b in range(blocks_here):
         before.append(carried)
         carried = block_state(carried, keys_blocks[b], values_blocks[b], cumulative[b], totals[b])
-    incoming = carry_in(carried, section_total)
+    incoming, held = carry_in(carried, section_total, held)
     outputs = [
         block_output(before[b], query_blocks[b], keys_blocks[b], values_blocks[b], cumulative[b])
         for b in range(blocks_here)
@@ -152,7 +152,7 @@
     )
     square_mean = jnp.mean(raw * raw, axis=2, keepdims=True)
     normed = raw * lax.rsqrt(square_mean + EPS) * norm_gain.reshape(heads, width)
-    return normed.astype(jnp.bfloat16).reshape(length, columns)
+    return normed.astype(jnp.bfloat16).reshape(length, columns), held
 
 
 def attend(query_blk, keys_sel, values_sel, allowed):
@@ -223,7 +223,9 @@
     block_count,
 ):
     heads = log_decay.shape[0]
-    linear_heads = linear_layer(linear_query, linear_key, linear_value, log_decay, norm_gain)
+    linear_heads, (soft_key, soft_value) = linear_layer(
+        linear_query, linear_key, linear_value, log_decay, norm_gain, (soft_key, soft_value)
+    )
     sections = lax.psum(1, CTX)
     softmax_heads = softmax_layer(
         soft_query, soft_key, soft_value, block_index, block_count, heads, sections

time: 234 us -> 240 us (1.026)
  waiting for transfers between devices: 108 us -> 122 us
  matrix products: 24.4 us -> 20.1 us
  other arithmetic: 26.1 us -> 23.1 us
    all_gather x1, waiting for transfers between devices: 0.01 us -> 60.2 us  [carry_in(): lax.all_gather(packed(chip_state, chip_factor), 'cz')]
    ppermute x2, waiting for transfers between devices: 64.7 us -> 36.3 us  [passed_along(): return lax.ppermute(block, axis, route)]
    all_to_all x1, waiting for transfers between devices: 13.9 us -> 0.01 us  [local(): lax.all_to_all(linear_heads, 'head', split_axis=0, concat_axis=1, tiled=T...]
    all_gather x1, waiting for transfers between devices: 16.6 us -> 9.38 us  [carry_in(): column_packed = lax.all_gather(packed(total, total_factor), 'cy')]
    all_to_all x1, waiting for transfers between devices: 9.3 us -> 13.2 us  [local(): lax.all_to_all(softmax_heads, 'head', split_axis=0, concat_axis=1, tiled=...]
    unnamed x58, local copies, waits for them, and re-layouts: 26.1 us -> 22.8 us
    select_n x2, other arithmetic: 6.52 us -> 3.39 us  [softmax_layer(): jnp.where(on_first, own, far)]
    dot_general x2, matrix products: 5.72 us -> 3.17 us  [block_output(): jnp.einsum('thd,hde->the', decayed_query, carried.astype(jnp.bfloat16), p...]
  transfers between devices with their start and end apart: 10 -> 10, of which waited for: 6 -> 6; matrix products, arithmetic and copies ran while one was open for 27% -> 26% of each run, Pallas kernels for 0% -> 0%
where the time goes in v5:
time: 240 us; the launch traced here: 239 us
  waiting for transfers between devices  122 us (51%)
  local copies, waits for them, and re-layouts  43 us (18%)
  other arithmetic  23.1 us (10%)
  matrix products  20.1 us (8%)
  starting transfers between devices  16.1 us (7%)
  between operations  14.6 us (6%)
    all_gather x1, waiting for transfers between devices, carry_in(): lax.all_gather(packed(chip_state, chip_factor), 'cz')  60.2 us
    ppermute x2, waiting for transfers between devices, passed_along(): return lax.ppermute(block, axis, route)  36.3 us
    unnamed x58, local copies, waits for them, and re-layouts  22.8 us
    all_to_all x1, waiting for transfers between devices, local(): lax.all_to_all(softmax_heads, 'head', split_axis=0, concat_axis=1, tiled=...  13.2 us
    all_gather x1, waiting for transfers between devices, carry_in(): column_packed = lax.all_gather(packed(total, total_factor), 'cy')  9.38 us
    ppermute x2, starting transfers between devices, passed_along(): return lax.ppermute(block, axis, route)  6.88 us
    dot_general x2, matrix products, block_output(): jnp.einsum('htj,jhd->thd', mixing, values_blk, preferred_element_type=jnp...  5.98 us
    dot_general x2, matrix products, attend(): jnp.einsum('htkj,kjhd->thd', weights, values_sel, preferred_element_type=...  5.81 us
  transfers between devices with their start and end apart: 10, of which 6 were waited for; matrix products, arithmetic and copies ran while one was open for 26% of the time, Pallas kernels for 0%

profile of v5, /device:TPU:8, one launch (start us, length us, event | category | flops | bytes accessed | tf_op | source)
XLA Modules:
  0.0 239.0 jit_solution(5883756062206185870)
XLA Ops:
  11.7 1.5 fusion.93
  15.9 3.1 %collective-permute-done = f32[16,136,128]{2,1,0:T(8,128)} collective-permute-done((f32[16,136,128]{2,1,0:T(8,128)}, f32[16,136,128]{2,1,0:T(8,128)}, u32[]{:S(2)}, u32[]{:S(2)}) %collective-permute-start) | collective-permute-done | bytes 1114144 | tf_op jit(solution)/shard_map/ppermute | solution.py:71
  22.7 60.2 %all-gather.5.cloned.1.call-done = f32[64,136,128]{2,1,0:T(8,128)} async-done(((f32[8,136,128]{2,1,0:T(8,128)}), f32[64,136,128]{2,1,0:T(8,128)}) %all-gather.5.cloned.1.call-update) | async-done | bytes 4456464 | tf_op jit(solution)/shard_map/all_gather | solution.py:93
  84.0 3.3 %fusion.47 = (f32[8,128,128]{2,1,0:T(8,128)S(1)}, f32[8,128,128]{2,1,0:T(8,128)}) fusion(f32[8,8,136,128]{3,2,1,0:T(8,128)} %bitcast.265, f32[8]{0:T(128)S(1)} %get-tuple-element.10, f32[8]{0:T(128)S(1)} %get-tuple-element.9, f32[8]{0:T(128)S(1)} %get-tuple-element.8, f32[8]{0:T(128)S(1)} %get-tuple-element.11, f32[8]{0:T(128)S(1)} %get-tuple-element.66, ...), kind=kLoop, calls=%fused_computation.70 | loop fusion | flops 1966080 | bytes 5243136 | tf_op jit(solution)/shard_map/add | solution.py:103
  89.3 2.2 copy.225
  91.5 2.0 copy.222
  93.7 2.3 fusion.91
  95.9 2.0 copy.229
  98.0 2.1 copy.228
  102.4 2.8 %convolution_bitcast_fusion.3 = f32[128,16,128]{2,0,1:T(8,128)} fusion(bf16[128,16,128]{0,2,1:T(8,128)(2,1)S(1)} %bitcast.273, bf16[128,16,128]{0,2,1:T(8,128)(2,1)} %bitcast.278, bf16[128,16,128]{0,2,1:T(8,128)(2,1)S(1)} %bitcast.275, f32[16,128]{1,0:T(8,128)S(1)} %get-tuple-element.56, pred[128,128]{1,0:T(8,128)(4,1)S(1)} %iota_compare_fusion), kind=kOutput, calls=%fused_computation.40 | convolution fusion | flops 135528448 | bytes 2646016 | tf_op jit(solution)/shard_map/htj,jhd->thd/dot_general | solution.py:48
  105.3 2.8 %fusion.22 = f32[128,16,128]{2,0,1:T(8,128)} fusion(f32[128,16,128]{2,0,1:T(8,128)} %convolution_bitcast_fusion.3, bf16[128,16,128]{0,2,1:T(8,128)(2,1)} %bitcast.279, f32[128,16]{0,1:T(8,128)S(1)} %get-tuple-element.53), kind=kOutput, calls=%fused_computation.39 | convolution fusion | flops 68157440 | bytes 2629632 | tf_op jit(solution)/shard_map/thd,hde->the/dot_general | solution.py:52
  108.1 3.2 %convolution_bitcast_fusion.1 = f32[128,16,128]{2,0,1:T(8,128)} fusion(bf16[128,16,128]{0,2,1:T(8,128)(2,1)} %bitcast.281, bf16[128,16,128]{0,2,1:T(8,128)(2,1)} %bitcast.276, bf16[128,16,128]{0,2,1:T(8,128)(2,1)} %bitcast.283, f32[16,128]{1,0:T(8,128)S(1)} %get-tuple-element.57, pred[128,128]{1,0:T(8,128)(4,1)S(1)} %iota_compare_fusion), kind=kOutput, calls=%fused_computation.36 | convolution fusion | flops 135528448 | bytes 2646016 | tf_op jit(solution)/shard_map/htj,jhd->thd/dot_general | solution.py:48
  111.2 9.4 %all-gather.7.cloned.1.call-done = f32[32,136,128]{2,1,0:T(8,128)} async-done(((f32[8,136,128]{2,1,0:T(8,128)}), f32[32,136,128]{2,1,0:T(8,128)}) %all-gather.7.cloned.1.call-update) | async-done | bytes 2228240 | tf_op jit(solution)/shard_map/all_gather | solution.py:105
  121.6 3.4 %collective-permute-start.4 = (bf16[256,2048]{1,0:T(8,128)(2,1)S(1)}, bf16[256,2048]{1,0:T(8,128)(2,1)S(1)}, u32[]{:S(2)}, u32[]{:S(2)}) collective-permute-start(bf16[256,2048]{1,0:T(8,128)(2,1)S(1)} %copy-done.2), channel_id=1, source_target_pairs={{0,8},{4,12},{8,16},{12,20},{16,24},{20,28},{24,32},{28,36},{32,40... | collective-permute-start | bytes 3145736 | tf_op jit(solution)/shard_map/ppermute | solution.py:21
  125.0 3.8 %fusion.58 = f32[8,128,128]{2,1,0:T(8,128)S(1)} fusion(f32[8,128,128]{2,1,0:T(8,128)} %get-tuple-element.25, f32[4,8,136,128]{3,2,1,0:T(8,128)} %bitcast.285, f32[8,8,136,128]{3,2,1,0:T(8,128)} %bitcast.266, f32[8]{0:T(128)S(1)} %get-tuple-element.17, f32[8]{0:T(128)S(1)} %get-tuple-element.18, f32[8]{0:T(128)S(1)} %get-tuple-element.19, ...), kind=kLoop, calls=%fused_computation.90 | loop fusion | flops 4063232 | bytes 6291819 | tf_op jit(solution)/shard_map/add | solution.py:112
  130.1 3.5 %collective-permute-start.2 = (bf16[256,2048]{1,0:T(8,128)(2,1)S(1)}, bf16[256,2048]{1,0:T(8,128)(2,1)S(1)}, u32[]{:S(2)}, u32[]{:S(2)}) collective-permute-start(bf16[256,2048]{1,0:T(8,128)(2,1)S(1)} %copy-done.3), channel_id=1, source_target_pairs={{0,8},{4,12},{8,16},{12,20},{16,24},{20,28},{24,32},{28,36},{32,40... | collective-permute-start | bytes 3145736 | tf_op jit(solution)/shard_map/ppermute | solution.py:21
  133.6 1.5 multiply_reduce_fusion
  135.1 16.5 %collective-permute-done.4 = bf16[256,2048]{1,0:T(8,128)(2,1)S(1)} collective-permute-done((bf16[256,2048]{1,0:T(8,128)(2,1)S(1)}, bf16[256,2048]{1,0:T(8,128)(2,1)S(1)}, u32[]{:S(2)}, u32[]{:S(2)}) %collective-permute-start.4) | collective-permute-done | bytes 1048608 | tf_op jit(solution)/shard_map/ppermute | solution.py:21
  151.7 1.9 broadcast_select_fusion
  153.5 19.8 %collective-permute-done.2 = bf16[256,2048]{1,0:T(8,128)(2,1)S(1)} collective-permute-done((bf16[256,2048]{1,0:T(8,128)(2,1)S(1)}, bf16[256,2048]{1,0:T(8,128)(2,1)S(1)}, u32[]{:S(2)}, u32[]{:S(2)}) %collective-permute-start.2) | collective-permute-done | bytes 1048608 | tf_op jit(solution)/shard_map/ppermute | solution.py:21
  173.3 1.5 broadcast_select_fusion.1
  175.6 1.6 copy.185
  177.2 2.3 all_to_all.28
  179.5 4.4 %all-to-all-start = ((bf16[4,64,2048]{2,1,0:T(8,128)(2,1)}), bf16[4,64,2048]{2,1,0:T(8,128)(2,1)}, u32[]{:S(2)}, u32[]{:S(2)}) async-start(bf16[4,64,2048]{2,1,0:T(8,128)(2,1)} %all_to_all.28), calls=%async_computation | async-start | bytes 2097152 | tf_op jit(solution)/shard_map/all_to_all | solution.py:234
  184.0 2.3 constant_dynamic-update-slice_fusion.4
  186.3 2.3 constant_dynamic-update-slice_fusion.3
  188.6 3.6 %slice_bitcast_fusion.2 = (bf16[80,8,16,128]{3,1,2,0:T(8,128)(2,1)S(1)}, bf16[80,8,16,128]{3,1,2,0:T(8,128)(2,1)S(1)}) fusion(bf16[768,2048]{1,0:T(8,128)(2,1)} %constant_dynamic-update-slice_fusion.3), kind=kLoop, calls=%fused_computation.12 | loop fusion | bytes 10485760
  200.8 2.8 %fusion.34 = bf16[128,16,128]{2,0,1:T(8,128)(2,1)S(1)} fusion(f32[16,5,128,128]{3,2,1,0:T(8,128)S(1)} %get-tuple-element.70, f32[16,128]{1,0:T(8,128)S(1)} %fusion.1, f32[16,128]{1,0:T(8,128)S(1)} %get-tuple-element.69, pred[128,5,128]{0,2,1:T(8,128)(4,1)S(1)} %get-tuple-element.47, bf16[5,128,16,128]{3,2,1,0:T(8,128)(2,1)S(1)} %bitcast.271), kind=kOutput, calls=%fused_computation.47 | convolution fusion | flops 342360064 | bytes 8486912 | tf_op jit(solution)/shard_map/htkj,kjhd->thd/dot_general | solution.py:169
  206.0 3.0 %fusion.31 = bf16[128,16,128]{2,0,1:T(8,128)(2,1)S(1)} fusion(f32[16,5,128,128]{3,2,1,0:T(8,128)S(1)} %get-tuple-element.72, f32[16,128]{1,0:T(8,128)S(1)} %fusion, f32[16,128]{1,0:T(8,128)S(1)} %get-tuple-element.71, pred[128,5,128]{0,2,1:T(8,128)(4,1)S(1)} %get-tuple-element.46, bf16[5,128,16,128]{3,2,1,0:T(8,128)(2,1)S(1)} %bitcast.269), kind=kOutput, calls=%fused_computation.46 | convolution fusion | flops 342360064 | bytes 8486912 | tf_op jit(solution)/shard_map/htkj,kjhd->thd/dot_general | solution.py:169
  211.1 4.6 %all-to-all-start.1 = ((bf16[4,64,2048]{2,1,0:T(8,128)(2,1)}), bf16[4,64,2048]{2,1,0:T(8,128)(2,1)S(1)}, u32[]{:S(2)}, u32[]{:S(2)}) async-start(bf16[4,64,2048]{2,1,0:T(8,128)(2,1)} %all_to_all.32), calls=%async_computation.1 | async-start | bytes 2097152 | tf_op jit(solution)/shard_map/all_to_all | solution.py:235
  215.7 2.3 copy.233
  218.0 13.2 %all-to-all-done.1 = bf16[4,64,2048]{2,1,0:T(8,128)(2,1)S(1)} async-done(((bf16[4,64,2048]{2,1,0:T(8,128)(2,1)}), bf16[4,64,2048]{2,1,0:T(8,128)(2,1)S(1)}, u32[]{:S(2)}, u32[]{:S(2)}) %all-to-all-start.1) | async-done | bytes 1048608 | tf_op jit(solution)/shard_map/all_to_all | solution.py:235
  (119 shorter events, 33.1 us)
Async XLA Ops:
  7.2 0.7 copy-start
  7.2 75.7 %all-gather.5.cloned.1.call-start = ((), (), s32[]{:S(2)}) async-start(), calls=%async_computation.2 | async-start | bytes 5013504 | tf_op jit(solution)/shard_map/all_gather | solution.py:93
  11.4 2.9 %copy-start.10 = (bf16[128,2048]{0,1:T(8,128)(2,1)}, bf16[128,2048]{0,1:T(8,128)(2,1)S(1)}, u32[]{:S(2)}) copy-start(bf16[128,2048]{0,1:T(8,128)(2,1)S(1)} %copy.227) | copy-start | bytes 1572868
  11.7 2.5 %copy-start.5 = (bf16[128,2048]{0,1:T(8,128)(2,1)}, bf16[128,2048]{0,1:T(8,128)(2,1)S(1)}, u32[]{:S(2)}) copy-start(bf16[128,2048]{0,1:T(8,128)(2,1)S(1)} %copy.224) | copy-start | bytes 1572868
  13.4 0.8 copy-start.7
  13.7 2.2 copy-start.11
  15.9 3.1 %collective-permute-start = (f32[16,136,128]{2,1,0:T(8,128)}, f32[16,136,128]{2,1,0:T(8,128)}, u32[]{:S(2)}, u32[]{:S(2)}) collective-permute-start(f32[16,136,128]{2,1,0:T(8,128)} %pad_maximum_fusion), channel_id=1, source_target_pairs={{0,4},{4,0},{1,5},{5,1},{2,6},{6,2},{3,7},{7,3},{8,12},{12,8},{9,1... | collective-permute-start | bytes 3342344 | tf_op jit(solution)/shard_map/ppermute | solution.py:71
  22.6 98.0 %all-gather.7.cloned.1.call-start = ((), (), s32[]{:S(2)}) async-start(), calls=%async_computation.3 | async-start | bytes 2785280 | tf_op jit(solution)/shard_map/all_gather | solution.py:105
  84.0 4.3 %copy-start.13 = (bf16[256,2048]{1,0:T(8,128)(2,1)S(1)}, bf16[256,2048]{1,0:T(8,128)(2,1)}, u32[]{:S(2)}) copy-start(bf16[256,2048]{1,0:T(8,128)(2,1)} %param.10) | copy-start | bytes 3145732
  89.3 10.8 %copy-start.19 = (s32[2]{0:T(128)S(1)}, s32[2]{0:T(128)}, u32[]{:S(2)}) copy-start(s32[2]{0:T(128)} %param.19) | copy-start | bytes 28
  89.3 12.7 %copy-start.20 = (s32[2,5]{1,0:T(2,128)S(1)}, s32[2,5]{1,0:T(2,128)}, u32[]{:S(2)}) copy-start(s32[2,5]{1,0:T(2,128)} %param.18) | copy-start | bytes 124
  89.3 13.1 %copy-start.6 = (bf16[128,2048]{0,1:T(8,128)(2,1)S(1)}, bf16[128,2048]{0,1:T(8,128)(2,1)}, u32[]{:S(2)}) copy-start(bf16[128,2048]{0,1:T(8,128)(2,1)} %copy-done.5) | copy-start | bytes 1572868
  89.3 13.1 %copy-start.8 = (bf16[128,2048]{0,1:T(8,128)(2,1)S(1)}, bf16[128,2048]{0,1:T(8,128)(2,1)}, u32[]{:S(2)}) copy-start(bf16[128,2048]{0,1:T(8,128)(2,1)} %copy-done.7) | copy-start | bytes 1572868
  105.3 16.3 %copy-start.2 = (bf16[256,2048]{1,0:T(8,128)(2,1)S(1)}, bf16[256,2048]{1,0:T(8,128)(2,1)}, u32[]{:S(2)}) copy-start(bf16[256,2048]{1,0:T(8,128)(2,1)} %param.16) | copy-start | bytes 3145732
  121.6 30.1 %collective-permute-start.4 = (bf16[256,2048]{1,0:T(8,128)(2,1)S(1)}, bf16[256,2048]{1,0:T(8,128)(2,1)S(1)}, u32[]{:S(2)}, u32[]{:S(2)}) collective-permute-start(bf16[256,2048]{1,0:T(8,128)(2,1)S(1)} %copy-done.2), channel_id=1, source_target_pairs={{0,8},{4,12},{8,16},{12,20},{16,24},{20,28},{24,32},{28,36},{32,40... | collective-permute-start | bytes 3145736 | tf_op jit(solution)/shard_map/ppermute | solution.py:21
  125.0 4.1 %copy-start.9 = (bf16[128,2048]{0,1:T(8,128)(2,1)S(1)}, bf16[128,2048]{0,1:T(8,128)(2,1)}, u32[]{:S(2)}) copy-start(bf16[128,2048]{0,1:T(8,128)(2,1)} %copy.225) | copy-start | bytes 1572868
  125.0 4.1 %copy-start.12 = (f32[128,16,128]{2,0,1:T(8,128)S(1)}, f32[128,16,128]{2,0,1:T(8,128)}, u32[]{:S(2)}) copy-start(f32[128,16,128]{2,0,1:T(8,128)} %convolution_bitcast_fusion.1) | copy-start | bytes 3145732
  128.9 1.2 copy-start.3
  128.9 4.7 %copy-start.14 = (bf16[256,2048]{1,0:T(8,128)(2,1)S(1)}, bf16[256,2048]{1,0:T(8,128)(2,1)}, u32[]{:S(2)}) copy-start(bf16[256,2048]{1,0:T(8,128)(2,1)} %param.10) | copy-start | bytes 3145732
  128.9 4.7 %copy-start.15 = (f32[128,16,128]{2,0,1:T(8,128)S(1)}, f32[128,16,128]{2,0,1:T(8,128)}, u32[]{:S(2)}) copy-start(f32[128,16,128]{2,0,1:T(8,128)} %fusion.22) | copy-start | bytes 3145732
  128.9 4.7 %collective-permute-start.1 = (f32[8,128,128]{2,1,0:T(8,128)S(1)}, f32[8,128,128]{2,1,0:T(8,128)S(1)}, u32[]{:S(2)}, u32[]{:S(2)}) collective-permute-start(f32[8,128,128]{2,1,0:T(8,128)S(1)} %fusion.58), channel_id=1, source_target_pairs={{0,4},{4,0},{1,5},{5,1},{2,6},{6,2},{3,7},{7,3},{8,12},{12,8},{9,1... | collective-permute-start | bytes 1572872 | tf_op jit(solution)/shard_map/ppermute | solution.py:71
  130.1 43.2 %collective-permute-start.2 = (bf16[256,2048]{1,0:T(8,128)(2,1)S(1)}, bf16[256,2048]{1,0:T(8,128)(2,1)S(1)}, u32[]{:S(2)}, u32[]{:S(2)}) collective-permute-start(bf16[256,2048]{1,0:T(8,128)(2,1)S(1)} %copy-done.3), channel_id=1, source_target_pairs={{0,8},{4,12},{8,16},{12,20},{16,24},{20,28},{24,32},{28,36},{32,40... | collective-permute-start | bytes 3145736 | tf_op jit(solution)/shard_map/ppermute | solution.py:21
  153.5 21.3 %copy-start.18 = (f32[2048]{0:T(1024)S(1)}, f32[2048]{0:T(1024)}, u32[]{:S(2)}) copy-start(f32[2048]{0:T(1024)} %param.14) | copy-start | bytes 24580
  153.5 30.4 %collective-permute-start.5 = (bf16[256,2048]{1,0:T(8,128)(2,1)}, bf16[256,2048]{1,0:T(8,128)(2,1)}, u32[]{:S(2)}, u32[]{:S(2)}) collective-permute-start(bf16[256,2048]{1,0:T(8,128)(2,1)} %get-tuple-element.38), channel_id=1, source_target_pairs={{0,4},{4,0},{1,5},{5,1},{2,6},{6,2},{3,7},{7,3},{8,12},{12,8},{9,1... | collective-permute-start | bytes 3145736 | tf_op jit(solution)/shard_map/ppermute | solution.py:71
  174.8 18.2 %collective-permute-start.3 = (bf16[256,2048]{1,0:T(8,128)(2,1)}, bf16[256,2048]{1,0:T(8,128)(2,1)}, u32[]{:S(2)}, u32[]{:S(2)}) collective-permute-start(bf16[256,2048]{1,0:T(8,128)(2,1)} %get-tuple-element.36), channel_id=1, source_target_pairs={{0,4},{4,0},{1,5},{5,1},{2,6},{6,2},{3,7},{7,3},{8,12},{12,8},{9,1... | collective-permute-start | bytes 3145736 | tf_op jit(solution)/shard_map/ppermute | solution.py:71
  179.5 31.6 %all-to-all-start = ((bf16[4,64,2048]{2,1,0:T(8,128)(2,1)}), bf16[4,64,2048]{2,1,0:T(8,128)(2,1)}, u32[]{:S(2)}, u32[]{:S(2)}) async-start(bf16[4,64,2048]{2,1,0:T(8,128)(2,1)} %all_to_all.28), calls=%async_computation | async-start | bytes 2097152 | tf_op jit(solution)/shard_map/all_to_all | solution.py:234
  192.2 2.1 copy-start.4
  197.3 1.0 copy-start.17
  200.8 2.8 %copy-start.16 = (bf16[128,2048]{0,1:T(8,128)(2,1)S(1)}, bf16[128,2048]{0,1:T(8,128)(2,1)}, u32[]{:S(2)}) copy-start(bf16[128,2048]{0,1:T(8,128)(2,1)} %copy.228) | copy-start | bytes 1572868
  209.8 22.4 %copy-start.1 = (f32[16,256]{1,0:T(8,128)S(1)}, f32[16,256]{1,0:T(8,128)}, u32[]{:S(2)}) copy-start(f32[16,256]{1,0:T(8,128)} %param.13) | copy-start | bytes 49156
  211.1 20.1 %all-to-all-start.1 = ((bf16[4,64,2048]{2,1,0:T(8,128)(2,1)}), bf16[4,64,2048]{2,1,0:T(8,128)(2,1)S(1)}, u32[]{:S(2)}, u32[]{:S(2)}) async-start(bf16[4,64,2048]{2,1,0:T(8,128)(2,1)} %all_to_all.32), calls=%async_computation.1 | async-start | bytes 2097152 | tf_op jit(solution)/shard_map/all_to_all | solution.py:235
Sparse Core Ops, SparseCore 0:
  22.7 60.1 all-gather.4
  88.4 32.1 all-gather.6

commit v6 on v5

--- a/solution.py
+++ b/solution.py
@@ -223,18 +223,16 @@
     block_count,
 ):
     heads = log_decay.shape[0]
-    linear_heads, (soft_key, soft_value) = linear_layer(
-        linear_query, linear_key, linear_value, log_decay, norm_gain, (soft_key, soft_value)
-    )
     sections = lax.psum(1, CTX)
     softmax_heads = softmax_layer(
         soft_query, soft_key, soft_value, block_index, block_count, heads, sections
     )
-    result = (
-        lax.all_to_all(linear_heads, "head", split_axis=0, concat_axis=1, tiled=True),
-        lax.all_to_all(softmax_heads, "head", split_axis=0, concat_axis=1, tiled=True),
-    )
-    return (result[0], result[1])
+    softmax_rows = lax.all_to_all(softmax_heads, "head", split_axis=0, concat_axis=1, tiled=True)
+    linear_heads, softmax_rows = linear_layer(
+        linear_query, linear_key, linear_value, log_decay, norm_gain, softmax_rows
+    )
+    linear_rows = lax.all_to_all(linear_heads, "head", split_axis=0, concat_axis=1, tiled=True)
+    return (linear_rows, softmax_rows)
 
 
 def solution(mesh):

time: 240 us -> 212 us (0.88)
  waiting for transfers between devices: 122 us -> 80 us
  blocking collectives: 0 us -> 19.4 us
  local copies, waits for them, and re-layouts: 43 us -> 36.6 us
  starting transfers between devices: 16.1 us -> 12.5 us
  other arithmetic: 23.1 us -> 25.7 us
    all_gather x1, waiting for transfers between devices: 60.2 us -> 0.02 us  [carry_in(): lax.all_gather(packed(chip_state, chip_factor), 'cz')]
    ppermute x2, waiting for transfers between devices: 36.3 us -> 64.9 us  [passed_along(): return lax.ppermute(block, axis, route)]
    all_to_all x0 -> x1, blocking collectives: none -> 19.4 us  [local(): lax.all_to_all(linear_heads, 'head', split_axis=0, concat_axis=1, tiled=T...]
    all_gather x1, waiting for transfers between devices: 9.38 us -> 2.7 us  [carry_in(): column_packed = lax.all_gather(packed(total, total_factor), 'cy')]
    all_to_all x1, waiting for transfers between devices: 13.2 us -> 8.09 us  [local(): lax.all_to_all(softmax_heads, 'head', split_axis=0, concat_axis=1, tiled=...]
    all_to_all x1 -> x0, starting transfers between devices: 4.44 us -> none  [local(): lax.all_to_all(linear_heads, 'head', split_axis=0, concat_axis=1, tiled=T...]
    all_to_all x2, local copies, waits for them, and re-layouts: 4.6 us -> 1.53 us  [local(): lax.all_to_all(linear_heads, 'head', split_axis=0, concat_axis=1, tiled=T...]
    dot_general x2, matrix products: 2.62 us -> 5.28 us  [attend(): jnp.einsum('thd,kjhd->htkj', query_blk, keys_sel, preferred_element_type=...]
  transfers between devices with their start and end apart: 10 -> 9, of which waited for: 6 -> 6; matrix products, arithmetic and copies ran while one was open for 26% -> 26% of each run, Pallas kernels for 0% -> 0%
where the time goes in v6:
time: 212 us; the launch traced here: 211 us
  waiting for transfers between devices  80 us (38%)
  local copies, waits for them, and re-layouts  36.6 us (17%)
  other arithmetic  25.7 us (12%)
  matrix products  21.6 us (10%)
  blocking collectives  19.4 us (9%)
  between operations  14.8 us (7%)
  starting transfers between devices  12.5 us (6%)
    ppermute x2, waiting for transfers between devices, passed_along(): return lax.ppermute(block, axis, route)  64.9 us
    unnamed x72, local copies, waits for them, and re-layouts  21.3 us
    all_to_all x1, blocking collectives, local(): lax.all_to_all(linear_heads, 'head', split_axis=0, concat_axis=1, tiled=T...  19.4 us
    all_to_all x1, waiting for transfers between devices, local(): lax.all_to_all(softmax_heads, 'head', split_axis=0, concat_axis=1, tiled=...  8.09 us
    ppermute x2, starting transfers between devices, passed_along(): return lax.ppermute(block, axis, route)  7.66 us
    dot_general x2, matrix products, attend(): jnp.einsum('htkj,kjhd->thd', weights, values_sel, preferred_element_type=...  5.81 us
    dot_general x2, matrix products, attend(): jnp.einsum('thd,kjhd->htkj', query_blk, keys_sel, preferred_element_type=...  5.28 us
    select_n x2, other arithmetic, softmax_layer(): jnp.where(on_first, own, far)  5.16 us
  transfers between devices with their start and end apart: 9, of which 6 were waited for; matrix products, arithmetic and copies ran while one was open for 26% of the time, Pallas kernels for 0%

profile of v6, /device:TPU:8, one launch (start us, length us, event | category | flops | bytes accessed | tf_op | source)
XLA Modules:
  0.0 210.7 jit_solution(7265395724447497407)
XLA Ops:
  10.3 1.5 fusion.94
  16.0 2.9 %collective-permute-done = f32[16,136,128]{2,1,0:T(8,128)} collective-permute-done((f32[16,136,128]{2,1,0:T(8,128)S(1)}, f32[16,136,128]{2,1,0:T(8,128)}, u32[]{:S(2)}, u32[]{:S(2)}) %collective-permute-start) | collective-permute-done | bytes 1114144 | tf_op jit(solution)/shard_map/ppermute | solution.py:71
  20.0 1.5 fusion.90
  23.5 3.8 %collective-permute-start.3 = (bf16[256,2048]{1,0:T(8,128)(2,1)S(1)}, bf16[256,2048]{1,0:T(8,128)(2,1)}, u32[]{:S(2)}, u32[]{:S(2)}) collective-permute-start(bf16[256,2048]{1,0:T(8,128)(2,1)S(1)} %copy-done.6), channel_id=1, source_target_pairs={{0,8},{4,12},{8,16},{12,20},{16,24},{20,28},{24,32},{28,36},{32,40... | collective-permute-start | bytes 3145736 | tf_op jit(solution)/shard_map/ppermute | solution.py:21
  27.3 3.8 %collective-permute-start.1 = (bf16[256,2048]{1,0:T(8,128)(2,1)}, bf16[256,2048]{1,0:T(8,128)(2,1)}, u32[]{:S(2)}, u32[]{:S(2)}) collective-permute-start(bf16[256,2048]{1,0:T(8,128)(2,1)} %param.17), channel_id=1, source_target_pairs={{0,8},{4,12},{8,16},{12,20},{16,24},{20,28},{24,32},{28,36},{32,40... | collective-permute-start | bytes 3145736 | tf_op jit(solution)/shard_map/ppermute | solution.py:21
  33.6 2.3 %fusion.92 = (bf16[128,2048]{1,0:T(8,128)(2,1)}, bf16[128,2048]{1,0:T(8,128)(2,1)}) fusion(bf16[256,2048]{1,0:T(8,128)(2,1)} %param.10), kind=kLoop, calls=%fused_computation.188 | loop fusion | bytes 2097152 | tf_op jit(solution)/shard_map/slice | solution.py:143
  36.8 32.0 %collective-permute-done.3 = bf16[256,2048]{1,0:T(8,128)(2,1)} collective-permute-done((bf16[256,2048]{1,0:T(8,128)(2,1)S(1)}, bf16[256,2048]{1,0:T(8,128)(2,1)}, u32[]{:S(2)}, u32[]{:S(2)}) %collective-permute-start.3) | collective-permute-done | bytes 1048608 | tf_op jit(solution)/shard_map/ppermute | solution.py:21
  68.8 3.0 %broadcast_select_fusion = (bf16[256,2048]{1,0:T(8,128)(2,1)}, bf16[768,2048]{1,0:T(8,128)(2,1)S(1)}) fusion(bf16[256,2048]{1,0:T(8,128)(2,1)} %param.16, bf16[256,2048]{1,0:T(8,128)(2,1)} %collective-permute-done.3, pred[]{:T(512)S(6)} %eq.56), kind=kLoop, calls=%fused_computation.65 | loop fusion | flops 524287 | bytes 4194305 | tf_op jit(solution)/shard_map/jit(_where)/select_n | solution.py:180
  72.0 2.1 copy.228
  74.1 2.0 copy.229
  76.1 2.0 copy.225
  78.2 2.1 copy.222
  80.4 32.9 %collective-permute-done.1 = bf16[256,2048]{1,0:T(8,128)(2,1)} collective-permute-done((bf16[256,2048]{1,0:T(8,128)(2,1)}, bf16[256,2048]{1,0:T(8,128)(2,1)}, u32[]{:S(2)}, u32[]{:S(2)}) %collective-permute-start.1) | collective-permute-done | bytes 1048608 | tf_op jit(solution)/shard_map/ppermute | solution.py:21
  113.3 2.1 %broadcast_select_fusion.1 = (bf16[256,2048]{1,0:T(8,128)(2,1)S(1)}, bf16[768,2048]{1,0:T(8,128)(2,1)S(1)}) fusion(bf16[256,2048]{1,0:T(8,128)(2,1)} %param.17, bf16[256,2048]{1,0:T(8,128)(2,1)} %collective-permute-done.1, pred[]{:T(512)S(6)} %eq.56), kind=kLoop, calls=%fused_computation.66 | loop fusion | flops 524287 | bytes 4194305 | tf_op jit(solution)/shard_map/jit(_where)/select_n | solution.py:180
  119.3 1.3 constant_dynamic-update-slice_fusion
  120.6 1.8 slice_bitcast_fusion.3
  124.1 2.3 %copy.237 = bf16[80,8,16,128]{3,2,1,0:T(8,128)(2,1)} copy(bf16[80,8,16,128]{3,1,2,0:T(8,128)(2,1)S(1)} %get-tuple-element.27) | data formatting | bytes 5242880
  127.7 4.0 %fusion.3 = (f32[16,128]{1,0:T(8,128)S(1)}, f32[16,5,128,128]{3,2,1,0:T(8,128)}) fusion(pred[128,5,128]{0,2,1:T(8,128)(4,1)S(1)} %get-tuple-element.45, bf16[128,16,128,1]{0,2,3,1:T(8,128)(2,1)S(1)} %bitcast.291, bf16[5,128,16,128]{3,2,1,0:T(8,128)(2,1)S(1)} %bitcast.274), kind=kOutput, calls=%fused_computation.9 | convolution fusion | flops 339474432 | bytes 8478720 | tf_op jit(solution)/shard_map/thd,kjhd->htkj/dot_general | solution.py:162
  133.9 2.6 %fusion.47 = (f32[8,128,128]{2,1,0:T(8,128)S(1)}, f32[8,128,128]{2,1,0:T(8,128)S(1)}) fusion(f32[8,8,136,128]{3,2,1,0:T(8,128)} %bitcast.265, f32[8]{0:T(128)S(1)} %get-tuple-element.8, f32[8]{0:T(128)S(1)} %get-tuple-element.7, f32[8]{0:T(128)S(1)} %get-tuple-element.6, f32[8]{0:T(128)S(1)} %get-tuple-element.9, f32[8]{0:T(128)S(1)} %get-tuple-element.62, ...), kind=kLoop, calls=%fused_computation.70 | loop fusion | flops 1966080 | bytes 5243136 | tf_op jit(solution)/shard_map/add | solution.py:103
  137.4 3.7 %fusion.1 = f32[16,128]{1,0:T(8,128)S(1)} fusion(f32[16,5,128,128]{3,2,1,0:T(8,128)} %get-tuple-element.66, f32[16,128]{1,0:T(8,128)S(1)} %get-tuple-element.65, pred[128,5,128]{0,2,1:T(8,128)(4,1)S(1)} %get-tuple-element.45), kind=kLoop, calls=%fused_computation.7 | loop fusion | flops 5240832 | bytes 5341184 | tf_op jit(solution)/shard_map/reduce_sum | solution.py:168
  141.4 2.8 %fusion.31 = bf16[128,16,128]{2,0,1:T(8,128)(2,1)S(1)} fusion(f32[16,5,128,128]{3,2,1,0:T(8,128)S(1)} %copy-done.5, f32[16,128]{1,0:T(8,128)S(1)} %fusion, f32[16,128]{1,0:T(8,128)S(1)} %get-tuple-element.67, pred[128,5,128]{0,2,1:T(8,128)(4,1)S(1)} %get-tuple-element.44, bf16[5,128,16,128]{3,2,1,0:T(8,128)(2,1)S(1)} %bitcast.271), kind=kOutput, calls=%fused_computation.46 | convolution fusion | flops 342360064 | bytes 8486912 | tf_op jit(solution)/shard_map/htkj,kjhd->thd/dot_general | solution.py:169
  144.2 3.0 %fusion.34 = bf16[128,16,128]{2,0,1:T(8,128)(2,1)S(1)} fusion(f32[16,5,128,128]{3,2,1,0:T(8,128)S(1)} %bitcast.268, f32[16,128]{1,0:T(8,128)S(1)} %fusion.1, f32[16,128]{1,0:T(8,128)S(1)} %get-tuple-element.65, pred[128,5,128]{0,2,1:T(8,128)(4,1)S(1)} %get-tuple-element.45, bf16[5,128,16,128]{3,2,1,0:T(8,128)(2,1)S(1)} %bitcast.272), kind=kOutput, calls=%fused_computation.47 | convolution fusion | flops 342360064 | bytes 8486912 | tf_op jit(solution)/shard_map/htkj,kjhd->thd/dot_general | solution.py:169
  149.4 4.3 %all-to-all-start = ((bf16[4,64,2048]{2,1,0:T(8,128)(2,1)}), bf16[4,64,2048]{2,1,0:T(8,128)(2,1)S(1)}, u32[]{:S(2)}, u32[]{:S(2)}) async-start(bf16[4,64,2048]{2,1,0:T(8,128)(2,1)} %all_to_all.28), calls=%async_computation | async-start | bytes 2097152 | tf_op jit(solution)/shard_map/all_to_all | solution.py:230
  153.7 2.9 %convolution_bitcast_fusion.3 = f32[128,16,128]{2,0,1:T(8,128)} fusion(bf16[128,16,128]{0,2,1:T(8,128)(2,1)S(1)} %bitcast.278, bf16[128,16,128]{0,2,1:T(8,128)(2,1)} %bitcast.281, bf16[128,16,128]{0,2,1:T(8,128)(2,1)S(1)} %bitcast.276, f32[16,128]{1,0:T(8,128)S(1)} %get-tuple-element.54, pred[128,128]{1,0:T(8,128)(4,1)S(1)} %iota_compare_fusion), kind=kOutput, calls=%fused_computation.40 | convolution fusion | flops 135528448 | bytes 2646016 | tf_op jit(solution)/shard_map/htj,jhd->thd/dot_general | solution.py:48
  156.6 2.7 %fusion.22 = f32[128,16,128]{2,0,1:T(8,128)} fusion(f32[128,16,128]{2,0,1:T(8,128)} %convolution_bitcast_fusion.3, bf16[128,16,128]{0,2,1:T(8,128)(2,1)} %bitcast.282, f32[128,16]{0,1:T(8,128)S(1)} %get-tuple-element.51), kind=kOutput, calls=%fused_computation.39 | convolution fusion | flops 68157440 | bytes 2629632 | tf_op jit(solution)/shard_map/thd,hde->the/dot_general | solution.py:52
  159.3 2.0 convolution_bitcast_fusion.1
  161.3 8.1 %all-to-all-done = bf16[4,64,2048]{2,1,0:T(8,128)(2,1)S(1)} async-done(((bf16[4,64,2048]{2,1,0:T(8,128)(2,1)}), bf16[4,64,2048]{2,1,0:T(8,128)(2,1)S(1)}, u32[]{:S(2)}, u32[]{:S(2)}) %all-to-all-start) | async-done | bytes 1048608 | tf_op jit(solution)/shard_map/all_to_all | solution.py:230
  170.5 2.7 %all-gather.7.cloned.1.call-done = f32[32,136,128]{2,1,0:T(8,128)} async-done(((f32[8,136,128]{2,1,0:T(8,128)}), f32[32,136,128]{2,1,0:T(8,128)}) %all-gather.7.cloned.1.call-update) | async-done | bytes 2228240 | tf_op jit(solution)/shard_map/all_gather | solution.py:105
  174.1 3.6 %fusion.58 = f32[8,128,128]{2,1,0:T(8,128)S(1)} fusion(f32[8,128,128]{2,1,0:T(8,128)S(1)} %get-tuple-element.23, f32[4,8,136,128]{3,2,1,0:T(8,128)} %bitcast.288, f32[8,8,136,128]{3,2,1,0:T(8,128)} %bitcast.266, f32[8]{0:T(128)S(1)} %get-tuple-element.15, f32[8]{0:T(128)S(1)} %get-tuple-element.16, f32[8]{0:T(128)S(1)} %get-tuple-element.17, ...), kind=kLoop, calls=%fused_computation.90 | loop fusion | flops 4063232 | bytes 6291819 | tf_op jit(solution)/shard_map/add | solution.py:112
  178.4 1.4 collective-permute-done.5
  179.8 1.5 multiply_reduce_fusion
  183.3 19.4 %all_to_all.38 = bf16[4,64,2048]{2,1,0:T(8,128)(2,1)S(1)} all-to-all(bf16[4,64,2048]{2,1,0:T(8,128)(2,1)S(1)} %all_to_all.32), channel_id=1, replica_groups=mesh['cy'=4,'cz'=8,'cc'=2,'head'=4] {'head'}, dimensions={0} | all-to-all | bytes 2097152 | tf_op jit(solution)/shard_map/all_to_all | solution.py:234
  (133 shorter events, 31.5 us)
Async XLA Ops:
  7.2 125.6 %all-gather.5.cloned.1.call-start = ((), (), s32[]{:S(2)}) async-start(), calls=%async_computation.2 | async-start | bytes 5013504 | tf_op jit(solution)/shard_map/all_gather | solution.py:93
  10.3 3.9 %copy-start.11 = (bf16[128,2048]{0,1:T(8,128)(2,1)}, bf16[128,2048]{0,1:T(8,128)(2,1)S(1)}, u32[]{:S(2)}) copy-start(bf16[128,2048]{0,1:T(8,128)(2,1)S(1)} %copy.223) | copy-start | bytes 1572868
  12.1 2.2 %copy-start.13 = (bf16[128,2048]{0,1:T(8,128)(2,1)}, bf16[128,2048]{0,1:T(8,128)(2,1)S(1)}, u32[]{:S(2)}) copy-start(bf16[128,2048]{0,1:T(8,128)(2,1)S(1)} %copy.224) | copy-start | bytes 1572868
  12.3 3.3 %copy-start.16 = (bf16[128,2048]{0,1:T(8,128)(2,1)}, bf16[128,2048]{0,1:T(8,128)(2,1)S(1)}, u32[]{:S(2)}) copy-start(bf16[128,2048]{0,1:T(8,128)(2,1)S(1)} %copy.227) | copy-start | bytes 1572868
  12.6 3.2 %copy-start.17 = (bf16[128,2048]{0,1:T(8,128)(2,1)}, bf16[128,2048]{0,1:T(8,128)(2,1)S(1)}, u32[]{:S(2)}) copy-start(bf16[128,2048]{0,1:T(8,128)(2,1)S(1)} %copy.226) | copy-start | bytes 1572868
  15.8 3.0 %collective-permute-start = (f32[16,136,128]{2,1,0:T(8,128)S(1)}, f32[16,136,128]{2,1,0:T(8,128)}, u32[]{:S(2)}, u32[]{:S(2)}) collective-permute-start(f32[16,136,128]{2,1,0:T(8,128)S(1)} %pad_maximum_fusion), channel_id=1, source_target_pairs={{0,4},{4,0},{1,5},{5,1},{2,6},{6,2},{3,7},{7,3},{8,12},{12,8},{9,1... | collective-permute-start | bytes 3342344 | tf_op jit(solution)/shard_map/ppermute | solution.py:71
  19.9 3.5 %copy-start.6 = (bf16[256,2048]{1,0:T(8,128)(2,1)S(1)}, bf16[256,2048]{1,0:T(8,128)(2,1)}, u32[]{:S(2)}) copy-start(bf16[256,2048]{1,0:T(8,128)(2,1)} %param.16) | copy-start | bytes 3145732
  20.0 11.3 %copy-start.24 = (s32[2]{0:T(128)S(1)}, s32[2]{0:T(128)}, u32[]{:S(2)}) copy-start(s32[2]{0:T(128)} %param.19) | copy-start | bytes 28
  20.0 11.9 %copy-start.18 = (bf16[256,2048]{1,0:T(8,128)(2,1)S(1)}, bf16[256,2048]{1,0:T(8,128)(2,1)}, u32[]{:S(2)}) copy-start(bf16[256,2048]{1,0:T(8,128)(2,1)} %param.15) | copy-start | bytes 3145732
  21.5 12.1 %copy-start.25 = (s32[2,5]{1,0:T(2,128)S(1)}, s32[2,5]{1,0:T(2,128)}, u32[]{:S(2)}) copy-start(s32[2,5]{1,0:T(2,128)} %param.18) | copy-start | bytes 124
  23.4 149.7 %all-gather.7.cloned.1.call-start = ((), (), s32[]{:S(2)}) async-start(), calls=%async_computation.3 | async-start | bytes 2785280 | tf_op jit(solution)/shard_map/all_gather | solution.py:105
  23.5 45.3 %collective-permute-start.3 = (bf16[256,2048]{1,0:T(8,128)(2,1)S(1)}, bf16[256,2048]{1,0:T(8,128)(2,1)}, u32[]{:S(2)}, u32[]{:S(2)}) collective-permute-start(bf16[256,2048]{1,0:T(8,128)(2,1)S(1)} %copy-done.6), channel_id=1, source_target_pairs={{0,8},{4,12},{8,16},{12,20},{16,24},{20,28},{24,32},{28,36},{32,40... | collective-permute-start | bytes 3145736 | tf_op jit(solution)/shard_map/ppermute | solution.py:21
  27.3 86.0 %collective-permute-start.1 = (bf16[256,2048]{1,0:T(8,128)(2,1)}, bf16[256,2048]{1,0:T(8,128)(2,1)}, u32[]{:S(2)}, u32[]{:S(2)}) collective-permute-start(bf16[256,2048]{1,0:T(8,128)(2,1)} %param.17), channel_id=1, source_target_pairs={{0,8},{4,12},{8,16},{12,20},{16,24},{20,28},{24,32},{28,36},{32,40... | collective-permute-start | bytes 3145736 | tf_op jit(solution)/shard_map/ppermute | solution.py:21
  71.9 43.9 %collective-permute-start.4 = (bf16[256,2048]{1,0:T(8,128)(2,1)}, bf16[256,2048]{1,0:T(8,128)(2,1)}, u32[]{:S(2)}, u32[]{:S(2)}) collective-permute-start(bf16[256,2048]{1,0:T(8,128)(2,1)} %get-tuple-element.36), channel_id=1, source_target_pairs={{0,4},{4,0},{1,5},{5,1},{2,6},{6,2},{3,7},{7,3},{8,12},{12,8},{9,1... | collective-permute-start | bytes 3145736 | tf_op jit(solution)/shard_map/ppermute | solution.py:71
  80.4 36.6 %copy-start.7 = (bf16[256,2048]{1,0:T(8,128)(2,1)S(1)}, bf16[256,2048]{1,0:T(8,128)(2,1)}, u32[]{:S(2)}) copy-start(bf16[256,2048]{1,0:T(8,128)(2,1)} %param.16) | copy-start | bytes 3145732
  115.4 3.7 %collective-permute-start.2 = (bf16[256,2048]{1,0:T(8,128)(2,1)S(1)}, bf16[256,2048]{1,0:T(8,128)(2,1)S(1)}, u32[]{:S(2)}, u32[]{:S(2)}) collective-permute-start(bf16[256,2048]{1,0:T(8,128)(2,1)S(1)} %get-tuple-element.34), channel_id=1, source_target_pairs={{0,4},{4,0},{1,5},{5,1},{2,6},{6,2},{3,7},{7,3},{8,12},{12,8},{9,1... | collective-permute-start | bytes 3145736 | tf_op jit(solution)/shard_map/ppermute | solution.py:71
  124.1 2.3 %copy-start.22 = (bf16[128,2048]{0,1:T(8,128)(2,1)S(1)}, bf16[128,2048]{0,1:T(8,128)(2,1)}, u32[]{:S(2)}) copy-start(bf16[128,2048]{0,1:T(8,128)(2,1)} %copy.228) | copy-start | bytes 1572868
  127.7 4.0 %copy-start.4 = (f32[16,5,128,128]{3,2,1,0:T(8,128)}, f32[16,5,128,128]{3,2,1,0:T(8,128)S(1)}, u32[]{:S(2)}) copy-start(f32[16,5,128,128]{3,2,1,0:T(8,128)S(1)} %get-tuple-element.68) | copy-start | bytes 15728644
  137.4 4.0 %copy-start.5 = (f32[16,5,128,128]{3,2,1,0:T(8,128)S(1)}, f32[16,5,128,128]{3,2,1,0:T(8,128)}, u32[]{:S(2)}) copy-start(f32[16,5,128,128]{3,2,1,0:T(8,128)} %copy-done.4) | copy-start | bytes 15728644
  137.4 6.8 %slice-start = ((s8[5242880]{0:T(1024)(128)(4,1)}), s8[4194304]{0:T(1024)(128)(4,1)S(1)}, s32[]{:S(2)}) async-start(s8[5242880]{0:T(1024)(128)(4,1)} %bitcast.267), calls=%async_computation.4 | async-start | bytes 8388608
  141.4 2.8 %slice-start.1 = ((s8[5242880]{0:T(1024)(128)(4,1)}), s8[1048576]{0:T(1024)(128)(4,1)S(1)}, s32[]{:S(2)}) async-start(s8[5242880]{0:T(1024)(128)(4,1)} %bitcast.267), calls=%async_computation.5 | async-start | bytes 2097152
  141.4 2.8 %copy-start.8 = (bf16[80,8,16,128]{3,2,1,0:T(8,128)(2,1)S(1)}, bf16[80,8,16,128]{3,2,1,0:T(8,128)(2,1)}, u32[]{:S(2)}) copy-start(bf16[80,8,16,128]{3,2,1,0:T(8,128)(2,1)} %copy.237) | copy-start | bytes 7864324
  147.3 6.3 %copy-start.12 = (bf16[128,2048]{0,1:T(8,128)(2,1)S(1)}, bf16[128,2048]{0,1:T(8,128)(2,1)}, u32[]{:S(2)}) copy-start(bf16[128,2048]{0,1:T(8,128)(2,1)} %copy-done.11) | copy-start | bytes 1572868
  147.4 6.3 %copy-start.14 = (bf16[128,2048]{0,1:T(8,128)(2,1)S(1)}, bf16[128,2048]{0,1:T(8,128)(2,1)}, u32[]{:S(2)}) copy-start(bf16[128,2048]{0,1:T(8,128)(2,1)} %copy-done.13) | copy-start | bytes 1572868
  149.4 20.1 %all-to-all-start = ((bf16[4,64,2048]{2,1,0:T(8,128)(2,1)}), bf16[4,64,2048]{2,1,0:T(8,128)(2,1)S(1)}, u32[]{:S(2)}, u32[]{:S(2)}) async-start(bf16[4,64,2048]{2,1,0:T(8,128)(2,1)} %all_to_all.28), calls=%async_computation | async-start | bytes 2097152 | tf_op jit(solution)/shard_map/all_to_all | solution.py:230
  153.7 5.6 %copy-start.15 = (bf16[128,2048]{0,1:T(8,128)(2,1)S(1)}, bf16[128,2048]{0,1:T(8,128)(2,1)}, u32[]{:S(2)}) copy-start(bf16[128,2048]{0,1:T(8,128)(2,1)} %copy.225) | copy-start | bytes 1572868
  174.1 3.9 %copy-start.3 = (f32[16,128,128]{2,1,0:T(8,128)S(1)}, f32[16,128,128]{2,1,0:T(8,128)}, u32[]{:S(2)}) copy-start(f32[16,128,128]{2,1,0:T(8,128)} %copy-done.2) | copy-start | bytes 3145732
  177.8 2.0 copy-start.10
  177.8 2.0 copy-start.19
  177.8 2.0 copy-start.20
  177.8 2.0 collective-permute-start.5
  182.1 21.7 %copy-start.1 = (f32[16,256]{1,0:T(8,128)S(1)}, f32[16,256]{1,0:T(8,128)}, u32[]{:S(2)}) copy-start(f32[16,256]{1,0:T(8,128)} %param.13) | copy-start | bytes 49156
  (5 other events, 5.6 us)
Sparse Core Ops, SparseCore 0:
  23.6 95.9 all-gather.4
  137.5 35.6 all-gather.6

commit v7 on v6

--- a/solution.py
+++ b/solution.py
@@ -71,7 +71,7 @@
     return lax.ppermute(block, "cc", [(0, 1), (1, 0)])
 
 
-def carry_in(final, section_total, held):
+def carry_in(final, section_total, pair, between):
     heads, width, _ = final.shape
     half = heads // 2
     core, row, column = (lax.axis_index("cc"), lax.axis_index("cz"), lax.axis_index("cy"))
@@ -89,9 +89,10 @@
     second_factor = lax.dynamic_slice_in_dim(second_all, low, half, 0)
     chip_state = second_factor[:, None, None] * first + second
     chip_factor = first_factor * second_factor
-    row_states, row_factors = unpacked(
-        lax.all_gather(packed(chip_state, chip_factor), "cz"), width
-    )
+    row_packed = lax.all_gather(packed(chip_state, chip_factor), "cz")
+    row_packed, pair = lax.optimization_barrier((row_packed, pair))
+    held = between(pair)
+    row_states, row_factors = unpacked(row_packed, width)
     total = jnp.zeros_like(chip_state)
     total_factor = jnp.ones_like(chip_factor)
     before = total
@@ -120,7 +121,7 @@
     return jnp.where(on_first, prefix, later), held
 
 
-def linear_layer(linear_query, linear_key, linear_value, log_decay, norm_gain, held):
+def linear_layer(linear_query, linear_key, linear_value, log_decay, norm_gain, pair, between):
     length, columns = linear_query.shape
     heads = log_decay.shape[0]
     width = columns // heads
@@ -138,7 +139,7 @@
     for b in range(blocks_here):
         before.append(carried)
         carried = block_state(carried, keys_blocks[b], values_blocks[b], cumulative[b], totals[b])
-    incoming, held = carry_in(carried, section_total, held)
+    incoming, held = carry_in(carried, section_total, pair, between)
     outputs = [
         block_output(before[b], query_blocks[b], keys_blocks[b], values_blocks[b], cumulative[b])
         for b in range(blocks_here)
@@ -224,12 +225,15 @@
 ):
     heads = log_decay.shape[0]
     sections = lax.psum(1, CTX)
-    softmax_heads = softmax_layer(
-        soft_query, soft_key, soft_value, block_index, block_count, heads, sections
-    )
-    softmax_rows = lax.all_to_all(softmax_heads, "head", split_axis=0, concat_axis=1, tiled=True)
+
+    def between(pair):
+        softmax_heads = softmax_layer(
+            soft_query, pair[0], pair[1], block_index, block_count, heads, sections
+        )
+        return lax.all_to_all(softmax_heads, "head", split_axis=0, concat_axis=1, tiled=True)
+
     linear_heads, softmax_rows = linear_layer(
-        linear_query, linear_key, linear_value, log_decay, norm_gain, softmax_rows
+        linear_query, linear_key, linear_value, log_decay, norm_gain, (soft_key, soft_value), between
     )
     linear_rows = lax.all_to_all(linear_heads, "head", split_axis=0, concat_axis=1, tiled=True)
     return (linear_rows, softmax_rows)

time: 212 us -> 223 us (1.052)
  waiting for transfers between devices: 80 us -> 103 us
  other arithmetic: 25.7 us -> 22.3 us
  matrix products: 21.6 us -> 18.7 us
  starting transfers between devices: 12.5 us -> 9.91 us
    all_gather x1, waiting for transfers between devices: 0.02 us -> 56.6 us  [carry_in(): row_packed = lax.all_gather(packed(chip_state, chip_factor), 'cz')]
    ppermute x2, waiting for transfers between devices: 64.9 us -> 33.5 us  [passed_along(): return lax.ppermute(block, axis, route)]
    all_gather x1, waiting for transfers between devices: 2.7 us -> 0.01 us  [carry_in(): column_packed = lax.all_gather(packed(total, total_factor), 'cy')]
    dot_general x2, matrix products: 5.28 us -> 2.62 us  [attend(): jnp.einsum('thd,kjhd->htkj', query_blk, keys_sel, preferred_element_type=...]
    reduce_sum x2, other arithmetic: 4.77 us -> 2.15 us  [attend(): jnp.sum(raised, axis=(2, 3), keepdims=True)]
    ppermute x2, starting transfers between devices: 7.66 us -> 5.39 us  [passed_along(): return lax.ppermute(block, axis, route)]
    unnamed x72 -> x70, local copies, waits for them, and re-layouts: 21.3 us -> 19.9 us
  transfers between devices with their start and end apart: 9 -> 9, of which waited for: 6 -> 6; matrix products, arithmetic and copies ran while one was open for 26% -> 23% of each run, Pallas kernels for 0% -> 0%
where the time goes in v7:
time: 223 us; the launch traced here: 222 us
  waiting for transfers between devices  103 us (46%)
  local copies, waits for them, and re-layouts  35.4 us (16%)
  other arithmetic  22.3 us (10%)
  matrix products  18.7 us (8%)
  blocking collectives  18.1 us (8%)
  between operations  14.7 us (7%)
  starting transfers between devices  9.91 us (4%)
    all_gather x1, waiting for transfers between devices, carry_in(): row_packed = lax.all_gather(packed(chip_state, chip_factor), 'cz')  56.6 us
    ppermute x2, waiting for transfers between devices, passed_along(): return lax.ppermute(block, axis, route)  33.5 us
    unnamed x70, local copies, waits for them, and re-layouts  19.9 us
    all_to_all x1, blocking collectives, local(): lax.all_to_all(linear_heads, 'head', split_axis=0, concat_axis=1, tiled=T...  18.1 us
    all_to_all x1, waiting for transfers between devices, between(): lax.all_to_all(softmax_heads, 'head', split_axis=0, concat_axis=1, tiled=...  8.33 us
    select_n x2, other arithmetic, softmax_layer(): jnp.where(on_first, own, far)  5.98 us
    dot_general x2, matrix products, attend(): jnp.einsum('htkj,kjhd->thd', weights, values_sel, preferred_element_type=...  5.81 us
    ppermute x2, starting transfers between devices, passed_along(): return lax.ppermute(block, axis, route)  5.39 us
  transfers between devices with their start and end apart: 9, of which 6 were waited for; matrix products, arithmetic and copies ran while one was open for 23% of the time, Pallas kernels for 0%

profile of v7, /device:TPU:8, one launch (start us, length us, event | category | flops | bytes accessed | tf_op | source)
XLA Modules:
  0.0 221.9 jit_solution(7867059488325665759)
XLA Ops:
  10.3 1.5 fusion.85
  16.0 2.9 %collective-permute-done = f32[16,136,128]{2,1,0:T(8,128)} collective-permute-done((f32[16,136,128]{2,1,0:T(8,128)S(1)}, f32[16,136,128]{2,1,0:T(8,128)}, u32[]{:S(2)}, u32[]{:S(2)}) %collective-permute-start) | collective-permute-done | bytes 1114144 | tf_op jit(solution)/shard_map/ppermute | solution.py:71
  20.0 1.5 fusion.81
  25.8 1.3 fusion.83
  27.1 56.6 %all-gather.5.cloned.1.call-done = f32[64,136,128]{2,1,0:T(8,128)} async-done(((f32[8,136,128]{2,1,0:T(8,128)}), f32[64,136,128]{2,1,0:T(8,128)}) %all-gather.5.cloned.1.call-update) | async-done | bytes 4456464 | tf_op jit(solution)/shard_map/all_gather | solution.py:92
  83.7 1.9 collective-permute-start.3
  86.3 2.1 copy.228
  88.4 2.0 copy.229
  92.9 3.5 %collective-permute-start.1 = (bf16[256,2048]{1,0:T(8,128)(2,1)}, bf16[256,2048]{1,0:T(8,128)(2,1)S(1)}, u32[]{:S(2)}, u32[]{:S(2)}) collective-permute-start(bf16[256,2048]{1,0:T(8,128)(2,1)} %param.17), channel_id=1, source_target_pairs={{0,8},{4,12},{8,16},{12,20},{16,24},{20,28},{24,32},{28,36},{32,40... | collective-permute-start | bytes 3145736 | tf_op jit(solution)/shard_map/ppermute | solution.py:21
  97.4 16.4 %collective-permute-done.3 = bf16[256,2048]{1,0:T(8,128)(2,1)} collective-permute-done((bf16[256,2048]{1,0:T(8,128)(2,1)S(1)}, bf16[256,2048]{1,0:T(8,128)(2,1)}, u32[]{:S(2)}, u32[]{:S(2)}) %collective-permute-start.3) | collective-permute-done | bytes 1048608 | tf_op jit(solution)/shard_map/ppermute | solution.py:21
  113.8 3.0 %broadcast_select_fusion = (bf16[256,2048]{1,0:T(8,128)(2,1)}, bf16[768,2048]{1,0:T(8,128)(2,1)S(1)}) fusion(bf16[256,2048]{1,0:T(8,128)(2,1)} %param.16, bf16[256,2048]{1,0:T(8,128)(2,1)} %collective-permute-done.3, pred[]{:T(512)S(6)} %eq.56), kind=kLoop, calls=%fused_computation.65 | loop fusion | flops 524287 | bytes 4194305 | tf_op jit(solution)/shard_map/jit(_where)/select_n | solution.py:181
  117.9 17.1 %collective-permute-done.1 = bf16[256,2048]{1,0:T(8,128)(2,1)S(1)} collective-permute-done((bf16[256,2048]{1,0:T(8,128)(2,1)}, bf16[256,2048]{1,0:T(8,128)(2,1)S(1)}, u32[]{:S(2)}, u32[]{:S(2)}) %collective-permute-start.1) | collective-permute-done | bytes 1048608 | tf_op jit(solution)/shard_map/ppermute | solution.py:21
  135.0 3.0 %broadcast_select_fusion.1 = (bf16[256,2048]{1,0:T(8,128)(2,1)}, bf16[768,2048]{1,0:T(8,128)(2,1)}) fusion(bf16[256,2048]{1,0:T(8,128)(2,1)} %param.17, bf16[256,2048]{1,0:T(8,128)(2,1)S(1)} %collective-permute-done.1, pred[]{:T(512)S(6)} %eq.56), kind=kLoop, calls=%fused_computation.66 | loop fusion | flops 524287 | bytes 4194305 | tf_op jit(solution)/shard_map/jit(_where)/select_n | solution.py:181
  139.0 1.3 constant_dynamic-update-slice_fusion.4
  140.3 1.3 constant_dynamic-update-slice_fusion.3
  144.7 1.3 constant_dynamic-update-slice_fusion.1
  146.1 1.3 constant_dynamic-update-slice_fusion
  147.4 1.8 slice_bitcast_fusion.3
  151.9 1.3 fusion.2
  154.3 1.3 fusion.3
  156.7 2.8 %fusion.31 = bf16[128,16,128]{2,0,1:T(8,128)(2,1)S(1)} fusion(f32[16,5,128,128]{3,2,1,0:T(8,128)S(1)} %get-tuple-element.74, f32[16,128]{1,0:T(8,128)S(1)} %fusion, f32[16,128]{1,0:T(8,128)S(1)} %get-tuple-element.73, pred[128,5,128]{0,2,1:T(8,128)(4,1)S(1)} %get-tuple-element.50, bf16[5,128,16,128]{3,2,1,0:T(8,128)(2,1)S(1)} %bitcast.255), kind=kOutput, calls=%fused_computation.46 | convolution fusion | flops 342360064 | bytes 8486912 | tf_op jit(solution)/shard_map/htkj,kjhd->thd/dot_general | solution.py:170
  159.5 3.0 %fusion.34 = bf16[128,16,128]{2,0,1:T(8,128)(2,1)S(1)} fusion(f32[16,5,128,128]{3,2,1,0:T(8,128)S(1)} %get-tuple-element.72, f32[16,128]{1,0:T(8,128)S(1)} %fusion.1, f32[16,128]{1,0:T(8,128)S(1)} %get-tuple-element.71, pred[128,5,128]{0,2,1:T(8,128)(4,1)S(1)} %get-tuple-element.51, bf16[5,128,16,128]{3,2,1,0:T(8,128)(2,1)S(1)} %bitcast.254), kind=kOutput, calls=%fused_computation.47 | convolution fusion | flops 342360064 | bytes 8486912 | tf_op jit(solution)/shard_map/htkj,kjhd->thd/dot_general | solution.py:170
  163.3 1.3 all_to_all.28
  164.6 4.2 %all-to-all-start = ((bf16[4,64,2048]{2,1,0:T(8,128)(2,1)}), bf16[4,64,2048]{2,1,0:T(8,128)(2,1)S(1)}, u32[]{:S(2)}, u32[]{:S(2)}) async-start(bf16[4,64,2048]{2,1,0:T(8,128)(2,1)} %all_to_all.28), calls=%async_computation | async-start | bytes 2097152 | tf_op jit(solution)/shard_map/all_to_all | solution.py:233
  168.9 1.8 convolution_bitcast_fusion.3
  170.7 2.5 %fusion.22 = f32[128,16,128]{2,0,1:T(8,128)} fusion(f32[128,16,128]{2,0,1:T(8,128)} %convolution_bitcast_fusion.3, bf16[128,16,128]{0,2,1:T(8,128)(2,1)S(1)} %bitcast.264, f32[128,16]{0,1:T(8,128)S(1)} %get-tuple-element.57), kind=kOutput, calls=%fused_computation.39 | convolution fusion | flops 68157440 | bytes 2629632 | tf_op jit(solution)/shard_map/thd,hde->the/dot_general | solution.py:52
  173.2 3.1 %convolution_bitcast_fusion.1 = f32[128,16,128]{2,0,1:T(8,128)} fusion(bf16[128,16,128]{0,2,1:T(8,128)(2,1)} %bitcast.266, bf16[128,16,128]{0,2,1:T(8,128)(2,1)S(1)} %bitcast.261, bf16[128,16,128]{0,2,1:T(8,128)(2,1)} %bitcast.268, f32[16,128]{1,0:T(8,128)S(1)} %get-tuple-element.61, pred[128,128]{1,0:T(8,128)(4,1)S(1)} %iota_compare_fusion), kind=kOutput, calls=%fused_computation.36 | convolution fusion | flops 135528448 | bytes 2646016 | tf_op jit(solution)/shard_map/htj,jhd->thd/dot_general | solution.py:48
  176.3 8.3 %all-to-all-done = bf16[4,64,2048]{2,1,0:T(8,128)(2,1)S(1)} async-done(((bf16[4,64,2048]{2,1,0:T(8,128)(2,1)}), bf16[4,64,2048]{2,1,0:T(8,128)(2,1)S(1)}, u32[]{:S(2)}, u32[]{:S(2)}) %all-to-all-start) | async-done | bytes 1048608 | tf_op jit(solution)/shard_map/all_to_all | solution.py:233
  186.6 3.7 %fusion.50 = f32[8,128,128]{2,1,0:T(8,128)S(1)} fusion(f32[8,128,128]{2,1,0:T(8,128)S(1)} %copy-done.9, f32[4,8,136,128]{3,2,1,0:T(8,128)} %bitcast.270, f32[8,8,136,128]{3,2,1,0:T(8,128)} %bitcast.249, f32[8]{0:T(128)S(1)} %get-tuple-element.21, f32[8]{0:T(128)S(1)} %get-tuple-element.22, f32[8]{0:T(128)S(1)} %get-tuple-element.23, ...), kind=kLoop, calls=%fused_computation.74 | loop fusion | flops 4063232 | bytes 6291819 | tf_op jit(solution)/shard_map/add | solution.py:113
  190.9 1.4 collective-permute-done.5
  192.4 1.5 multiply_reduce_fusion
  195.9 18.1 %all_to_all.38 = bf16[4,64,2048]{2,1,0:T(8,128)(2,1)S(1)} all-to-all(bf16[4,64,2048]{2,1,0:T(8,128)(2,1)S(1)} %all_to_all.32), channel_id=1, replica_groups=mesh['cy'=4,'cz'=8,'cc'=2,'head'=4] {'head'}, dimensions={0} | all-to-all | bytes 2097152 | tf_op jit(solution)/shard_map/all_to_all | solution.py:238
  (130 shorter events, 33.0 us)
Async XLA Ops:
  7.2 76.5 %all-gather.5.cloned.1.call-start = ((), (), s32[]{:S(2)}) async-start(), calls=%async_computation.2 | async-start | bytes 5013504 | tf_op jit(solution)/shard_map/all_gather | solution.py:92
  10.3 3.9 %copy-start.10 = (bf16[128,2048]{0,1:T(8,128)(2,1)}, bf16[128,2048]{0,1:T(8,128)(2,1)S(1)}, u32[]{:S(2)}) copy-start(bf16[128,2048]{0,1:T(8,128)(2,1)S(1)} %copy.223) | copy-start | bytes 1572868
  12.1 2.2 copy-start.12
  12.3 13.5 %copy-start.16 = (bf16[128,2048]{0,1:T(8,128)(2,1)}, bf16[128,2048]{0,1:T(8,128)(2,1)S(1)}, u32[]{:S(2)}) copy-start(bf16[128,2048]{0,1:T(8,128)(2,1)S(1)} %copy.227) | copy-start | bytes 1572868
  12.6 14.5 %copy-start.17 = (bf16[128,2048]{0,1:T(8,128)(2,1)}, bf16[128,2048]{0,1:T(8,128)(2,1)S(1)}, u32[]{:S(2)}) copy-start(bf16[128,2048]{0,1:T(8,128)(2,1)S(1)} %copy.226) | copy-start | bytes 1572868
  15.8 3.0 %collective-permute-start = (f32[16,136,128]{2,1,0:T(8,128)S(1)}, f32[16,136,128]{2,1,0:T(8,128)}, u32[]{:S(2)}, u32[]{:S(2)}) collective-permute-start(f32[16,136,128]{2,1,0:T(8,128)S(1)} %pad_maximum_fusion), channel_id=1, source_target_pairs={{0,4},{4,0},{1,5},{5,1},{2,6},{6,2},{3,7},{7,3},{8,12},{12,8},{9,1... | collective-permute-start | bytes 3342344 | tf_op jit(solution)/shard_map/ppermute | solution.py:71
  20.0 3.5 %copy-start.25 = (s32[2]{0:T(128)S(1)}, s32[2]{0:T(128)}, u32[]{:S(2)}) copy-start(s32[2]{0:T(128)} %param.19) | copy-start | bytes 28
  20.0 4.8 %copy-start.19 = (bf16[256,2048]{1,0:T(8,128)(2,1)S(1)}, bf16[256,2048]{1,0:T(8,128)(2,1)}, u32[]{:S(2)}) copy-start(bf16[256,2048]{1,0:T(8,128)(2,1)} %param.15) | copy-start | bytes 3145732
  22.4 61.3 %copy-start.6 = (bf16[256,2048]{1,0:T(8,128)(2,1)S(1)}, bf16[256,2048]{1,0:T(8,128)(2,1)}, u32[]{:S(2)}) copy-start(bf16[256,2048]{1,0:T(8,128)(2,1)} %param.16) | copy-start | bytes 3145732
  23.4 162.3 %all-gather.7.cloned.1.call-start = ((), (), s32[]{:S(2)}) async-start(), calls=%async_computation.3 | async-start | bytes 2785280 | tf_op jit(solution)/shard_map/all_gather | solution.py:106
  25.8 66.6 %copy-start.26 = (s32[2,5]{1,0:T(2,128)S(1)}, s32[2,5]{1,0:T(2,128)}, u32[]{:S(2)}) copy-start(s32[2,5]{1,0:T(2,128)} %param.18) | copy-start | bytes 124
  83.7 30.1 %collective-permute-start.3 = (bf16[256,2048]{1,0:T(8,128)(2,1)S(1)}, bf16[256,2048]{1,0:T(8,128)(2,1)}, u32[]{:S(2)}, u32[]{:S(2)}) collective-permute-start(bf16[256,2048]{1,0:T(8,128)(2,1)S(1)} %copy-done.6), channel_id=1, source_target_pairs={{0,8},{4,12},{8,16},{12,20},{16,24},{20,28},{24,32},{28,36},{32,40... | collective-permute-start | bytes 3145736 | tf_op jit(solution)/shard_map/ppermute | solution.py:21
  92.4 24.4 %copy-start.3 = (f32[64,136,128]{2,1,0:T(8,128)S(1)}, f32[64,136,128]{2,1,0:T(8,128)}, u32[]{:S(2)}) copy-start(f32[64,136,128]{2,1,0:T(8,128)} %all-gather.5.cloned.1.call-done) | copy-start | bytes 13369348
  92.9 42.2 %collective-permute-start.1 = (bf16[256,2048]{1,0:T(8,128)(2,1)}, bf16[256,2048]{1,0:T(8,128)(2,1)S(1)}, u32[]{:S(2)}, u32[]{:S(2)}) collective-permute-start(bf16[256,2048]{1,0:T(8,128)(2,1)} %param.17), channel_id=1, source_target_pairs={{0,8},{4,12},{8,16},{12,20},{16,24},{20,28},{24,32},{28,36},{32,40... | collective-permute-start | bytes 3145736 | tf_op jit(solution)/shard_map/ppermute | solution.py:21
  116.8 22.2 %collective-permute-start.4 = (bf16[256,2048]{1,0:T(8,128)(2,1)}, bf16[256,2048]{1,0:T(8,128)(2,1)}, u32[]{:S(2)}, u32[]{:S(2)}) collective-permute-start(bf16[256,2048]{1,0:T(8,128)(2,1)} %get-tuple-element.42), channel_id=1, source_target_pairs={{0,4},{4,0},{1,5},{5,1},{2,6},{6,2},{3,7},{7,3},{8,12},{12,8},{9,1... | collective-permute-start | bytes 3145736 | tf_op jit(solution)/shard_map/ppermute | solution.py:71
  138.0 5.6 %collective-permute-start.2 = (bf16[256,2048]{1,0:T(8,128)(2,1)}, bf16[256,2048]{1,0:T(8,128)(2,1)}, u32[]{:S(2)}, u32[]{:S(2)}) collective-permute-start(bf16[256,2048]{1,0:T(8,128)(2,1)} %get-tuple-element.40), channel_id=1, source_target_pairs={{0,4},{4,0},{1,5},{5,1},{2,6},{6,2},{3,7},{7,3},{8,12},{12,8},{9,1... | collective-permute-start | bytes 3145736 | tf_op jit(solution)/shard_map/ppermute | solution.py:71
  142.8 1.9 copy-start.2
  153.2 1.1 copy-start.22
  162.6 6.2 %copy-start.11 = (bf16[128,2048]{0,1:T(8,128)(2,1)S(1)}, bf16[128,2048]{0,1:T(8,128)(2,1)}, u32[]{:S(2)}) copy-start(bf16[128,2048]{0,1:T(8,128)(2,1)} %copy-done.10) | copy-start | bytes 1572868
  162.6 6.2 %copy-start.13 = (bf16[128,2048]{0,1:T(8,128)(2,1)S(1)}, bf16[128,2048]{0,1:T(8,128)(2,1)}, u32[]{:S(2)}) copy-start(bf16[128,2048]{0,1:T(8,128)(2,1)} %copy-done.12) | copy-start | bytes 1572868
  162.6 6.2 %copy-start.15 = (bf16[128,2048]{0,1:T(8,128)(2,1)S(1)}, bf16[128,2048]{0,1:T(8,128)(2,1)}, u32[]{:S(2)}) copy-start(bf16[128,2048]{0,1:T(8,128)(2,1)} %copy.222) | copy-start | bytes 1572868
  164.6 20.0 %all-to-all-start = ((bf16[4,64,2048]{2,1,0:T(8,128)(2,1)}), bf16[4,64,2048]{2,1,0:T(8,128)(2,1)S(1)}, u32[]{:S(2)}, u32[]{:S(2)}) async-start(bf16[4,64,2048]{2,1,0:T(8,128)(2,1)} %all_to_all.28), calls=%async_computation | async-start | bytes 2097152 | tf_op jit(solution)/shard_map/all_to_all | solution.py:233
  168.8 4.4 %copy-start.14 = (bf16[128,2048]{0,1:T(8,128)(2,1)S(1)}, bf16[128,2048]{0,1:T(8,128)(2,1)}, u32[]{:S(2)}) copy-start(bf16[128,2048]{0,1:T(8,128)(2,1)} %copy.225) | copy-start | bytes 1572868
  173.2 13.4 %copy-start.9 = (f32[8,128,128]{2,1,0:T(8,128)S(1)}, f32[8,128,128]{2,1,0:T(8,128)}, u32[]{:S(2)}) copy-start(f32[8,128,128]{2,1,0:T(8,128)} %get-tuple-element.29) | copy-start | bytes 1572868
  186.6 4.0 %copy-start.5 = (f32[16,128,128]{2,1,0:T(8,128)S(1)}, f32[16,128,128]{2,1,0:T(8,128)}, u32[]{:S(2)}) copy-start(f32[16,128,128]{2,1,0:T(8,128)} %copy-done.4) | copy-start | bytes 3145732
  186.6 3.9 %copy-start.18 = (f32[128,16,128]{2,0,1:T(8,128)S(1)}, f32[128,16,128]{2,0,1:T(8,128)}, u32[]{:S(2)}) copy-start(f32[128,16,128]{2,0,1:T(8,128)} %convolution_bitcast_fusion.1) | copy-start | bytes 3145732
  190.4 2.0 copy-start.8
  190.4 2.0 copy-start.20
  190.4 2.0 copy-start.21
  190.4 2.0 collective-permute-start.5
  192.4 1.6 copy-start.24
  194.7 20.3 %copy-start.1 = (f32[16,256]{1,0:T(8,128)S(1)}, f32[16,256]{1,0:T(8,128)}, u32[]{:S(2)}) copy-start(f32[16,256]{1,0:T(8,128)} %param.13) | copy-start | bytes 49156
  (4 other events, 3.7 us)
Sparse Core Ops, SparseCore 0:
  23.5 60.1 all-gather.4
  139.1 31.4 all-gather.6

commit v8 on v6

--- a/solution.py
+++ b/solution.py
@@ -65,6 +65,32 @@
 
 def unpacked(both, width):
     return both[..., :width, :], both[..., width, 0]
+
+
+def narrow(state, factor):
+    heads, width, _ = state.shape
+    high = factor.astype(jnp.bfloat16)
+    low = (factor - high.astype(jnp.float32)).astype(jnp.bfloat16)
+    rows = lambda part: jnp.broadcast_to(part[:, None, None], (heads, 8, width))
+    return jnp.concatenate([state.astype(jnp.bfloat16), rows(high), rows(low)], axis=1)
+
+
+def widened(both, width):
+    wide = both.astype(jnp.float32)
+    return wide[..., :width, :], wide[..., width, 0] + wide[..., width + 8, 0]
+
+
+def folded(states, factors, upto):
+    places = jnp.arange(states.shape[0])
+    between = (places[:, None] < places[None, :]) & (places[None, :] < upto)
+    weights = jnp.prod(jnp.where(between[:, :, None], factors[None], 1.0), axis=1)
+    weights = jnp.where((places < upto)[:, None], weights, 0.0)
+    return jnp.sum(weights[:, :, None, None] * states, axis=0)
+
+
+def spanned(factors, upto):
+    places = jnp.arange(factors.shape[0])
+    return jnp.prod(jnp.where((places < upto)[:, None], factors, 1.0), axis=0)
 
 
 def swapped(block):
@@ -89,26 +115,18 @@
     second_factor = lax.dynamic_slice_in_dim(second_all, low, half, 0)
     chip_state = second_factor[:, None, None] * first + second
     chip_factor = first_factor * second_factor
-    row_states, row_factors = unpacked(
-        lax.all_gather(packed(chip_state, chip_factor), "cz"), width
-    )
-    total = jnp.zeros_like(chip_state)
-    total_factor = jnp.ones_like(chip_factor)
-    before = total
-    before_factor = total_factor
-    for z in range(row_states.shape[0]):
-        here = z == row
-        before = jnp.where(here, total, before)
-        before_factor = jnp.where(here, total_factor, before_factor)
-        total = row_factors[z][:, None, None] * total + row_states[z]
-        total_factor = total_factor * row_factors[z]
-    column_packed = lax.all_gather(packed(total, total_factor), "cy")
+    row_states, row_factors = widened(
+        lax.all_gather(narrow(chip_state, chip_factor), "cz"), width
+    )
+    count = row_states.shape[0]
+    before = folded(row_states, row_factors, row)
+    before_factor = spanned(row_factors, row)
+    total = folded(row_states, row_factors, count)
+    total_factor = spanned(row_factors, count)
+    column_packed = lax.all_gather(narrow(total, total_factor), "cy")
     column_packed, held = lax.optimization_barrier((column_packed, held))
-    column_states, column_factors = unpacked(column_packed, width)
-    above = jnp.zeros_like(chip_state)
-    for y in range(column_states.shape[0]):
-        joined = column_factors[y][:, None, None] * above + column_states[y]
-        above = jnp.where(y < column, joined, above)
+    column_states, column_factors = widened(column_packed, width)
+    above = folded(column_states, column_factors, column)
     prefix_half = before_factor[:, None, None] * above + before
     other_half = swapped(prefix_half)
     prefix = jnp.where(

time: 212 us -> 177 us (0.83)
  waiting for transfers between devices: 80 us -> 42.6 us
  local copies, waits for them, and re-layouts: 36.6 us -> 39.4 us
    ppermute x2, waiting for transfers between devices: 64.9 us -> 16.8 us  [passed_along(): return lax.ppermute(block, axis, route)]
    all_gather x2, waiting for transfers between devices: 2.72 us -> 17.8 us  [the longest x1 17.8 us: carry_in(): lax.all_gather(narrow(chip_state, chip_factor), 'cz')]
    convert_element_type x0 -> x5, other arithmetic: none -> 4.1 us  [the longest x2 3.86 us: widened(): wide = both.astype(jnp.float32)]
    add x1, other arithmetic: 3.65 us -> 0.12 us  [carry_in(): prefix_half = before_factor[:, None, None] * above + before]
    unnamed x72 -> x64, local copies, waits for them, and re-layouts: 21.3 us -> 24.3 us
    dot_general x2, matrix products: 5.81 us -> 8.73 us  [attend(): jnp.einsum('htkj,kjhd->thd', weights, values_sel, preferred_element_type=...]
    ppermute x4, waiting for transfers between devices: 4.31 us -> 1.46 us  [swapped(): return lax.ppermute(block, 'cc', [(0, 1), (1, 0)])]
    dot_general x2, matrix products: 5.28 us -> 2.63 us  [attend(): jnp.einsum('thd,kjhd->htkj', query_blk, keys_sel, preferred_element_type=...]
  transfers between devices with their start and end apart: 9 -> 9, of which waited for: 6 -> 4; matrix products, arithmetic and copies ran while one was open for 26% -> 41% of each run, Pallas kernels for 0% -> 0%
where the time goes in v8:
time: 177 us; the launch traced here: 175 us
  waiting for transfers between devices  42.6 us (24%)
  local copies, waits for them, and re-layouts  39.4 us (22%)
  other arithmetic  24.1 us (14%)
  matrix products  23 us (13%)
  blocking collectives  18.8 us (11%)
  between operations  14.7 us (8%)
  starting transfers between devices  12.7 us (7%)
    unnamed x64, local copies, waits for them, and re-layouts  24.3 us
    all_to_all x1, blocking collectives, local(): lax.all_to_all(linear_heads, 'head', split_axis=0, concat_axis=1, tiled=T...  18.8 us
    all_gather x1, waiting for transfers between devices, carry_in(): lax.all_gather(narrow(chip_state, chip_factor), 'cz')  17.8 us
    ppermute x2, waiting for transfers between devices, passed_along(): return lax.ppermute(block, axis, route)  16.8 us
    dot_general x2, matrix products, attend(): jnp.einsum('htkj,kjhd->thd', weights, values_sel, preferred_element_type=...  8.73 us
    ppermute x2, starting transfers between devices, passed_along(): return lax.ppermute(block, axis, route)  7.66 us
    all_to_all x1, waiting for transfers between devices, local(): lax.all_to_all(softmax_heads, 'head', split_axis=0, concat_axis=1, tiled=...  6.54 us
    dot_general x2, matrix products, block_output(): jnp.einsum('htj,jhd->thd', mixing, values_blk, preferred_element_type=jnp...  6.28 us
  transfers between devices with their start and end apart: 9, of which 4 were waited for; matrix products, arithmetic and copies ran while one was open for 41% of the time, Pallas kernels for 0%

profile of v8, /device:TPU:8, one launch (start us, length us, event | category | flops | bytes accessed | tf_op | source)
XLA Modules:
  0.0 175.4 jit_solution(4541688428464686131)
XLA Ops:
  7.2 3.8 %collective-permute-start.3 = (bf16[256,2048]{1,0:T(8,128)(2,1)}, bf16[256,2048]{1,0:T(8,128)(2,1)}, u32[]{:S(2)}, u32[]{:S(2)}) collective-permute-start(bf16[256,2048]{1,0:T(8,128)(2,1)} %param.16), channel_id=1, source_target_pairs={{0,8},{4,12},{8,16},{12,20},{16,24},{20,28},{24,32},{28,36},{32,40... | collective-permute-start | bytes 3145736 | tf_op jit(solution)/shard_map/ppermute | solution.py:21
  11.1 3.8 %collective-permute-start.1 = (bf16[256,2048]{1,0:T(8,128)(2,1)}, bf16[256,2048]{1,0:T(8,128)(2,1)}, u32[]{:S(2)}, u32[]{:S(2)}) collective-permute-start(bf16[256,2048]{1,0:T(8,128)(2,1)} %param.17), channel_id=1, source_target_pairs={{0,8},{4,12},{8,16},{12,20},{16,24},{20,28},{24,32},{28,36},{32,40... | collective-permute-start | bytes 3145736 | tf_op jit(solution)/shard_map/ppermute | solution.py:21
  17.4 1.5 fusion.87
  25.2 2.3 %fusion.84 = (bf16[128,2048]{1,0:T(8,128)(2,1)}, bf16[128,2048]{1,0:T(8,128)(2,1)}) fusion(bf16[256,2048]{1,0:T(8,128)(2,1)} %param.15), kind=kLoop, calls=%fused_computation.170 | loop fusion | bytes 2097152 | tf_op jit(solution)/shard_map/slice | solution.py:222
  27.9 2.1 %fusion.85 = (bf16[128,2048]{1,0:T(8,128)(2,1)S(1)}, bf16[128,2048]{1,0:T(8,128)(2,1)}) fusion(bf16[256,2048]{1,0:T(8,128)(2,1)} %param.10), kind=kLoop, calls=%fused_computation.171 | loop fusion | bytes 2097152 | tf_op jit(solution)/shard_map/slice | solution.py:161
  31.0 3.2 %convolution_bitcast_fusion.3 = f32[128,16,128]{2,0,1:T(8,128)} fusion(bf16[128,16,128]{0,2,1:T(8,128)(2,1)} %bitcast.185, bf16[128,16,128]{0,2,1:T(8,128)(2,1)} %bitcast.180, bf16[128,16,128]{0,2,1:T(8,128)(2,1)} %bitcast.183, f32[16,128]{1,0:T(8,128)S(1)} %get-tuple-element.44, pred[128,128]{1,0:T(8,128)(4,1)S(1)} %iota_compare_fusion), kind=kOutput, calls=%fused_computation.44 | convolution fusion | flops 135528448 | bytes 2646016 | tf_op jit(solution)/shard_map/htj,jhd->thd/dot_general | solution.py:48
  34.2 2.0 %copy.313 = bf16[128,2048]{0,1:T(8,128)(2,1)} copy(bf16[128,2048]{1,0:T(8,128)(2,1)} %get-tuple-element.22) | data formatting | bytes 1048576
  36.3 2.1 %copy.314 = bf16[128,2048]{0,1:T(8,128)(2,1)} copy(bf16[128,2048]{1,0:T(8,128)(2,1)} %get-tuple-element.23) | data formatting | bytes 1048576
  38.3 2.1 %copy.310 = bf16[128,2048]{0,1:T(8,128)(2,1)} copy(bf16[128,2048]{1,0:T(8,128)(2,1)} %get-tuple-element.29) | data formatting | bytes 1048576
  40.4 3.1 %broadcast_select_fusion = (bf16[256,2048]{1,0:T(8,128)(2,1)}, bf16[768,2048]{1,0:T(8,128)(2,1)}) fusion(bf16[256,2048]{1,0:T(8,128)(2,1)S(1)} %copy-done.4, bf16[256,2048]{1,0:T(8,128)(2,1)} %collective-permute-done.3, pred[]{:T(512)S(6)} %eq.34), kind=kLoop, calls=%fused_computation.69 | loop fusion | flops 524287 | bytes 4194305 | tf_op jit(solution)/shard_map/jit(_where)/select_n | solution.py:198
  44.0 16.8 %collective-permute-done.1 = bf16[256,2048]{1,0:T(8,128)(2,1)} collective-permute-done((bf16[256,2048]{1,0:T(8,128)(2,1)}, bf16[256,2048]{1,0:T(8,128)(2,1)}, u32[]{:S(2)}, u32[]{:S(2)}) %collective-permute-start.1) | collective-permute-done | bytes 1048608 | tf_op jit(solution)/shard_map/ppermute | solution.py:21
  60.8 3.1 %broadcast_select_fusion.1 = (bf16[256,2048]{1,0:T(8,128)(2,1)}, bf16[768,2048]{1,0:T(8,128)(2,1)}) fusion(bf16[256,2048]{1,0:T(8,128)(2,1)S(1)} %copy-done.5, bf16[256,2048]{1,0:T(8,128)(2,1)} %collective-permute-done.1, pred[]{:T(512)S(6)} %eq.34), kind=kLoop, calls=%fused_computation.70 | loop fusion | flops 524287 | bytes 4194305 | tf_op jit(solution)/shard_map/jit(_where)/select_n | solution.py:198
  65.1 1.4 fusion.83
  68.6 2.4 %constant_dynamic-update-slice_fusion.4 = bf16[768,2048]{1,0:T(8,128)(2,1)} fusion(bf16[768,2048]{1,0:T(8,128)(2,1)} %get-tuple-element.27, bf16[256,2048]{1,0:T(8,128)(2,1)} %collective-permute-done.4), kind=kLoop, calls=%fused_computation.114 | loop fusion | bytes 2097152
  72.0 3.6 %slice_bitcast_fusion.2 = (bf16[80,8,16,128]{3,1,2,0:T(8,128)(2,1)S(1)}, bf16[80,8,16,128]{3,1,2,0:T(8,128)(2,1)S(1)}) fusion(bf16[768,2048]{1,0:T(8,128)(2,1)} %constant_dynamic-update-slice_fusion.3), kind=kLoop, calls=%fused_computation.14 | loop fusion | bytes 10485760
  77.5 1.3 constant_dynamic-update-slice_fusion.1
  79.0 1.8 %slice_bitcast_fusion.3 = (bf16[80,8,16,128]{3,1,2,0:T(8,128)(2,1)S(1)}, bf16[80,8,16,128]{3,1,2,0:T(8,128)(2,1)S(1)}) fusion(bf16[768,2048]{1,0:T(8,128)(2,1)S(1)} %constant_dynamic-update-slice_fusion), kind=kLoop, calls=%fused_computation.15 | loop fusion | bytes 10485760
  82.5 2.3 %copy.322 = bf16[80,8,16,128]{3,2,1,0:T(8,128)(2,1)} copy(bf16[80,8,16,128]{3,1,2,0:T(8,128)(2,1)S(1)} %get-tuple-element.17) | data formatting | bytes 5242880
  86.1 1.3 fusion.3
  89.8 2.8 %fusion.32 = bf16[128,16,128]{2,0,1:T(8,128)(2,1)S(1)} fusion(f32[16,5,128,128]{3,2,1,0:T(8,128)S(1)} %get-tuple-element.62, f32[16,128]{1,0:T(8,128)S(1)} %fusion, f32[16,128]{1,0:T(8,128)S(1)} %get-tuple-element.61, pred[128,5,128]{0,2,1:T(8,128)(4,1)S(1)} %get-tuple-element.34, bf16[5,128,16,128]{3,2,1,0:T(8,128)(2,1)S(1)} %bitcast.176), kind=kOutput, calls=%fused_computation.50 | convolution fusion | flops 342360064 | bytes 8486912 | tf_op jit(solution)/shard_map/htkj,kjhd->thd/dot_general | solution.py:187
  92.6 17.8 %all-gather.5.cloned.1.call-done = bf16[64,144,128]{2,1,0:T(8,128)(2,1)} async-done(((bf16[8,144,128]{2,1,0:T(8,128)(2,1)}), bf16[64,144,128]{2,1,0:T(8,128)(2,1)}) %all-gather.5.cloned.1.call-update) | async-done | bytes 2359312 | tf_op jit(solution)/shard_map/all_gather | solution.py:119
  110.4 2.3 %bitcast_convert_fusion = f32[8,8,144,128]{3,2,1,0:T(8,128)S(1)} fusion(bf16[64,144,128]{2,1,0:T(8,128)(2,1)} %all-gather.5.cloned.1.call-done), kind=kLoop, calls=%fused_computation.157 | loop fusion | flops 1179648 | bytes 7077888 | tf_op jit(solution)/shard_map/convert_element_type | solution.py:79
  113.1 1.5 multiply_reduce_fusion.1
  115.5 5.9 %fusion.35 = bf16[128,16,128]{2,0,1:T(8,128)(2,1)S(1)} fusion(f32[16,5,128,128]{3,2,1,0:T(8,128)} %copy-done.3, f32[16,128]{1,0:T(8,128)S(1)} %fusion.1, f32[16,128]{1,0:T(8,128)S(1)} %get-tuple-element.59, pred[128,5,128]{0,2,1:T(8,128)(4,1)S(1)} %get-tuple-element.35, bf16[5,128,16,128]{3,2,1,0:T(8,128)(2,1)} %bitcast.174), kind=kOutput, calls=%fused_computation.51 | convolution fusion | flops 342360064 | bytes 8486912 | tf_op jit(solution)/shard_map/htkj,kjhd->thd/dot_general | solution.py:187
  123.5 4.2 %all-to-all-start = ((bf16[4,64,2048]{2,1,0:T(8,128)(2,1)}), bf16[4,64,2048]{2,1,0:T(8,128)(2,1)S(1)}, u32[]{:S(2)}, u32[]{:S(2)}) async-start(bf16[4,64,2048]{2,1,0:T(8,128)(2,1)} %all_to_all.28), calls=%async_computation | async-start | bytes 2097152 | tf_op jit(solution)/shard_map/all_to_all | solution.py:248
  127.7 2.5 %fusion.23 = f32[128,16,128]{2,0,1:T(8,128)} fusion(f32[128,16,128]{2,0,1:T(8,128)} %convolution_bitcast_fusion.3, bf16[128,16,128]{0,2,1:T(8,128)(2,1)S(1)} %bitcast.181, f32[128,16]{0,1:T(8,128)S(1)} %get-tuple-element.41), kind=kOutput, calls=%fused_computation.43 | convolution fusion | flops 68157440 | bytes 2629632 | tf_op jit(solution)/shard_map/thd,hde->the/dot_general | solution.py:52
  130.2 3.0 %convolution_bitcast_fusion.1 = f32[128,16,128]{2,0,1:T(8,128)} fusion(bf16[128,16,128]{0,2,1:T(8,128)(2,1)} %bitcast.187, bf16[128,16,128]{0,2,1:T(8,128)(2,1)S(1)} %bitcast.178, bf16[128,16,128]{0,2,1:T(8,128)(2,1)} %bitcast.189, f32[16,128]{1,0:T(8,128)S(1)} %get-tuple-element.45, pred[128,128]{1,0:T(8,128)(4,1)S(1)} %iota_compare_fusion), kind=kOutput, calls=%fused_computation.40 | convolution fusion | flops 135528448 | bytes 2646016 | tf_op jit(solution)/shard_map/htj,jhd->thd/dot_general | solution.py:48
  133.3 6.5 %all-to-all-done = bf16[4,64,2048]{2,1,0:T(8,128)(2,1)S(1)} async-done(((bf16[4,64,2048]{2,1,0:T(8,128)(2,1)}), bf16[4,64,2048]{2,1,0:T(8,128)(2,1)S(1)}, u32[]{:S(2)}, u32[]{:S(2)}) %all-to-all-start) | async-done | bytes 1048608 | tf_op jit(solution)/shard_map/all_to_all | solution.py:248
  140.9 1.6 convert_element_type.139
  143.7 1.4 collective-permute-done.5
  145.2 1.5 multiply_reduce_fusion.2
  148.7 18.8 %all_to_all.38 = bf16[4,64,2048]{2,1,0:T(8,128)(2,1)S(1)} all-to-all(bf16[4,64,2048]{2,1,0:T(8,128)(2,1)S(1)} %all_to_all.32), channel_id=1, replica_groups=mesh['cy'=4,'cz'=8,'cc'=2,'head'=4] {'head'}, dimensions={0} | all-to-all | bytes 2097152 | tf_op jit(solution)/shard_map/all_to_all | solution.py:252
  (138 shorter events, 30.6 us)
Async XLA Ops:
  7.2 7.7 %copy-start = (f32[16,256]{1,0:T(8,128)S(1)}, f32[16,256]{1,0:T(8,128)}, u32[]{:S(2)}) copy-start(f32[16,256]{1,0:T(8,128)} %param.13) | copy-start | bytes 49156
  7.2 103.2 %all-gather.5.cloned.1.call-start = ((), (), s32[]{:S(2)}) async-start(), calls=%async_computation.2 | async-start | bytes 2654208 | tf_op jit(solution)/shard_map/all_gather | solution.py:119
  7.2 33.1 %collective-permute-start.3 = (bf16[256,2048]{1,0:T(8,128)(2,1)}, bf16[256,2048]{1,0:T(8,128)(2,1)}, u32[]{:S(2)}, u32[]{:S(2)}) collective-permute-start(bf16[256,2048]{1,0:T(8,128)(2,1)} %param.16), channel_id=1, source_target_pairs={{0,8},{4,12},{8,16},{12,20},{16,24},{20,28},{24,32},{28,36},{32,40... | collective-permute-start | bytes 3145736 | tf_op jit(solution)/shard_map/ppermute | solution.py:21
  11.1 49.8 %collective-permute-start.1 = (bf16[256,2048]{1,0:T(8,128)(2,1)}, bf16[256,2048]{1,0:T(8,128)(2,1)}, u32[]{:S(2)}, u32[]{:S(2)}) collective-permute-start(bf16[256,2048]{1,0:T(8,128)(2,1)} %param.17), channel_id=1, source_target_pairs={{0,8},{4,12},{8,16},{12,20},{16,24},{20,28},{24,32},{28,36},{32,40... | collective-permute-start | bytes 3145736 | tf_op jit(solution)/shard_map/ppermute | solution.py:21
  17.4 3.9 %copy-start.11 = (bf16[128,2048]{0,1:T(8,128)(2,1)}, bf16[128,2048]{0,1:T(8,128)(2,1)S(1)}, u32[]{:S(2)}) copy-start(bf16[128,2048]{0,1:T(8,128)(2,1)S(1)} %copy.308) | copy-start | bytes 1572868
  19.2 2.2 %copy-start.12 = (bf16[128,2048]{0,1:T(8,128)(2,1)}, bf16[128,2048]{0,1:T(8,128)(2,1)S(1)}, u32[]{:S(2)}) copy-start(bf16[128,2048]{0,1:T(8,128)(2,1)S(1)} %copy.309) | copy-start | bytes 1572868
  19.4 2.4 %copy-start.14 = (bf16[128,2048]{0,1:T(8,128)(2,1)}, bf16[128,2048]{0,1:T(8,128)(2,1)S(1)}, u32[]{:S(2)}) copy-start(bf16[128,2048]{0,1:T(8,128)(2,1)S(1)} %copy.312) | copy-start | bytes 1572868
  19.7 3.3 %copy-start.15 = (bf16[128,2048]{0,1:T(8,128)(2,1)}, bf16[128,2048]{0,1:T(8,128)(2,1)S(1)}, u32[]{:S(2)}) copy-start(bf16[128,2048]{0,1:T(8,128)(2,1)S(1)} %copy.311) | copy-start | bytes 1572868
  21.3 1.8 %copy-start.22 = (s32[2]{0:T(128)S(1)}, s32[2]{0:T(128)}, u32[]{:S(2)}) copy-start(s32[2]{0:T(128)} %param.19) | copy-start | bytes 28
  21.3 3.7 %copy-start.23 = (s32[2,5]{1,0:T(2,128)S(1)}, s32[2,5]{1,0:T(2,128)}, u32[]{:S(2)}) copy-start(s32[2,5]{1,0:T(2,128)} %param.18) | copy-start | bytes 124
  23.0 40.9 %collective-permute-start = (f32[16,136,128]{2,1,0:T(8,128)}, f32[16,136,128]{2,1,0:T(8,128)}, u32[]{:S(2)}, u32[]{:S(2)}) collective-permute-start(f32[16,136,128]{2,1,0:T(8,128)} %pad_maximum_fusion), channel_id=1, source_target_pairs={{0,4},{4,0},{1,5},{5,1},{2,6},{6,2},{3,7},{7,3},{8,12},{12,8},{9,1... | collective-permute-start | bytes 3342344 | tf_op jit(solution)/shard_map/ppermute | solution.py:97
  31.0 9.4 %copy-start.4 = (bf16[256,2048]{1,0:T(8,128)(2,1)S(1)}, bf16[256,2048]{1,0:T(8,128)(2,1)}, u32[]{:S(2)}) copy-start(bf16[256,2048]{1,0:T(8,128)(2,1)} %param.16) | copy-start | bytes 3145732
  40.4 20.4 %copy-start.5 = (bf16[256,2048]{1,0:T(8,128)(2,1)S(1)}, bf16[256,2048]{1,0:T(8,128)(2,1)}, u32[]{:S(2)}) copy-start(bf16[256,2048]{1,0:T(8,128)(2,1)} %param.17) | copy-start | bytes 3145732
  43.5 25.1 %collective-permute-start.4 = (bf16[256,2048]{1,0:T(8,128)(2,1)}, bf16[256,2048]{1,0:T(8,128)(2,1)}, u32[]{:S(2)}, u32[]{:S(2)}) collective-permute-start(bf16[256,2048]{1,0:T(8,128)(2,1)} %get-tuple-element.26), channel_id=1, source_target_pairs={{0,4},{4,0},{1,5},{5,1},{2,6},{6,2},{3,7},{7,3},{8,12},{12,8},{9,1... | collective-permute-start | bytes 3145736 | tf_op jit(solution)/shard_map/ppermute | solution.py:97
  63.9 12.6 %collective-permute-start.2 = (bf16[256,2048]{1,0:T(8,128)(2,1)}, bf16[256,2048]{1,0:T(8,128)(2,1)}, u32[]{:S(2)}, u32[]{:S(2)}) collective-permute-start(bf16[256,2048]{1,0:T(8,128)(2,1)} %get-tuple-element.24), channel_id=1, source_target_pairs={{0,4},{4,0},{1,5},{5,1},{2,6},{6,2},{3,7},{7,3},{8,12},{12,8},{9,1... | collective-permute-start | bytes 3145736 | tf_op jit(solution)/shard_map/ppermute | solution.py:97
  68.4 72.5 %all-gather.7.cloned.1.call-start = ((), (), s32[]{:S(2)}) async-start(), calls=%async_computation.3 | async-start | bytes 1474560 | tf_op jit(solution)/shard_map/all_gather | solution.py:126
  75.6 1.9 %copy-start.2 = (bf16[768,2048]{1,0:T(8,128)(2,1)S(1)}, bf16[768,2048]{1,0:T(8,128)(2,1)}, u32[]{:S(2)}) copy-start(bf16[768,2048]{1,0:T(8,128)(2,1)} %get-tuple-element.25) | copy-start | bytes 9437188
  75.7 3.2 %copy-start.6 = (bf16[256,2048]{1,0:T(8,128)(2,1)S(1)}, bf16[256,2048]{1,0:T(8,128)(2,1)}, u32[]{:S(2)}) copy-start(bf16[256,2048]{1,0:T(8,128)(2,1)} %param.17) | copy-start | bytes 3145732
  82.5 2.3 %copy-start.20 = (bf16[128,2048]{0,1:T(8,128)(2,1)S(1)}, bf16[128,2048]{0,1:T(8,128)(2,1)}, u32[]{:S(2)}) copy-start(bf16[128,2048]{0,1:T(8,128)(2,1)} %copy.313) | copy-start | bytes 1572868
  84.8 1.3 copy-start.19
  87.4 2.4 %copy-start.3 = (f32[16,5,128,128]{3,2,1,0:T(8,128)}, f32[16,5,128,128]{3,2,1,0:T(8,128)S(1)}, u32[]{:S(2)}) copy-start(f32[16,5,128,128]{3,2,1,0:T(8,128)S(1)} %get-tuple-element.60) | copy-start | bytes 15728644
  121.5 6.2 %copy-start.10 = (bf16[128,2048]{0,1:T(8,128)(2,1)S(1)}, bf16[128,2048]{0,1:T(8,128)(2,1)}, u32[]{:S(2)}) copy-start(bf16[128,2048]{0,1:T(8,128)(2,1)} %copy.307) | copy-start | bytes 1572868
  122.2 8.0 %copy-start.9 = (bf16[128,2048]{0,1:T(8,128)(2,1)S(1)}, bf16[128,2048]{0,1:T(8,128)(2,1)}, u32[]{:S(2)}) copy-start(bf16[128,2048]{0,1:T(8,128)(2,1)} %copy.310) | copy-start | bytes 1572868
  123.5 16.3 %all-to-all-start = ((bf16[4,64,2048]{2,1,0:T(8,128)(2,1)}), bf16[4,64,2048]{2,1,0:T(8,128)(2,1)S(1)}, u32[]{:S(2)}, u32[]{:S(2)}) async-start(bf16[4,64,2048]{2,1,0:T(8,128)(2,1)} %all_to_all.28), calls=%async_computation | async-start | bytes 2097152 | tf_op jit(solution)/shard_map/all_to_all | solution.py:248
  140.9 2.2 %copy-start.13 = (f32[8,128,128]{2,1,0:T(8,128)S(1)}, f32[8,128,128]{2,1,0:T(8,128)}, u32[]{:S(2)}) copy-start(f32[8,128,128]{2,1,0:T(8,128)} %get-tuple-element.7) | copy-start | bytes 1572868
  140.9 2.5 %copy-start.16 = (f32[128,16,128]{2,0,1:T(8,128)S(1)}, f32[128,16,128]{2,0,1:T(8,128)}, u32[]{:S(2)}) copy-start(f32[128,16,128]{2,0,1:T(8,128)} %convolution_bitcast_fusion.1) | copy-start | bytes 3145732
  143.0 2.2 %copy-start.8 = (f32[16,128,128]{2,1,0:T(8,128)S(1)}, f32[16,128,128]{2,1,0:T(8,128)}, u32[]{:S(2)}) copy-start(f32[16,128,128]{2,1,0:T(8,128)} %copy-done.7) | copy-start | bytes 3145732
  143.0 2.2 %copy-start.17 = (bf16[256,2048]{1,0:T(8,128)(2,1)S(1)}, bf16[256,2048]{1,0:T(8,128)(2,1)}, u32[]{:S(2)}) copy-start(bf16[256,2048]{1,0:T(8,128)(2,1)} %param.10) | copy-start | bytes 3145732
  143.0 2.1 %copy-start.18 = (f32[128,16,128]{2,0,1:T(8,128)S(1)}, f32[128,16,128]{2,0,1:T(8,128)}, u32[]{:S(2)}) copy-start(f32[128,16,128]{2,0,1:T(8,128)} %fusion.23) | copy-start | bytes 3145732
  143.2 2.0 %collective-permute-start.5 = (f32[8,128,128]{2,1,0:T(8,128)S(1)}, f32[8,128,128]{2,1,0:T(8,128)S(1)}, u32[]{:S(2)}, u32[]{:S(2)}) collective-permute-start(f32[8,128,128]{2,1,0:T(8,128)S(1)} %multiply_add_fusion), channel_id=1, source_target_pairs={{0,4},{4,0},{1,5},{5,1},{2,6},{6,2},{3,7},{7,3},{8,12},{12,8},{9,1... | collective-permute-start | bytes 1572872 | tf_op jit(solution)/shard_map/ppermute | solution.py:97
  145.2 1.6 copy-start.21
  147.5 21.0 %copy-start.1 = (f32[16,256]{1,0:T(8,128)S(1)}, f32[16,256]{1,0:T(8,128)}, u32[]{:S(2)}) copy-start(f32[16,256]{1,0:T(8,128)} %param.13) | copy-start | bytes 49156
  (1 other events, 1.0 us)
Sparse Core Ops, SparseCore 0:
  68.5 41.8 all-gather.4
  115.6 24.5 all-gather.6

commit v9 on v8

--- a/solution.py
+++ b/solution.py
@@ -65,19 +65,6 @@
 
 def unpacked(both, width):
     return both[..., :width, :], both[..., width, 0]
-
-
-def narrow(state, factor):
-    heads, width, _ = state.shape
-    high = factor.astype(jnp.bfloat16)
-    low = (factor - high.astype(jnp.float32)).astype(jnp.bfloat16)
-    rows = lambda part: jnp.broadcast_to(part[:, None, None], (heads, 8, width))
-    return jnp.concatenate([state.astype(jnp.bfloat16), rows(high), rows(low)], axis=1)
-
-
-def widened(both, width):
-    wide = both.astype(jnp.float32)
-    return wide[..., :width, :], wide[..., width, 0] + wide[..., width + 8, 0]
 
 
 def folded(states, factors, upto):
@@ -115,17 +102,17 @@
     second_factor = lax.dynamic_slice_in_dim(second_all, low, half, 0)
     chip_state = second_factor[:, None, None] * first + second
     chip_factor = first_factor * second_factor
-    row_states, row_factors = widened(
-        lax.all_gather(narrow(chip_state, chip_factor), "cz"), width
+    row_states, row_factors = unpacked(
+        lax.all_gather(packed(chip_state, chip_factor), "cz"), width
     )
     count = row_states.shape[0]
     before = folded(row_states, row_factors, row)
     before_factor = spanned(row_factors, row)
     total = folded(row_states, row_factors, count)
     total_factor = spanned(row_factors, count)
-    column_packed = lax.all_gather(narrow(total, total_factor), "cy")
+    column_packed = lax.all_gather(packed(total, total_factor), "cy")
     column_packed, held = lax.optimization_barrier((column_packed, held))
-    column_states, column_factors = widened(column_packed, width)
+    column_states, column_factors = unpacked(column_packed, width)
     above = folded(column_states, column_factors, column)
     prefix_half = before_factor[:, None, None] * above + before
     other_half = swapped(prefix_half)

time: 177 us -> 225 us (1.27)
  waiting for transfers between devices: 42.6 us -> 84.1 us
  local copies, waits for them, and re-layouts: 39.4 us -> 44.1 us
    ppermute x2, waiting for transfers between devices: 16.8 us -> 67.2 us  [passed_along(): return lax.ppermute(block, axis, route)]
    all_gather x2, waiting for transfers between devices: 17.8 us -> 2.69 us  [the longest x1 2.67 us: carry_in(): column_packed = lax.all_gather(packed(total, total_factor), 'cy')]
    all_to_all x1, waiting for transfers between devices: 6.54 us -> 11.3 us  [local(): lax.all_to_all(softmax_heads, 'head', split_axis=0, concat_axis=1, tiled=...]
    convert_element_type x5 -> x0, other arithmetic: 4.1 us -> none  [the longest x2 3.86 us: widened(): wide = both.astype(jnp.float32)]
    reduce_sum x2, other arithmetic: 1.72 us -> 5.66 us  [folded(): return jnp.sum(weights[:, :, None, None] * states, axis=0)]
    dot_general x2, matrix products: 8.73 us -> 5.81 us  [attend(): jnp.einsum('htkj,kjhd->thd', weights, values_sel, preferred_element_type=...]
    dot_general x2, matrix products: 2.63 us -> 5.27 us  [attend(): jnp.einsum('thd,kjhd->htkj', query_blk, keys_sel, preferred_element_type=...]
    reduce_sum x2, other arithmetic: 2.17 us -> 4.77 us  [attend(): jnp.sum(raised, axis=(2, 3), keepdims=True)]
  transfers between devices with their start and end apart: 9 -> 9, of which waited for: 4 -> 6; matrix products, arithmetic and copies ran while one was open for 41% -> 28% of each run, Pallas kernels for 0% -> 0%
where the time goes in v9:
time: 225 us; the launch traced here: 223 us
  waiting for transfers between devices  84.1 us (37%)
  local copies, waits for them, and re-layouts  44.1 us (20%)
  other arithmetic  25.2 us (11%)
  matrix products  22.6 us (10%)
  blocking collectives  19.6 us (9%)
  between operations  14.7 us (7%)
  starting transfers between devices  12.5 us (6%)
    ppermute x2, waiting for transfers between devices, passed_along(): return lax.ppermute(block, axis, route)  67.2 us
    unnamed x82, local copies, waits for them, and re-layouts  25.4 us
    all_to_all x1, blocking collectives, local(): lax.all_to_all(linear_heads, 'head', split_axis=0, concat_axis=1, tiled=T...  19.6 us
    all_to_all x1, waiting for transfers between devices, local(): lax.all_to_all(softmax_heads, 'head', split_axis=0, concat_axis=1, tiled=...  11.3 us
    ppermute x2, starting transfers between devices, passed_along(): return lax.ppermute(block, axis, route)  7.79 us
    dot_general x2, matrix products, attend(): jnp.einsum('htkj,kjhd->thd', weights, values_sel, preferred_element_type=...  5.81 us
    select_n x2, other arithmetic, softmax_layer(): jnp.where(on_first, own, far)  5.68 us
    reduce_sum x2, other arithmetic, folded(): return jnp.sum(weights[:, :, None, None] * states, axis=0)  5.66 us
  transfers between devices with their start and end apart: 9, of which 6 were waited for; matrix products, arithmetic and copies ran while one was open for 28% of the time, Pallas kernels for 0%

profile of v9, /device:TPU:8, one launch (start us, length us, event | category | flops | bytes accessed | tf_op | source)
XLA Modules:
  0.0 222.7 jit_solution(8236748957941102032)
XLA Ops:
  16.0 2.9 %collective-permute-done = f32[16,136,128]{2,1,0:T(8,128)} collective-permute-done((f32[16,136,128]{2,1,0:T(8,128)S(1)}, f32[16,136,128]{2,1,0:T(8,128)}, u32[]{:S(2)}, u32[]{:S(2)}) %collective-permute-start) | collective-permute-done | bytes 1114144 | tf_op jit(solution)/shard_map/ppermute | solution.py:84
  20.0 1.5 fusion.78
  23.5 4.0 %collective-permute-start.3 = (bf16[256,2048]{1,0:T(8,128)(2,1)S(1)}, bf16[256,2048]{1,0:T(8,128)(2,1)}, u32[]{:S(2)}, u32[]{:S(2)}) collective-permute-start(bf16[256,2048]{1,0:T(8,128)(2,1)S(1)} %copy-done.6), channel_id=1, source_target_pairs={{0,8},{4,12},{8,16},{12,20},{16,24},{20,28},{24,32},{28,36},{32,40... | collective-permute-start | bytes 3145736 | tf_op jit(solution)/shard_map/ppermute | solution.py:21
  27.5 3.8 %collective-permute-start.1 = (bf16[256,2048]{1,0:T(8,128)(2,1)S(1)}, bf16[256,2048]{1,0:T(8,128)(2,1)}, u32[]{:S(2)}, u32[]{:S(2)}) collective-permute-start(bf16[256,2048]{1,0:T(8,128)(2,1)S(1)} %copy-done.7), channel_id=1, source_target_pairs={{0,8},{4,12},{8,16},{12,20},{16,24},{20,28},{24,32},{28,36},{32,40... | collective-permute-start | bytes 3145736 | tf_op jit(solution)/shard_map/ppermute | solution.py:21
  33.6 2.3 %fusion.80 = (bf16[128,2048]{1,0:T(8,128)(2,1)}, bf16[128,2048]{1,0:T(8,128)(2,1)}) fusion(bf16[256,2048]{1,0:T(8,128)(2,1)} %param.10), kind=kLoop, calls=%fused_computation.163 | loop fusion | bytes 2097152 | tf_op jit(solution)/shard_map/slice | solution.py:148
  36.0 2.0 copy.303
  38.3 2.3 %fusion.79 = (bf16[128,2048]{1,0:T(8,128)(2,1)}, bf16[128,2048]{1,0:T(8,128)(2,1)}) fusion(bf16[256,2048]{1,0:T(8,128)(2,1)} %param.15), kind=kLoop, calls=%fused_computation.162 | loop fusion | bytes 2097152 | tf_op jit(solution)/shard_map/slice | solution.py:209
  40.6 2.8 %convolution_bitcast_fusion.3 = f32[128,16,128]{2,0,1:T(8,128)} fusion(bf16[128,16,128]{0,2,1:T(8,128)(2,1)S(1)} %bitcast.183, bf16[128,16,128]{0,2,1:T(8,128)(2,1)} %bitcast.184, bf16[128,16,128]{0,2,1:T(8,128)(2,1)S(1)} %bitcast.181, f32[16,128]{1,0:T(8,128)S(1)} %get-tuple-element.46, pred[128,128]{1,0:T(8,128)(4,1)S(1)} %iota_compare_fusion), kind=kOutput, calls=%fused_computation.43 | convolution fusion | flops 135528448 | bytes 2646016 | tf_op jit(solution)/shard_map/htj,jhd->thd/dot_general | solution.py:48
  43.4 25.7 %collective-permute-done.3 = bf16[256,2048]{1,0:T(8,128)(2,1)} collective-permute-done((bf16[256,2048]{1,0:T(8,128)(2,1)S(1)}, bf16[256,2048]{1,0:T(8,128)(2,1)}, u32[]{:S(2)}, u32[]{:S(2)}) %collective-permute-start.3) | collective-permute-done | bytes 1048608 | tf_op jit(solution)/shard_map/ppermute | solution.py:21
  69.1 3.0 %broadcast_select_fusion = (bf16[256,2048]{1,0:T(8,128)(2,1)}, bf16[768,2048]{1,0:T(8,128)(2,1)}) fusion(bf16[256,2048]{1,0:T(8,128)(2,1)S(1)} %copy-done.6, bf16[256,2048]{1,0:T(8,128)(2,1)} %collective-permute-done.3, pred[]{:T(512)S(6)} %eq.34), kind=kLoop, calls=%fused_computation.68 | loop fusion | flops 524287 | bytes 4194305 | tf_op jit(solution)/shard_map/jit(_where)/select_n | solution.py:185
  72.2 41.4 %collective-permute-done.1 = bf16[256,2048]{1,0:T(8,128)(2,1)} collective-permute-done((bf16[256,2048]{1,0:T(8,128)(2,1)S(1)}, bf16[256,2048]{1,0:T(8,128)(2,1)}, u32[]{:S(2)}, u32[]{:S(2)}) %collective-permute-start.1) | collective-permute-done | bytes 1048608 | tf_op jit(solution)/shard_map/ppermute | solution.py:21
  113.6 2.7 %broadcast_select_fusion.1 = (bf16[256,2048]{1,0:T(8,128)(2,1)}, bf16[768,2048]{1,0:T(8,128)(2,1)S(1)}) fusion(bf16[256,2048]{1,0:T(8,128)(2,1)S(1)} %copy-done.8, bf16[256,2048]{1,0:T(8,128)(2,1)} %collective-permute-done.1, pred[]{:T(512)S(6)} %eq.34), kind=kLoop, calls=%fused_computation.69 | loop fusion | flops 524287 | bytes 4194305 | tf_op jit(solution)/shard_map/jit(_where)/select_n | solution.py:185
  116.3 2.1 copy.309
  118.3 2.0 copy.310
  120.4 2.0 copy.306
  122.4 2.4 %constant_dynamic-update-slice_fusion.4 = bf16[768,2048]{1,0:T(8,128)(2,1)} fusion(bf16[768,2048]{1,0:T(8,128)(2,1)} %get-tuple-element.29, bf16[256,2048]{1,0:T(8,128)(2,1)} %collective-permute-done.4), kind=kLoop, calls=%fused_computation.110 | loop fusion | bytes 2097152
  124.8 2.3 %constant_dynamic-update-slice_fusion.3 = bf16[768,2048]{1,0:T(8,128)(2,1)} fusion(bf16[768,2048]{1,0:T(8,128)(2,1)} %constant_dynamic-update-slice_fusion.4, bf16[256,2048]{1,0:T(8,128)(2,1)} %param.16), kind=kLoop, calls=%fused_computation.109 | loop fusion | bytes 2097152 | tf_op jit(solution)/shard_map/concatenate | solution.py:188
  127.1 3.6 %slice_bitcast_fusion.2 = (bf16[80,8,16,128]{3,1,2,0:T(8,128)(2,1)S(1)}, bf16[80,8,16,128]{3,1,2,0:T(8,128)(2,1)S(1)}) fusion(bf16[768,2048]{1,0:T(8,128)(2,1)} %constant_dynamic-update-slice_fusion.3), kind=kLoop, calls=%fused_computation.14 | loop fusion | bytes 10485760
  135.9 2.3 %copy.318 = bf16[80,8,16,128]{3,2,1,0:T(8,128)(2,1)} copy(bf16[80,8,16,128]{3,1,2,0:T(8,128)(2,1)S(1)} %get-tuple-element.19) | data formatting | bytes 5242880
  139.5 4.0 %fusion.3 = (f32[16,128]{1,0:T(8,128)S(1)}, f32[16,5,128,128]{3,2,1,0:T(8,128)}) fusion(pred[128,5,128]{0,2,1:T(8,128)(4,1)S(1)} %get-tuple-element.37, bf16[128,16,128,1]{0,2,3,1:T(8,128)(2,1)S(1)} %bitcast.196, bf16[5,128,16,128]{3,2,1,0:T(8,128)(2,1)S(1)} %bitcast.179), kind=kOutput, calls=%fused_computation.11 | convolution fusion | flops 339474432 | bytes 8478720 | tf_op jit(solution)/shard_map/thd,kjhd->htkj/dot_general | solution.py:167
  145.9 3.8 %multiply_reduce_fusion.1 = (f32[8,128,128]{2,1,0:T(8,128)S(1)}, f32[8,128,128]{2,1,0:T(8,128)}) fusion(f32[8,8,136,128]{3,2,1,0:T(8,128)} %bitcast.175, f32[8,8]{1,0:T(8,128)S(1)} %get-tuple-element.54, f32[8,8]{1,0:T(8,128)S(1)} %get-tuple-element.55), kind=kLoop, calls=%fused_computation.9 | loop fusion | flops 3932160 | bytes 5243392 | tf_op jit(solution)/shard_map/reduce_sum | solution.py:75
  150.7 3.7 %fusion.1 = f32[16,128]{1,0:T(8,128)S(1)} fusion(f32[16,5,128,128]{3,2,1,0:T(8,128)} %get-tuple-element.57, f32[16,128]{1,0:T(8,128)S(1)} %get-tuple-element.56, pred[128,5,128]{0,2,1:T(8,128)(4,1)S(1)} %get-tuple-element.37), kind=kLoop, calls=%fused_computation.7 | loop fusion | flops 5240832 | bytes 5341184 | tf_op jit(solution)/shard_map/reduce_sum | solution.py:173
  154.7 3.0 %fusion.31 = bf16[128,16,128]{2,0,1:T(8,128)(2,1)S(1)} fusion(f32[16,5,128,128]{3,2,1,0:T(8,128)S(1)} %copy-done.5, f32[16,128]{1,0:T(8,128)S(1)} %fusion, f32[16,128]{1,0:T(8,128)S(1)} %get-tuple-element.58, pred[128,5,128]{0,2,1:T(8,128)(4,1)S(1)} %get-tuple-element.36, bf16[5,128,16,128]{3,2,1,0:T(8,128)(2,1)S(1)} %bitcast.176), kind=kOutput, calls=%fused_computation.49 | convolution fusion | flops 342360064 | bytes 8486912 | tf_op jit(solution)/shard_map/htkj,kjhd->thd/dot_general | solution.py:174
  157.7 2.8 %fusion.34 = bf16[128,16,128]{2,0,1:T(8,128)(2,1)S(1)} fusion(f32[16,5,128,128]{3,2,1,0:T(8,128)S(1)} %bitcast.171, f32[16,128]{1,0:T(8,128)S(1)} %fusion.1, f32[16,128]{1,0:T(8,128)S(1)} %get-tuple-element.56, pred[128,5,128]{0,2,1:T(8,128)(4,1)S(1)} %get-tuple-element.37, bf16[5,128,16,128]{3,2,1,0:T(8,128)(2,1)S(1)} %bitcast.177), kind=kOutput, calls=%fused_computation.50 | convolution fusion | flops 342360064 | bytes 8486912 | tf_op jit(solution)/shard_map/htkj,kjhd->thd/dot_general | solution.py:174
  162.6 4.4 %all-to-all-start = ((bf16[4,64,2048]{2,1,0:T(8,128)(2,1)}), bf16[4,64,2048]{2,1,0:T(8,128)(2,1)S(1)}, u32[]{:S(2)}, u32[]{:S(2)}) async-start(bf16[4,64,2048]{2,1,0:T(8,128)(2,1)} %all_to_all.28), calls=%async_computation | async-start | bytes 2097152 | tf_op jit(solution)/shard_map/all_to_all | solution.py:235
  167.0 2.6 %fusion.22 = f32[128,16,128]{2,0,1:T(8,128)} fusion(f32[128,16,128]{2,0,1:T(8,128)} %convolution_bitcast_fusion.3, bf16[128,16,128]{0,2,1:T(8,128)(2,1)S(1)} %bitcast.185, f32[128,16]{0,1:T(8,128)S(1)} %get-tuple-element.43), kind=kOutput, calls=%fused_computation.42 | convolution fusion | flops 68157440 | bytes 2629632 | tf_op jit(solution)/shard_map/thd,hde->the/dot_general | solution.py:52
  169.7 1.8 convolution_bitcast_fusion.1
  171.5 11.3 %all-to-all-done = bf16[4,64,2048]{2,1,0:T(8,128)(2,1)S(1)} async-done(((bf16[4,64,2048]{2,1,0:T(8,128)(2,1)}), bf16[4,64,2048]{2,1,0:T(8,128)(2,1)S(1)}, u32[]{:S(2)}, u32[]{:S(2)}) %all-to-all-start) | async-done | bytes 1048608 | tf_op jit(solution)/shard_map/all_to_all | solution.py:235
  183.8 2.7 %all-gather.7.cloned.1.call-done = f32[32,136,128]{2,1,0:T(8,128)} async-done(((f32[8,136,128]{2,1,0:T(8,128)}), f32[32,136,128]{2,1,0:T(8,128)}) %all-gather.7.cloned.1.call-update) | async-done | bytes 2228240 | tf_op jit(solution)/shard_map/all_gather | solution.py:113
  187.7 1.9 multiply_reduce_fusion.3
  189.9 1.7 fusion.21
  195.3 19.6 %all_to_all.38 = bf16[4,64,2048]{2,1,0:T(8,128)(2,1)S(1)} all-to-all(bf16[4,64,2048]{2,1,0:T(8,128)(2,1)S(1)} %all_to_all.32), channel_id=1, replica_groups=mesh['cy'=4,'cz'=8,'cc'=2,'head'=4] {'head'}, dimensions={0} | all-to-all | bytes 2097152 | tf_op jit(solution)/shard_map/all_to_all | solution.py:239
  (152 shorter events, 33.4 us)
Async XLA Ops:
  7.2 137.4 %all-gather.5.cloned.1.call-start = ((), (), s32[]{:S(2)}) async-start(), calls=%async_computation.2 | async-start | bytes 5013504 | tf_op jit(solution)/shard_map/all_gather | solution.py:106
  10.3 3.9 %copy-start.13 = (bf16[128,2048]{0,1:T(8,128)(2,1)}, bf16[128,2048]{0,1:T(8,128)(2,1)S(1)}, u32[]{:S(2)}) copy-start(bf16[128,2048]{0,1:T(8,128)(2,1)S(1)} %copy.304) | copy-start | bytes 1572868
  12.1 3.6 %copy-start.15 = (bf16[128,2048]{0,1:T(8,128)(2,1)}, bf16[128,2048]{0,1:T(8,128)(2,1)S(1)}, u32[]{:S(2)}) copy-start(bf16[128,2048]{0,1:T(8,128)(2,1)S(1)} %copy.305) | copy-start | bytes 1572868
  12.3 3.4 %copy-start.20 = (bf16[128,2048]{0,1:T(8,128)(2,1)}, bf16[128,2048]{0,1:T(8,128)(2,1)S(1)}, u32[]{:S(2)}) copy-start(bf16[128,2048]{0,1:T(8,128)(2,1)S(1)} %copy.308) | copy-start | bytes 1572868
  12.6 3.2 %copy-start.22 = (bf16[128,2048]{0,1:T(8,128)(2,1)}, bf16[128,2048]{0,1:T(8,128)(2,1)S(1)}, u32[]{:S(2)}) copy-start(bf16[128,2048]{0,1:T(8,128)(2,1)S(1)} %copy.307) | copy-start | bytes 1572868
  15.9 3.0 %collective-permute-start = (f32[16,136,128]{2,1,0:T(8,128)S(1)}, f32[16,136,128]{2,1,0:T(8,128)}, u32[]{:S(2)}, u32[]{:S(2)}) collective-permute-start(f32[16,136,128]{2,1,0:T(8,128)S(1)} %pad_maximum_fusion), channel_id=1, source_target_pairs={{0,4},{4,0},{1,5},{5,1},{2,6},{6,2},{3,7},{7,3},{8,12},{12,8},{9,1... | collective-permute-start | bytes 3342344 | tf_op jit(solution)/shard_map/ppermute | solution.py:84
  20.0 3.5 %copy-start.6 = (bf16[256,2048]{1,0:T(8,128)(2,1)S(1)}, bf16[256,2048]{1,0:T(8,128)(2,1)}, u32[]{:S(2)}) copy-start(bf16[256,2048]{1,0:T(8,128)(2,1)} %param.16) | copy-start | bytes 3145732
  20.0 7.5 %copy-start.7 = (bf16[256,2048]{1,0:T(8,128)(2,1)S(1)}, bf16[256,2048]{1,0:T(8,128)(2,1)}, u32[]{:S(2)}) copy-start(bf16[256,2048]{1,0:T(8,128)(2,1)} %param.17) | copy-start | bytes 3145732
  20.0 11.4 %copy-start.29 = (s32[2]{0:T(128)S(1)}, s32[2]{0:T(128)}, u32[]{:S(2)}) copy-start(s32[2]{0:T(128)} %param.19) | copy-start | bytes 28
  20.0 13.4 %copy-start.30 = (s32[2,5]{1,0:T(2,128)S(1)}, s32[2,5]{1,0:T(2,128)}, u32[]{:S(2)}) copy-start(s32[2,5]{1,0:T(2,128)} %param.18) | copy-start | bytes 124
  23.5 17.1 %copy-start.14 = (bf16[128,2048]{0,1:T(8,128)(2,1)S(1)}, bf16[128,2048]{0,1:T(8,128)(2,1)}, u32[]{:S(2)}) copy-start(bf16[128,2048]{0,1:T(8,128)(2,1)} %copy-done.13) | copy-start | bytes 1572868
  23.5 17.1 %copy-start.16 = (bf16[128,2048]{0,1:T(8,128)(2,1)S(1)}, bf16[128,2048]{0,1:T(8,128)(2,1)}, u32[]{:S(2)}) copy-start(bf16[128,2048]{0,1:T(8,128)(2,1)} %copy-done.15) | copy-start | bytes 1572868
  23.5 163.0 %all-gather.7.cloned.1.call-start = ((), (), s32[]{:S(2)}) async-start(), calls=%async_computation.3 | async-start | bytes 2785280 | tf_op jit(solution)/shard_map/all_gather | solution.py:113
  23.5 45.6 %collective-permute-start.3 = (bf16[256,2048]{1,0:T(8,128)(2,1)S(1)}, bf16[256,2048]{1,0:T(8,128)(2,1)}, u32[]{:S(2)}, u32[]{:S(2)}) collective-permute-start(bf16[256,2048]{1,0:T(8,128)(2,1)S(1)} %copy-done.6), channel_id=1, source_target_pairs={{0,8},{4,12},{8,16},{12,20},{16,24},{20,28},{24,32},{28,36},{32,40... | collective-permute-start | bytes 3145736 | tf_op jit(solution)/shard_map/ppermute | solution.py:21
  27.5 86.1 %collective-permute-start.1 = (bf16[256,2048]{1,0:T(8,128)(2,1)S(1)}, bf16[256,2048]{1,0:T(8,128)(2,1)}, u32[]{:S(2)}, u32[]{:S(2)}) collective-permute-start(bf16[256,2048]{1,0:T(8,128)(2,1)S(1)} %copy-done.7), channel_id=1, source_target_pairs={{0,8},{4,12},{8,16},{12,20},{16,24},{20,28},{24,32},{28,36},{32,40... | collective-permute-start | bytes 3145736 | tf_op jit(solution)/shard_map/ppermute | solution.py:21
  43.4 70.2 %copy-start.8 = (bf16[256,2048]{1,0:T(8,128)(2,1)S(1)}, bf16[256,2048]{1,0:T(8,128)(2,1)}, u32[]{:S(2)}) copy-start(bf16[256,2048]{1,0:T(8,128)(2,1)} %param.17) | copy-start | bytes 3145732
  72.1 50.3 %collective-permute-start.4 = (bf16[256,2048]{1,0:T(8,128)(2,1)}, bf16[256,2048]{1,0:T(8,128)(2,1)}, u32[]{:S(2)}, u32[]{:S(2)}) collective-permute-start(bf16[256,2048]{1,0:T(8,128)(2,1)} %get-tuple-element.28), channel_id=1, source_target_pairs={{0,4},{4,0},{1,5},{5,1},{2,6},{6,2},{3,7},{7,3},{8,12},{12,8},{9,1... | collective-permute-start | bytes 3145736 | tf_op jit(solution)/shard_map/ppermute | solution.py:84
  116.3 15.3 %collective-permute-start.2 = (bf16[256,2048]{1,0:T(8,128)(2,1)}, bf16[256,2048]{1,0:T(8,128)(2,1)}, u32[]{:S(2)}, u32[]{:S(2)}) collective-permute-start(bf16[256,2048]{1,0:T(8,128)(2,1)} %get-tuple-element.26), channel_id=1, source_target_pairs={{0,4},{4,0},{1,5},{5,1},{2,6},{6,2},{3,7},{7,3},{8,12},{12,8},{9,1... | collective-permute-start | bytes 3145736 | tf_op jit(solution)/shard_map/ppermute | solution.py:84
  139.5 4.0 %copy-start.4 = (f32[16,5,128,128]{3,2,1,0:T(8,128)}, f32[16,5,128,128]{3,2,1,0:T(8,128)S(1)}, u32[]{:S(2)}) copy-start(f32[16,5,128,128]{3,2,1,0:T(8,128)S(1)} %get-tuple-element.59) | copy-start | bytes 15728644
  150.6 4.0 %copy-start.5 = (f32[16,5,128,128]{3,2,1,0:T(8,128)S(1)}, f32[16,5,128,128]{3,2,1,0:T(8,128)}, u32[]{:S(2)}) copy-start(f32[16,5,128,128]{3,2,1,0:T(8,128)} %copy-done.4) | copy-start | bytes 15728644
  150.6 7.1 %slice-start = ((s8[5242880]{0:T(1024)(128)(4,1)}), s8[4194304]{0:T(1024)(128)(4,1)S(1)}, s32[]{:S(2)}) async-start(s8[5242880]{0:T(1024)(128)(4,1)} %bitcast.170), calls=%async_computation.4 | async-start | bytes 8388608
  154.7 3.0 %slice-start.1 = ((s8[5242880]{0:T(1024)(128)(4,1)}), s8[1048576]{0:T(1024)(128)(4,1)S(1)}, s32[]{:S(2)}) async-start(s8[5242880]{0:T(1024)(128)(4,1)} %bitcast.170), calls=%async_computation.5 | async-start | bytes 2097152
  154.7 3.0 %copy-start.10 = (bf16[80,8,16,128]{3,2,1,0:T(8,128)(2,1)S(1)}, bf16[80,8,16,128]{3,2,1,0:T(8,128)(2,1)}, u32[]{:S(2)}) copy-start(bf16[80,8,16,128]{3,2,1,0:T(8,128)(2,1)} %copy.318) | copy-start | bytes 7864324
  160.6 6.4 %copy-start.17 = (bf16[128,2048]{0,1:T(8,128)(2,1)S(1)}, bf16[128,2048]{0,1:T(8,128)(2,1)}, u32[]{:S(2)}) copy-start(bf16[128,2048]{0,1:T(8,128)(2,1)} %copy.303) | copy-start | bytes 1572868
  161.3 8.3 %copy-start.18 = (bf16[128,2048]{0,1:T(8,128)(2,1)S(1)}, bf16[128,2048]{0,1:T(8,128)(2,1)}, u32[]{:S(2)}) copy-start(bf16[128,2048]{0,1:T(8,128)(2,1)} %copy.306) | copy-start | bytes 1572868
  162.6 7.1 %copy-start.21 = (bf16[128,2048]{0,1:T(8,128)(2,1)S(1)}, bf16[128,2048]{0,1:T(8,128)(2,1)}, u32[]{:S(2)}) copy-start(bf16[128,2048]{0,1:T(8,128)(2,1)} %copy-done.20) | copy-start | bytes 1572868
  162.6 7.1 %copy-start.23 = (bf16[128,2048]{0,1:T(8,128)(2,1)S(1)}, bf16[128,2048]{0,1:T(8,128)(2,1)}, u32[]{:S(2)}) copy-start(bf16[128,2048]{0,1:T(8,128)(2,1)} %copy-done.22) | copy-start | bytes 1572868
  162.6 20.2 %all-to-all-start = ((bf16[4,64,2048]{2,1,0:T(8,128)(2,1)}), bf16[4,64,2048]{2,1,0:T(8,128)(2,1)S(1)}, u32[]{:S(2)}, u32[]{:S(2)}) async-start(bf16[4,64,2048]{2,1,0:T(8,128)(2,1)} %all_to_all.28), calls=%async_computation | async-start | bytes 2097152 | tf_op jit(solution)/shard_map/all_to_all | solution.py:235
  169.7 20.0 %copy-start.19 = (f32[8,128,128]{2,1,0:T(8,128)S(1)}, f32[8,128,128]{2,1,0:T(8,128)}, u32[]{:S(2)}) copy-start(f32[8,128,128]{2,1,0:T(8,128)} %get-tuple-element.7) | copy-start | bytes 1572868
  182.8 7.1 %copy-start.3 = (f32[16,128,128]{2,1,0:T(8,128)S(1)}, f32[16,128,128]{2,1,0:T(8,128)}, u32[]{:S(2)}) copy-start(f32[16,128,128]{2,1,0:T(8,128)} %copy-done.2) | copy-start | bytes 3145732
  189.8 2.0 collective-permute-start.5
  194.1 21.8 %copy-start.1 = (f32[16,256]{1,0:T(8,128)S(1)}, f32[16,256]{1,0:T(8,128)}, u32[]{:S(2)}) copy-start(f32[16,256]{1,0:T(8,128)} %param.13) | copy-start | bytes 49156
  (10 other events, 16.5 us)
Sparse Core Ops, SparseCore 0:
  23.6 96.1 all-gather.4
  150.8 35.6 all-gather.6

commit v10 on v8

--- a/solution.py
+++ b/solution.py
@@ -123,9 +123,9 @@
     before_factor = spanned(row_factors, row)
     total = folded(row_states, row_factors, count)
     total_factor = spanned(row_factors, count)
-    column_packed = lax.all_gather(narrow(total, total_factor), "cy")
+    column_packed = lax.all_gather(packed(total, total_factor), "cy")
     column_packed, held = lax.optimization_barrier((column_packed, held))
-    column_states, column_factors = widened(column_packed, width)
+    column_states, column_factors = unpacked(column_packed, width)
     above = folded(column_states, column_factors, column)
     prefix_half = before_factor[:, None, None] * above + before
     other_half = swapped(prefix_half)

time: 177 us -> 167 us (0.944)
  waiting for transfers between devices: 42.6 us -> 30.5 us
  other arithmetic: 24.1 us -> 26.7 us
    all_gather x1, waiting for transfers between devices: 17.8 us -> 0.02 us  [carry_in(): lax.all_gather(narrow(chip_state, chip_factor), 'cz')]
    all_to_all x1, waiting for transfers between devices: 6.54 us -> 11.4 us  [local(): lax.all_to_all(softmax_heads, 'head', split_axis=0, concat_axis=1, tiled=...]
    dot_general x2, matrix products: 8.73 us -> 5.81 us  [attend(): jnp.einsum('htkj,kjhd->thd', weights, values_sel, preferred_element_type=...]
    dot_general x2, matrix products: 2.63 us -> 5.28 us  [attend(): jnp.einsum('thd,kjhd->htkj', query_blk, keys_sel, preferred_element_type=...]
    reduce_sum x2, other arithmetic: 2.17 us -> 4.8 us  [attend(): jnp.sum(raised, axis=(2, 3), keepdims=True)]
    unnamed x64 -> x78, local copies, waits for them, and re-layouts: 24.3 us -> 22.4 us
    convert_element_type x2 -> x1, other arithmetic: 3.86 us -> 2.08 us  [widened(): wide = both.astype(jnp.float32)]
  transfers between devices with their start and end apart: 9 -> 9, of which waited for: 4 -> 5; matrix products, arithmetic and copies ran while one was open for 41% -> 43% of each run, Pallas kernels for 0% -> 0%
where the time goes in v10:
time: 167 us; the launch traced here: 165 us
  local copies, waits for them, and re-layouts  38.7 us (23%)
  waiting for transfers between devices  30.5 us (18%)
  other arithmetic  26.7 us (16%)
  matrix products  22.5 us (13%)
  blocking collectives  19.6 us (12%)
  between operations  14.8 us (9%)
  starting transfers between devices  12.3 us (7%)
    unnamed x78, local copies, waits for them, and re-layouts  22.4 us
    all_to_all x1, blocking collectives, local(): lax.all_to_all(linear_heads, 'head', split_axis=0, concat_axis=1, tiled=T...  19.6 us
    ppermute x2, waiting for transfers between devices, passed_along(): return lax.ppermute(block, axis, route)  18.2 us
    all_to_all x1, waiting for transfers between devices, local(): lax.all_to_all(softmax_heads, 'head', split_axis=0, concat_axis=1, tiled=...  11.4 us
    ppermute x2, starting transfers between devices, passed_along(): return lax.ppermute(block, axis, route)  7.66 us
    select_n x2, other arithmetic, softmax_layer(): jnp.where(on_first, own, far)  6.47 us
    dot_general x2, matrix products, attend(): jnp.einsum('htkj,kjhd->thd', weights, values_sel, preferred_element_type=...  5.81 us
    dot_general x2, matrix products, attend(): jnp.einsum('thd,kjhd->htkj', query_blk, keys_sel, preferred_element_type=...  5.28 us
  transfers between devices with their start and end apart: 9, of which 5 were waited for; matrix products, arithmetic and copies ran while one was open for 43% of the time, Pallas kernels for 0%

profile of v10, /device:TPU:8, one launch (start us, length us, event | category | flops | bytes accessed | tf_op | source)
XLA Modules:
  0.0 165.1 jit_solution(5718634528231044774)
XLA Ops:
  7.2 3.8 %collective-permute-start.3 = (bf16[256,2048]{1,0:T(8,128)(2,1)}, bf16[256,2048]{1,0:T(8,128)(2,1)}, u32[]{:S(2)}, u32[]{:S(2)}) collective-permute-start(bf16[256,2048]{1,0:T(8,128)(2,1)} %param.16), channel_id=1, source_target_pairs={{0,8},{4,12},{8,16},{12,20},{16,24},{20,28},{24,32},{28,36},{32,40... | collective-permute-start | bytes 3145736 | tf_op jit(solution)/shard_map/ppermute | solution.py:21
  11.1 3.8 %collective-permute-start.1 = (bf16[256,2048]{1,0:T(8,128)(2,1)}, bf16[256,2048]{1,0:T(8,128)(2,1)}, u32[]{:S(2)}, u32[]{:S(2)}) collective-permute-start(bf16[256,2048]{1,0:T(8,128)(2,1)} %param.17), channel_id=1, source_target_pairs={{0,8},{4,12},{8,16},{12,20},{16,24},{20,28},{24,32},{28,36},{32,40... | collective-permute-start | bytes 3145736 | tf_op jit(solution)/shard_map/ppermute | solution.py:21
  25.7 2.3 %fusion.83 = (bf16[128,2048]{1,0:T(8,128)(2,1)}, bf16[128,2048]{1,0:T(8,128)(2,1)}) fusion(bf16[256,2048]{1,0:T(8,128)(2,1)} %param.10), kind=kLoop, calls=%fused_computation.168 | loop fusion | bytes 2097152 | tf_op jit(solution)/shard_map/slice | solution.py:161
  28.0 1.4 copy.307
  29.9 2.8 %convolution_bitcast_fusion.3 = f32[128,16,128]{2,0,1:T(8,128)} fusion(bf16[128,16,128]{0,2,1:T(8,128)(2,1)} %bitcast.187, bf16[128,16,128]{0,2,1:T(8,128)(2,1)S(1)} %bitcast.180, bf16[128,16,128]{0,2,1:T(8,128)(2,1)S(1)} %bitcast.185, f32[16,128]{1,0:T(8,128)S(1)} %get-tuple-element.44, pred[128,128]{1,0:T(8,128)(4,1)S(1)} %iota_compare_fusion), kind=kOutput, calls=%fused_computation.43 | convolution fusion | flops 135528448 | bytes 2646016 | tf_op jit(solution)/shard_map/htj,jhd->thd/dot_general | solution.py:48
  32.7 2.3 %fusion.82 = (bf16[128,2048]{1,0:T(8,128)(2,1)}, bf16[128,2048]{1,0:T(8,128)(2,1)}) fusion(bf16[256,2048]{1,0:T(8,128)(2,1)} %param.15), kind=kLoop, calls=%fused_computation.167 | loop fusion | bytes 2097152 | tf_op jit(solution)/shard_map/slice | solution.py:222
  35.0 4.2 %collective-permute-done.3 = bf16[256,2048]{1,0:T(8,128)(2,1)} collective-permute-done((bf16[256,2048]{1,0:T(8,128)(2,1)}, bf16[256,2048]{1,0:T(8,128)(2,1)}, u32[]{:S(2)}, u32[]{:S(2)}) %collective-permute-start.3) | collective-permute-done | bytes 1048608 | tf_op jit(solution)/shard_map/ppermute | solution.py:21
  39.2 3.1 %broadcast_select_fusion = (bf16[256,2048]{1,0:T(8,128)(2,1)}, bf16[768,2048]{1,0:T(8,128)(2,1)}) fusion(bf16[256,2048]{1,0:T(8,128)(2,1)S(1)} %copy-done.8, bf16[256,2048]{1,0:T(8,128)(2,1)} %collective-permute-done.3, pred[]{:T(512)S(6)} %eq.34), kind=kLoop, calls=%fused_computation.68 | loop fusion | flops 524287 | bytes 4194305 | tf_op jit(solution)/shard_map/jit(_where)/select_n | solution.py:198
  43.4 1.4 fusion.81
  46.8 14.1 %collective-permute-done.1 = bf16[256,2048]{1,0:T(8,128)(2,1)} collective-permute-done((bf16[256,2048]{1,0:T(8,128)(2,1)}, bf16[256,2048]{1,0:T(8,128)(2,1)}, u32[]{:S(2)}, u32[]{:S(2)}) %collective-permute-start.1) | collective-permute-done | bytes 1048608 | tf_op jit(solution)/shard_map/ppermute | solution.py:21
  60.8 3.4 %broadcast_select_fusion.1 = (bf16[256,2048]{1,0:T(8,128)(2,1)}, bf16[768,2048]{1,0:T(8,128)(2,1)}) fusion(bf16[256,2048]{1,0:T(8,128)(2,1)} %param.17, bf16[256,2048]{1,0:T(8,128)(2,1)} %collective-permute-done.1, pred[]{:T(512)S(6)} %eq.34), kind=kLoop, calls=%fused_computation.69 | loop fusion | flops 524287 | bytes 4194305 | tf_op jit(solution)/shard_map/jit(_where)/select_n | solution.py:198
  64.2 2.1 %copy.313 = bf16[128,2048]{0,1:T(8,128)(2,1)} copy(bf16[128,2048]{1,0:T(8,128)(2,1)} %get-tuple-element.22) | data formatting | bytes 1048576
  66.3 2.1 %copy.314 = bf16[128,2048]{0,1:T(8,128)(2,1)} copy(bf16[128,2048]{1,0:T(8,128)(2,1)} %get-tuple-element.23) | data formatting | bytes 1048576
  68.4 2.1 %copy.310 = bf16[128,2048]{0,1:T(8,128)(2,1)} copy(bf16[128,2048]{1,0:T(8,128)(2,1)} %get-tuple-element.29) | data formatting | bytes 1048576
  76.2 1.3 constant_dynamic-update-slice_fusion.1
  77.6 1.8 %slice_bitcast_fusion.3 = (bf16[80,8,16,128]{3,1,2,0:T(8,128)(2,1)S(1)}, bf16[80,8,16,128]{3,1,2,0:T(8,128)(2,1)S(1)}) fusion(bf16[768,2048]{1,0:T(8,128)(2,1)S(1)} %constant_dynamic-update-slice_fusion), kind=kLoop, calls=%fused_computation.15 | loop fusion | bytes 10485760
  81.1 2.3 %copy.322 = bf16[80,8,16,128]{3,2,1,0:T(8,128)(2,1)} copy(bf16[80,8,16,128]{3,1,2,0:T(8,128)(2,1)S(1)} %get-tuple-element.17) | data formatting | bytes 5242880
  83.5 1.3 fusion.2
  84.8 4.0 %fusion.3 = (f32[16,128]{1,0:T(8,128)S(1)}, f32[16,5,128,128]{3,2,1,0:T(8,128)}) fusion(pred[128,5,128]{0,2,1:T(8,128)(4,1)S(1)} %get-tuple-element.35, bf16[128,16,128,1]{0,2,3,1:T(8,128)(2,1)S(1)} %bitcast.196, bf16[5,128,16,128]{3,2,1,0:T(8,128)(2,1)S(1)} %bitcast.179), kind=kOutput, calls=%fused_computation.11 | convolution fusion | flops 339474432 | bytes 8478720 | tf_op jit(solution)/shard_map/thd,kjhd->htkj/dot_general | solution.py:180
  89.9 2.1 %bitcast_convert_fusion = f32[8,8,144,128]{3,2,1,0:T(8,128)S(1)} fusion(bf16[64,144,128]{2,1,0:T(8,128)(2,1)} %all-gather.5.cloned.1.call-done), kind=kLoop, calls=%fused_computation.154 | loop fusion | flops 1179648 | bytes 7077888 | tf_op jit(solution)/shard_map/convert_element_type | solution.py:79
  92.4 1.5 multiply_reduce_fusion.1
  94.9 3.7 %fusion.1 = f32[16,128]{1,0:T(8,128)S(1)} fusion(f32[16,5,128,128]{3,2,1,0:T(8,128)} %get-tuple-element.58, f32[16,128]{1,0:T(8,128)S(1)} %get-tuple-element.57, pred[128,5,128]{0,2,1:T(8,128)(4,1)S(1)} %get-tuple-element.35), kind=kLoop, calls=%fused_computation.7 | loop fusion | flops 5240832 | bytes 5341184 | tf_op jit(solution)/shard_map/reduce_sum | solution.py:186
  98.9 3.0 %fusion.31 = bf16[128,16,128]{2,0,1:T(8,128)(2,1)S(1)} fusion(f32[16,5,128,128]{3,2,1,0:T(8,128)S(1)} %copy-done.7, f32[16,128]{1,0:T(8,128)S(1)} %fusion, f32[16,128]{1,0:T(8,128)S(1)} %get-tuple-element.59, pred[128,5,128]{0,2,1:T(8,128)(4,1)S(1)} %get-tuple-element.34, bf16[5,128,16,128]{3,2,1,0:T(8,128)(2,1)S(1)} %bitcast.176), kind=kOutput, calls=%fused_computation.49 | convolution fusion | flops 342360064 | bytes 8486912 | tf_op jit(solution)/shard_map/htkj,kjhd->thd/dot_general | solution.py:187
  101.9 2.8 %fusion.34 = bf16[128,16,128]{2,0,1:T(8,128)(2,1)S(1)} fusion(f32[16,5,128,128]{3,2,1,0:T(8,128)S(1)} %bitcast.173, f32[16,128]{1,0:T(8,128)S(1)} %fusion.1, f32[16,128]{1,0:T(8,128)S(1)} %get-tuple-element.57, pred[128,5,128]{0,2,1:T(8,128)(4,1)S(1)} %get-tuple-element.35, bf16[5,128,16,128]{3,2,1,0:T(8,128)(2,1)S(1)} %bitcast.177), kind=kOutput, calls=%fused_computation.50 | convolution fusion | flops 342360064 | bytes 8486912 | tf_op jit(solution)/shard_map/htkj,kjhd->thd/dot_general | solution.py:187
  106.8 4.4 %all-to-all-start = ((bf16[4,64,2048]{2,1,0:T(8,128)(2,1)}), bf16[4,64,2048]{2,1,0:T(8,128)(2,1)S(1)}, u32[]{:S(2)}, u32[]{:S(2)}) async-start(bf16[4,64,2048]{2,1,0:T(8,128)(2,1)} %all_to_all.28), calls=%async_computation | async-start | bytes 2097152 | tf_op jit(solution)/shard_map/all_to_all | solution.py:248
  111.3 2.6 %fusion.22 = f32[128,16,128]{2,0,1:T(8,128)} fusion(f32[128,16,128]{2,0,1:T(8,128)} %convolution_bitcast_fusion.3, bf16[128,16,128]{0,2,1:T(8,128)(2,1)S(1)} %bitcast.181, f32[128,16]{0,1:T(8,128)S(1)} %get-tuple-element.41), kind=kOutput, calls=%fused_computation.42 | convolution fusion | flops 68157440 | bytes 2629632 | tf_op jit(solution)/shard_map/thd,hde->the/dot_general | solution.py:52
  113.9 1.8 %convolution_bitcast_fusion.1 = f32[128,16,128]{2,0,1:T(8,128)} fusion(bf16[128,16,128]{0,2,1:T(8,128)(2,1)S(1)} %bitcast.189, bf16[128,16,128]{0,2,1:T(8,128)(2,1)S(1)} %bitcast.182, bf16[128,16,128]{0,2,1:T(8,128)(2,1)S(1)} %bitcast.191, f32[16,128]{1,0:T(8,128)S(1)} %get-tuple-element.45, pred[128,128]{1,0:T(8,128)(4,1)S(1)} %iota_compare_fusion), kind=kOutput, calls=%fused_computation.39 | convolution fusion | flops 135528448 | bytes 2646016 | tf_op jit(solution)/shard_map/htj,jhd->thd/dot_general | solution.py:48
  115.6 11.4 %all-to-all-done = bf16[4,64,2048]{2,1,0:T(8,128)(2,1)S(1)} async-done(((bf16[4,64,2048]{2,1,0:T(8,128)(2,1)}), bf16[4,64,2048]{2,1,0:T(8,128)(2,1)S(1)}, u32[]{:S(2)}, u32[]{:S(2)}) %all-to-all-start) | async-done | bytes 1048608 | tf_op jit(solution)/shard_map/all_to_all | solution.py:248
  130.0 1.9 %multiply_reduce_fusion.3 = f32[8,128,128]{2,1,0:T(8,128)S(1)} fusion(f32[4,8,136,128]{3,2,1,0:T(8,128)} %bitcast.193, f32[4,8]{1,0:T(4,128)S(1)} %broadcast_select_fusion.6), kind=kLoop, calls=%fused_computation.32 | loop fusion | flops 917504 | bytes 2621568 | tf_op jit(solution)/shard_map/reduce_sum | solution.py:88
  132.3 1.7 %fusion.21 = f32[128,16,128]{2,0,1:T(8,128)S(1)} fusion(f32[128,16,128]{2,0,1:T(8,128)} %convolution_bitcast_fusion.1, bf16[128,16,128]{0,2,1:T(8,128)(2,1)S(1)} %bitcast.183, f32[128,16]{0,1:T(8,128)S(1)} %get-tuple-element.39, f32[16,128,128]{2,1,0:T(8,128)S(1)} %copy-done.5), kind=kOutput, calls=%fused_computation.37 | convolution fusion | flops 68419584 | bytes 3678208 | tf_op jit(solution)/shard_map/thd,hde->the/dot_general | solution.py:52
  134.1 1.5 multiply_reduce_fusion.2
  137.6 19.6 %all_to_all.38 = bf16[4,64,2048]{2,1,0:T(8,128)(2,1)S(1)} all-to-all(bf16[4,64,2048]{2,1,0:T(8,128)(2,1)S(1)} %all_to_all.32), channel_id=1, replica_groups=mesh['cy'=4,'cz'=8,'cc'=2,'head'=4] {'head'}, dimensions={0} | all-to-all | bytes 2097152 | tf_op jit(solution)/shard_map/all_to_all | solution.py:252
  (150 shorter events, 32.8 us)
Async XLA Ops:
  7.2 7.7 %copy-start = (f32[16,256]{1,0:T(8,128)S(1)}, f32[16,256]{1,0:T(8,128)}, u32[]{:S(2)}) copy-start(f32[16,256]{1,0:T(8,128)} %param.13) | copy-start | bytes 49156
  7.2 82.7 %all-gather.5.cloned.1.call-start = ((), (), s32[]{:S(2)}) async-start(), calls=%async_computation.2 | async-start | bytes 2654208 | tf_op jit(solution)/shard_map/all_gather | solution.py:119
  7.2 31.9 %collective-permute-start.3 = (bf16[256,2048]{1,0:T(8,128)(2,1)}, bf16[256,2048]{1,0:T(8,128)(2,1)}, u32[]{:S(2)}, u32[]{:S(2)}) collective-permute-start(bf16[256,2048]{1,0:T(8,128)(2,1)} %param.16), channel_id=1, source_target_pairs={{0,8},{4,12},{8,16},{12,20},{16,24},{20,28},{24,32},{28,36},{32,40... | collective-permute-start | bytes 3145736 | tf_op jit(solution)/shard_map/ppermute | solution.py:21
  11.1 49.8 %collective-permute-start.1 = (bf16[256,2048]{1,0:T(8,128)(2,1)}, bf16[256,2048]{1,0:T(8,128)(2,1)}, u32[]{:S(2)}, u32[]{:S(2)}) collective-permute-start(bf16[256,2048]{1,0:T(8,128)(2,1)} %param.17), channel_id=1, source_target_pairs={{0,8},{4,12},{8,16},{12,20},{16,24},{20,28},{24,32},{28,36},{32,40... | collective-permute-start | bytes 3145736 | tf_op jit(solution)/shard_map/ppermute | solution.py:21
  18.9 2.2 %copy-start.16 = (bf16[128,2048]{0,1:T(8,128)(2,1)}, bf16[128,2048]{0,1:T(8,128)(2,1)S(1)}, u32[]{:S(2)}) copy-start(bf16[128,2048]{0,1:T(8,128)(2,1)S(1)} %copy.309) | copy-start | bytes 1572868
  19.2 3.3 %copy-start.18 = (bf16[128,2048]{0,1:T(8,128)(2,1)}, bf16[128,2048]{0,1:T(8,128)(2,1)S(1)}, u32[]{:S(2)}) copy-start(bf16[128,2048]{0,1:T(8,128)(2,1)S(1)} %copy.312) | copy-start | bytes 1572868
  19.5 4.2 %copy-start.20 = (bf16[128,2048]{0,1:T(8,128)(2,1)}, bf16[128,2048]{0,1:T(8,128)(2,1)S(1)}, u32[]{:S(2)}) copy-start(bf16[128,2048]{0,1:T(8,128)(2,1)S(1)} %copy.311) | copy-start | bytes 1572868
  21.1 2.8 %copy-start.27 = (s32[2]{0:T(128)S(1)}, s32[2]{0:T(128)}, u32[]{:S(2)}) copy-start(s32[2]{0:T(128)} %param.19) | copy-start | bytes 28
  21.1 4.5 %copy-start.28 = (s32[2,5]{1,0:T(2,128)S(1)}, s32[2,5]{1,0:T(2,128)}, u32[]{:S(2)}) copy-start(s32[2,5]{1,0:T(2,128)} %param.18) | copy-start | bytes 124
  23.7 18.5 %collective-permute-start = (f32[16,136,128]{2,1,0:T(8,128)}, f32[16,136,128]{2,1,0:T(8,128)}, u32[]{:S(2)}, u32[]{:S(2)}) collective-permute-start(f32[16,136,128]{2,1,0:T(8,128)} %pad_maximum_fusion), channel_id=1, source_target_pairs={{0,4},{4,0},{1,5},{5,1},{2,6},{6,2},{3,7},{7,3},{8,12},{12,8},{9,1... | collective-permute-start | bytes 3342344 | tf_op jit(solution)/shard_map/ppermute | solution.py:97
  28.0 11.1 %copy-start.8 = (bf16[256,2048]{1,0:T(8,128)(2,1)S(1)}, bf16[256,2048]{1,0:T(8,128)(2,1)}, u32[]{:S(2)}) copy-start(bf16[256,2048]{1,0:T(8,128)(2,1)} %param.16) | copy-start | bytes 3145732
  29.4 12.8 %copy-start.13 = (bf16[128,2048]{0,1:T(8,128)(2,1)}, bf16[128,2048]{0,1:T(8,128)(2,1)S(1)}, u32[]{:S(2)}) copy-start(bf16[128,2048]{0,1:T(8,128)(2,1)S(1)} %copy.307) | copy-start | bytes 1572868
  42.2 28.2 %collective-permute-start.4 = (bf16[256,2048]{1,0:T(8,128)(2,1)}, bf16[256,2048]{1,0:T(8,128)(2,1)}, u32[]{:S(2)}, u32[]{:S(2)}) collective-permute-start(bf16[256,2048]{1,0:T(8,128)(2,1)} %get-tuple-element.26), channel_id=1, source_target_pairs={{0,4},{4,0},{1,5},{5,1},{2,6},{6,2},{3,7},{7,3},{8,12},{12,8},{9,1... | collective-permute-start | bytes 3145736 | tf_op jit(solution)/shard_map/ppermute | solution.py:97
  46.7 82.1 %all-gather.7.cloned.1.call-start = ((), (), s32[]{:S(2)}) async-start(), calls=%async_computation.3 | async-start | bytes 2785280 | tf_op jit(solution)/shard_map/all_gather | solution.py:126
  46.8 23.7 %copy-start.2 = (bf16[768,2048]{1,0:T(8,128)(2,1)S(1)}, bf16[768,2048]{1,0:T(8,128)(2,1)}, u32[]{:S(2)}) copy-start(bf16[768,2048]{1,0:T(8,128)(2,1)} %get-tuple-element.27) | copy-start | bytes 9437188
  64.2 10.9 %collective-permute-start.2 = (bf16[256,2048]{1,0:T(8,128)(2,1)}, bf16[256,2048]{1,0:T(8,128)(2,1)}, u32[]{:S(2)}, u32[]{:S(2)}) collective-permute-start(bf16[256,2048]{1,0:T(8,128)(2,1)} %get-tuple-element.24), channel_id=1, source_target_pairs={{0,4},{4,0},{1,5},{5,1},{2,6},{6,2},{3,7},{7,3},{8,12},{12,8},{9,1... | collective-permute-start | bytes 3145736 | tf_op jit(solution)/shard_map/ppermute | solution.py:97
  74.3 3.2 %copy-start.9 = (bf16[256,2048]{1,0:T(8,128)(2,1)S(1)}, bf16[256,2048]{1,0:T(8,128)(2,1)}, u32[]{:S(2)}) copy-start(bf16[256,2048]{1,0:T(8,128)(2,1)} %param.17) | copy-start | bytes 3145732
  81.1 2.4 %copy-start.25 = (bf16[128,2048]{0,1:T(8,128)(2,1)S(1)}, bf16[128,2048]{0,1:T(8,128)(2,1)}, u32[]{:S(2)}) copy-start(bf16[128,2048]{0,1:T(8,128)(2,1)} %copy.313) | copy-start | bytes 1572868
  84.8 4.0 %copy-start.6 = (f32[16,5,128,128]{3,2,1,0:T(8,128)}, f32[16,5,128,128]{3,2,1,0:T(8,128)S(1)}, u32[]{:S(2)}) copy-start(f32[16,5,128,128]{3,2,1,0:T(8,128)S(1)} %get-tuple-element.60) | copy-start | bytes 15728644
  94.8 4.0 %copy-start.7 = (f32[16,5,128,128]{3,2,1,0:T(8,128)S(1)}, f32[16,5,128,128]{3,2,1,0:T(8,128)}, u32[]{:S(2)}) copy-start(f32[16,5,128,128]{3,2,1,0:T(8,128)} %copy-done.6) | copy-start | bytes 15728644
  94.8 7.1 %slice-start = ((s8[5242880]{0:T(1024)(128)(4,1)}), s8[4194304]{0:T(1024)(128)(4,1)S(1)}, s32[]{:S(2)}) async-start(s8[5242880]{0:T(1024)(128)(4,1)} %bitcast.172), calls=%async_computation.4 | async-start | bytes 8388608
  98.9 3.0 %slice-start.1 = ((s8[5242880]{0:T(1024)(128)(4,1)}), s8[1048576]{0:T(1024)(128)(4,1)S(1)}, s32[]{:S(2)}) async-start(s8[5242880]{0:T(1024)(128)(4,1)} %bitcast.172), calls=%async_computation.5 | async-start | bytes 2097152
  98.9 3.0 %copy-start.10 = (bf16[80,8,16,128]{3,2,1,0:T(8,128)(2,1)S(1)}, bf16[80,8,16,128]{3,2,1,0:T(8,128)(2,1)}, u32[]{:S(2)}) copy-start(bf16[80,8,16,128]{3,2,1,0:T(8,128)(2,1)} %copy.322) | copy-start | bytes 7864324
  104.8 6.4 %copy-start.14 = (bf16[128,2048]{0,1:T(8,128)(2,1)S(1)}, bf16[128,2048]{0,1:T(8,128)(2,1)}, u32[]{:S(2)}) copy-start(bf16[128,2048]{0,1:T(8,128)(2,1)} %copy-done.13) | copy-start | bytes 1572868
  105.5 8.3 %copy-start.15 = (bf16[128,2048]{0,1:T(8,128)(2,1)S(1)}, bf16[128,2048]{0,1:T(8,128)(2,1)}, u32[]{:S(2)}) copy-start(bf16[128,2048]{0,1:T(8,128)(2,1)} %copy.310) | copy-start | bytes 1572868
  106.8 7.0 %copy-start.19 = (bf16[128,2048]{0,1:T(8,128)(2,1)S(1)}, bf16[128,2048]{0,1:T(8,128)(2,1)}, u32[]{:S(2)}) copy-start(bf16[128,2048]{0,1:T(8,128)(2,1)} %copy-done.18) | copy-start | bytes 1572868
  106.8 7.0 %copy-start.21 = (bf16[128,2048]{0,1:T(8,128)(2,1)S(1)}, bf16[128,2048]{0,1:T(8,128)(2,1)}, u32[]{:S(2)}) copy-start(bf16[128,2048]{0,1:T(8,128)(2,1)} %copy-done.20) | copy-start | bytes 1572868
  106.8 20.2 %all-to-all-start = ((bf16[4,64,2048]{2,1,0:T(8,128)(2,1)}), bf16[4,64,2048]{2,1,0:T(8,128)(2,1)S(1)}, u32[]{:S(2)}, u32[]{:S(2)}) async-start(bf16[4,64,2048]{2,1,0:T(8,128)(2,1)} %all_to_all.28), calls=%async_computation | async-start | bytes 2097152 | tf_op jit(solution)/shard_map/all_to_all | solution.py:248
  113.8 18.1 %copy-start.17 = (f32[8,128,128]{2,1,0:T(8,128)S(1)}, f32[8,128,128]{2,1,0:T(8,128)}, u32[]{:S(2)}) copy-start(f32[8,128,128]{2,1,0:T(8,128)} %get-tuple-element.7) | copy-start | bytes 1572868
  127.0 5.2 %copy-start.5 = (f32[16,128,128]{2,1,0:T(8,128)S(1)}, f32[16,128,128]{2,1,0:T(8,128)}, u32[]{:S(2)}) copy-start(f32[16,128,128]{2,1,0:T(8,128)} %copy-done.4) | copy-start | bytes 3145732
  132.1 2.0 %collective-permute-start.5 = (f32[8,128,128]{2,1,0:T(8,128)S(1)}, f32[8,128,128]{2,1,0:T(8,128)S(1)}, u32[]{:S(2)}, u32[]{:S(2)}) collective-permute-start(f32[8,128,128]{2,1,0:T(8,128)S(1)} %multiply_add_fusion), channel_id=1, source_target_pairs={{0,4},{4,0},{1,5},{5,1},{2,6},{6,2},{3,7},{7,3},{8,12},{12,8},{9,1... | collective-permute-start | bytes 1572872 | tf_op jit(solution)/shard_map/ppermute | solution.py:97
  136.4 21.9 %copy-start.1 = (f32[16,256]{1,0:T(8,128)S(1)}, f32[16,256]{1,0:T(8,128)}, u32[]{:S(2)}) copy-start(f32[16,256]{1,0:T(8,128)} %param.13) | copy-start | bytes 49156
  (8 other events, 13.2 us)
Sparse Core Ops, SparseCore 0:
  46.8 42.2 all-gather.4
  95.0 33.8 all-gather.6

commit v11 on v10

--- a/solution.py
+++ b/solution.py
@@ -80,11 +80,15 @@
     return wide[..., :width, :], wide[..., width, 0] + wide[..., width + 8, 0]
 
 
-def folded(states, factors, upto):
-    places = jnp.arange(states.shape[0])
+def folding_weights(factors, upto):
+    places = jnp.arange(factors.shape[0])
     between = (places[:, None] < places[None, :]) & (places[None, :] < upto)
     weights = jnp.prod(jnp.where(between[:, :, None], factors[None], 1.0), axis=1)
-    weights = jnp.where((places < upto)[:, None], weights, 0.0)
+    return jnp.where((places < upto)[:, None], weights, 0.0)
+
+
+def folded(states, factors, upto):
+    weights = folding_weights(factors, upto)
     return jnp.sum(weights[:, :, None, None] * states, axis=0)
 
 
@@ -123,10 +127,16 @@
     before_factor = spanned(row_factors, row)
     total = folded(row_states, row_factors, count)
     total_factor = spanned(row_factors, count)
-    column_packed = lax.all_gather(packed(total, total_factor), "cy")
-    column_packed, held = lax.optimization_barrier((column_packed, held))
-    column_states, column_factors = unpacked(column_packed, width)
-    above = folded(column_states, column_factors, column)
+    mine = packed(total, total_factor)
+    columns = lax.psum(1, "cy")
+    received = [
+        lax.ppermute(mine, "cy", [(i, i + d) for i in range(columns) if i + d < columns])
+        for d in range(columns - 1, 0, -1)
+    ]
+    received, held = lax.optimization_barrier((received, held))
+    parts = [unpacked(piece, width) for piece in received]
+    weights = folding_weights(jnp.stack([part[1] for part in parts]), columns - 1)
+    above = sum(weight[:, None, None] * part[0] for weight, part in zip(weights, parts))
     prefix_half = before_factor[:, None, None] * above + before
     other_half = swapped(prefix_half)
     prefix = jnp.where(

time: 167 us -> 182 us (1.090)
  waiting for transfers between devices: 30.5 us -> 44.6 us
  starting transfers between devices: 12.3 us -> 20.8 us
  other arithmetic: 26.7 us -> 22.7 us
  matrix products: 22.5 us -> 18.9 us
    ppermute x0 -> x3, waiting for transfers between devices: none -> 15.3 us  [carry_in(): lax.ppermute(mine, 'cy', [(i, i + d) for i in range(columns) if i + d < c...]
    all_to_all x1, waiting for transfers between devices: 11.4 us -> 0.01 us  [local(): lax.all_to_all(softmax_heads, 'head', split_axis=0, concat_axis=1, tiled=...]
    all_gather x1, waiting for transfers between devices: 0.02 us -> 11 us  [carry_in(): lax.all_gather(narrow(chip_state, chip_factor), 'cz')]
    ppermute x0 -> x3, starting transfers between devices: none -> 8.16 us  [carry_in(): lax.ppermute(mine, 'cy', [(i, i + d) for i in range(columns) if i + d < c...]
    reduce_sum x2 -> x1, other arithmetic: 3.38 us -> 0.68 us  [folded(): return jnp.sum(weights[:, :, None, None] * states, axis=0)]
    dot_general x2, matrix products: 5.28 us -> 2.62 us  [attend(): jnp.einsum('thd,kjhd->htkj', query_blk, keys_sel, preferred_element_type=...]
    reduce_sum x2, other arithmetic: 4.8 us -> 2.15 us  [attend(): jnp.sum(raised, axis=(2, 3), keepdims=True)]
    dot_general x2, matrix products: 4.31 us -> 1.75 us  [block_output(): jnp.einsum('thd,hde->the', decayed_query, carried.astype(jnp.bfloat16), p...]
  transfers between devices with their start and end apart: 9 -> 11, of which waited for: 5 -> 5; matrix products, arithmetic and copies ran while one was open for 43% -> 39% of each run, Pallas kernels for 0% -> 0%
where the time goes in v11:
time: 182 us; the launch traced here: 181 us
  waiting for transfers between devices  44.6 us (25%)
  local copies, waits for them, and re-layouts  39.7 us (22%)
  other arithmetic  22.7 us (12%)
  starting transfers between devices  20.8 us (11%)
  blocking collectives  19.4 us (11%)
  matrix products  18.9 us (10%)
  between operations  14.7 us (8%)
    unnamed x62, local copies, waits for them, and re-layouts  21.9 us
    all_to_all x1, blocking collectives, local(): lax.all_to_all(linear_heads, 'head', split_axis=0, concat_axis=1, tiled=T...  19.4 us
    ppermute x2, waiting for transfers between devices, passed_along(): return lax.ppermute(block, axis, route)  16.8 us
    ppermute x3, waiting for transfers between devices, carry_in(): lax.ppermute(mine, 'cy', [(i, i + d) for i in range(columns) if i + d < c...  15.3 us
    all_gather x1, waiting for transfers between devices, carry_in(): lax.all_gather(narrow(chip_state, chip_factor), 'cz')  11 us
    ppermute x3, starting transfers between devices, carry_in(): lax.ppermute(mine, 'cy', [(i, i + d) for i in range(columns) if i + d < c...  8.16 us
    ppermute x2, starting transfers between devices, passed_along(): return lax.ppermute(block, axis, route)  7.66 us
    dot_general x2, matrix products, block_output(): jnp.einsum('htj,jhd->thd', mixing, values_blk, preferred_element_type=jnp...  6.23 us
  transfers between devices with their start and end apart: 11, of which 5 were waited for; matrix products, arithmetic and copies ran while one was open for 39% of the time, Pallas kernels for 0%

profile of v11, /device:TPU:8, one launch (start us, length us, event | category | flops | bytes accessed | tf_op | source)
XLA Modules:
  0.0 180.8 jit_solution(4912455631792399709)
XLA Ops:
  7.2 3.8 %collective-permute-start.6 = (bf16[256,2048]{1,0:T(8,128)(2,1)}, bf16[256,2048]{1,0:T(8,128)(2,1)}, u32[]{:S(2)}, u32[]{:S(2)}) collective-permute-start(bf16[256,2048]{1,0:T(8,128)(2,1)} %param.16), channel_id=1, source_target_pairs={{0,8},{4,12},{8,16},{12,20},{16,24},{20,28},{24,32},{28,36},{32,40... | collective-permute-start | bytes 3145736 | tf_op jit(solution)/shard_map/ppermute | solution.py:21
  11.1 3.8 %collective-permute-start.4 = (bf16[256,2048]{1,0:T(8,128)(2,1)}, bf16[256,2048]{1,0:T(8,128)(2,1)}, u32[]{:S(2)}, u32[]{:S(2)}) collective-permute-start(bf16[256,2048]{1,0:T(8,128)(2,1)} %param.17), channel_id=1, source_target_pairs={{0,8},{4,12},{8,16},{12,20},{16,24},{20,28},{24,32},{28,36},{32,40... | collective-permute-start | bytes 3145736 | tf_op jit(solution)/shard_map/ppermute | solution.py:21
  17.4 1.5 fusion.85
  25.2 2.1 %fusion.83 = (bf16[128,2048]{1,0:T(8,128)(2,1)S(1)}, bf16[128,2048]{1,0:T(8,128)(2,1)}) fusion(bf16[256,2048]{1,0:T(8,128)(2,1)} %param.10), kind=kLoop, calls=%fused_computation.173 | loop fusion | bytes 2097152 | tf_op jit(solution)/shard_map/slice | solution.py:171
  28.7 2.3 %fusion.82 = (bf16[128,2048]{1,0:T(8,128)(2,1)}, bf16[128,2048]{1,0:T(8,128)(2,1)}) fusion(bf16[256,2048]{1,0:T(8,128)(2,1)} %param.15), kind=kLoop, calls=%fused_computation.172 | loop fusion | bytes 2097152 | tf_op jit(solution)/shard_map/slice | solution.py:232
  31.0 3.2 %convolution_bitcast_fusion.3 = f32[128,16,128]{2,0,1:T(8,128)} fusion(bf16[128,16,128]{0,2,1:T(8,128)(2,1)} %bitcast.193, bf16[128,16,128]{0,2,1:T(8,128)(2,1)} %bitcast.188, bf16[128,16,128]{0,2,1:T(8,128)(2,1)} %bitcast.191, f32[16,128]{1,0:T(8,128)S(1)} %get-tuple-element.48, pred[128,128]{1,0:T(8,128)(4,1)S(1)} %iota_compare_fusion), kind=kOutput, calls=%fused_computation.42 | convolution fusion | flops 135528448 | bytes 2646016 | tf_op jit(solution)/shard_map/htj,jhd->thd/dot_general | solution.py:48
  34.3 2.0 %copy.313 = bf16[128,2048]{0,1:T(8,128)(2,1)} copy(bf16[128,2048]{1,0:T(8,128)(2,1)} %get-tuple-element.26) | data formatting | bytes 1048576
  36.3 2.1 %copy.314 = bf16[128,2048]{0,1:T(8,128)(2,1)} copy(bf16[128,2048]{1,0:T(8,128)(2,1)} %get-tuple-element.27) | data formatting | bytes 1048576
  38.4 2.0 %copy.310 = bf16[128,2048]{0,1:T(8,128)(2,1)} copy(bf16[128,2048]{1,0:T(8,128)(2,1)} %get-tuple-element.33) | data formatting | bytes 1048576
  40.4 3.1 %broadcast_select_fusion = (bf16[256,2048]{1,0:T(8,128)(2,1)}, bf16[768,2048]{1,0:T(8,128)(2,1)}) fusion(bf16[256,2048]{1,0:T(8,128)(2,1)S(1)} %copy-done.3, bf16[256,2048]{1,0:T(8,128)(2,1)} %collective-permute-done.6, pred[]{:T(512)S(6)} %eq.34), kind=kLoop, calls=%fused_computation.67 | loop fusion | flops 524287 | bytes 4194305 | tf_op jit(solution)/shard_map/jit(_where)/select_n | solution.py:208
  44.0 16.8 %collective-permute-done.4 = bf16[256,2048]{1,0:T(8,128)(2,1)} collective-permute-done((bf16[256,2048]{1,0:T(8,128)(2,1)}, bf16[256,2048]{1,0:T(8,128)(2,1)}, u32[]{:S(2)}, u32[]{:S(2)}) %collective-permute-start.4) | collective-permute-done | bytes 1048608 | tf_op jit(solution)/shard_map/ppermute | solution.py:21
  60.8 3.0 %broadcast_select_fusion.1 = (bf16[256,2048]{1,0:T(8,128)(2,1)}, bf16[768,2048]{1,0:T(8,128)(2,1)}) fusion(bf16[256,2048]{1,0:T(8,128)(2,1)S(1)} %copy-done.4, bf16[256,2048]{1,0:T(8,128)(2,1)} %collective-permute-done.4, pred[]{:T(512)S(6)} %eq.34), kind=kLoop, calls=%fused_computation.68 | loop fusion | flops 524287 | bytes 4194305 | tf_op jit(solution)/shard_map/jit(_where)/select_n | solution.py:208
  65.0 1.4 fusion.81
  68.3 2.3 %constant_dynamic-update-slice_fusion.4 = bf16[768,2048]{1,0:T(8,128)(2,1)} fusion(bf16[768,2048]{1,0:T(8,128)(2,1)} %get-tuple-element.31, bf16[256,2048]{1,0:T(8,128)(2,1)} %collective-permute-done.7), kind=kLoop, calls=%fused_computation.110 | loop fusion | bytes 2097152
  71.7 3.8 %slice_bitcast_fusion.2 = (bf16[80,8,16,128]{3,1,2,0:T(8,128)(2,1)S(1)}, bf16[80,8,16,128]{3,1,2,0:T(8,128)(2,1)S(1)}) fusion(bf16[768,2048]{1,0:T(8,128)(2,1)} %constant_dynamic-update-slice_fusion.3), kind=kLoop, calls=%fused_computation.14 | loop fusion | bytes 10485760
  75.5 1.3 constant_dynamic-update-slice_fusion.1
  77.0 1.8 slice_bitcast_fusion.3
  87.1 3.0 %fusion.31 = bf16[128,16,128]{2,0,1:T(8,128)(2,1)S(1)} fusion(f32[16,5,128,128]{3,2,1,0:T(8,128)S(1)} %get-tuple-element.67, f32[16,128]{1,0:T(8,128)S(1)} %fusion, f32[16,128]{1,0:T(8,128)S(1)} %get-tuple-element.66, pred[128,5,128]{0,2,1:T(8,128)(4,1)S(1)} %get-tuple-element.38, bf16[5,128,16,128]{3,2,1,0:T(8,128)(2,1)S(1)} %bitcast.182), kind=kOutput, calls=%fused_computation.48 | convolution fusion | flops 342360064 | bytes 8486912 | tf_op jit(solution)/shard_map/htkj,kjhd->thd/dot_general | solution.py:197
  90.1 2.8 %fusion.34 = bf16[128,16,128]{2,0,1:T(8,128)(2,1)S(1)} fusion(f32[16,5,128,128]{3,2,1,0:T(8,128)S(1)} %get-tuple-element.65, f32[16,128]{1,0:T(8,128)S(1)} %fusion.1, f32[16,128]{1,0:T(8,128)S(1)} %get-tuple-element.64, pred[128,5,128]{0,2,1:T(8,128)(4,1)S(1)} %get-tuple-element.39, bf16[5,128,16,128]{3,2,1,0:T(8,128)(2,1)S(1)} %bitcast.183), kind=kOutput, calls=%fused_computation.49 | convolution fusion | flops 342360064 | bytes 8486912 | tf_op jit(solution)/shard_map/htkj,kjhd->thd/dot_general | solution.py:197
  95.0 4.3 %all-to-all-start = ((bf16[4,64,2048]{2,1,0:T(8,128)(2,1)}), bf16[4,64,2048]{2,1,0:T(8,128)(2,1)S(1)}, u32[]{:S(2)}, u32[]{:S(2)}) async-start(bf16[4,64,2048]{2,1,0:T(8,128)(2,1)} %all_to_all.28), calls=%async_computation | async-start | bytes 2097152 | tf_op jit(solution)/shard_map/all_to_all | solution.py:258
  99.3 11.0 %all-gather.3.cloned.1.call-done = bf16[64,144,128]{2,1,0:T(8,128)(2,1)} async-done(((bf16[8,144,128]{2,1,0:T(8,128)(2,1)}), bf16[64,144,128]{2,1,0:T(8,128)(2,1)}) %all-gather.3.cloned.1.call-update) | async-done | bytes 2359312 | tf_op jit(solution)/shard_map/all_gather | solution.py:123
  110.2 2.1 %bitcast_convert_fusion = f32[8,8,144,128]{3,2,1,0:T(8,128)S(1)} fusion(bf16[64,144,128]{2,1,0:T(8,128)(2,1)} %all-gather.3.cloned.1.call-done), kind=kLoop, calls=%fused_computation.159 | loop fusion | flops 1179648 | bytes 7077888 | tf_op jit(solution)/shard_map/convert_element_type | solution.py:79
  114.3 1.5 collective-permute-start.1
  115.8 4.8 %collective-permute-start.2 = (f32[8,136,128]{2,1,0:T(8,128)}, f32[8,136,128]{2,1,0:T(8,128)}, u32[]{:S(2)}, u32[]{:S(2)}) collective-permute-start(f32[8,136,128]{2,1,0:T(8,128)} %pad_maximum_fusion.2), channel_id=1, source_target_pairs={{0,128},{64,192},{1,129},{65,193},{2,130},{66,194},{3,131},{67,195... | collective-permute-start | bytes 1671176 | tf_op jit(solution)/shard_map/ppermute | solution.py:133
  120.6 1.9 %collective-permute-start.3 = (f32[8,136,128]{2,1,0:T(8,128)}, f32[8,136,128]{2,1,0:T(8,128)}, u32[]{:S(2)}, u32[]{:S(2)}) collective-permute-start(f32[8,136,128]{2,1,0:T(8,128)} %pad_maximum_fusion.2), channel_id=1, source_target_pairs={{0,64},{64,128},{128,192},{1,65},{65,129},{129,193},{2,66},{66,130... | collective-permute-start | bytes 1671176 | tf_op jit(solution)/shard_map/ppermute | solution.py:133
  122.5 1.4 fusion.22
  123.9 3.0 %convolution_bitcast_fusion.1 = f32[128,16,128]{2,0,1:T(8,128)} fusion(bf16[128,16,128]{0,2,1:T(8,128)(2,1)} %bitcast.195, bf16[128,16,128]{0,2,1:T(8,128)(2,1)S(1)} %bitcast.186, bf16[128,16,128]{0,2,1:T(8,128)(2,1)} %bitcast.197, f32[16,128]{1,0:T(8,128)S(1)} %get-tuple-element.49, pred[128,128]{1,0:T(8,128)(4,1)S(1)} %iota_compare_fusion), kind=kOutput, calls=%fused_computation.38 | convolution fusion | flops 135528448 | bytes 2646016 | tf_op jit(solution)/shard_map/htj,jhd->thd/dot_general | solution.py:48
  128.9 14.4 %collective-permute-done.3 = f32[8,136,128]{2,1,0:T(8,128)} collective-permute-done((f32[8,136,128]{2,1,0:T(8,128)}, f32[8,136,128]{2,1,0:T(8,128)}, u32[]{:S(2)}, u32[]{:S(2)}) %collective-permute-start.3) | collective-permute-done | bytes 557088 | tf_op jit(solution)/shard_map/ppermute | solution.py:133
  146.2 1.7 multiply_add_fusion
  148.5 1.4 collective-permute-done.8
  149.9 1.6 multiply_reduce_fusion.2
  153.5 19.4 %all_to_all.38 = bf16[4,64,2048]{2,1,0:T(8,128)(2,1)S(1)} all-to-all(bf16[4,64,2048]{2,1,0:T(8,128)(2,1)S(1)} %all_to_all.32), channel_id=1, replica_groups=mesh['cy'=4,'cz'=8,'cc'=2,'head'=4] {'head'}, dimensions={0} | all-to-all | bytes 2097152 | tf_op jit(solution)/shard_map/all_to_all | solution.py:262
  (139 shorter events, 35.4 us)
Async XLA Ops:
  7.2 7.7 %copy-start = (f32[16,256]{1,0:T(8,128)S(1)}, f32[16,256]{1,0:T(8,128)}, u32[]{:S(2)}) copy-start(f32[16,256]{1,0:T(8,128)} %param.13) | copy-start | bytes 49156
  7.2 103.1 %all-gather.3.cloned.1.call-start = ((), (), s32[]{:S(2)}) async-start(), calls=%async_computation.2 | async-start | bytes 2654208 | tf_op jit(solution)/shard_map/all_gather | solution.py:123
  7.2 33.2 %collective-permute-start.6 = (bf16[256,2048]{1,0:T(8,128)(2,1)}, bf16[256,2048]{1,0:T(8,128)(2,1)}, u32[]{:S(2)}, u32[]{:S(2)}) collective-permute-start(bf16[256,2048]{1,0:T(8,128)(2,1)} %param.16), channel_id=1, source_target_pairs={{0,8},{4,12},{8,16},{12,20},{16,24},{20,28},{24,32},{28,36},{32,40... | collective-permute-start | bytes 3145736 | tf_op jit(solution)/shard_map/ppermute | solution.py:21
  11.1 49.8 %collective-permute-start.4 = (bf16[256,2048]{1,0:T(8,128)(2,1)}, bf16[256,2048]{1,0:T(8,128)(2,1)}, u32[]{:S(2)}, u32[]{:S(2)}) collective-permute-start(bf16[256,2048]{1,0:T(8,128)(2,1)} %param.17), channel_id=1, source_target_pairs={{0,8},{4,12},{8,16},{12,20},{16,24},{20,28},{24,32},{28,36},{32,40... | collective-permute-start | bytes 3145736 | tf_op jit(solution)/shard_map/ppermute | solution.py:21
  17.4 3.9 %copy-start.10 = (bf16[128,2048]{0,1:T(8,128)(2,1)}, bf16[128,2048]{0,1:T(8,128)(2,1)S(1)}, u32[]{:S(2)}) copy-start(bf16[128,2048]{0,1:T(8,128)(2,1)S(1)} %copy.308) | copy-start | bytes 1572868
  19.2 2.2 %copy-start.11 = (bf16[128,2048]{0,1:T(8,128)(2,1)}, bf16[128,2048]{0,1:T(8,128)(2,1)S(1)}, u32[]{:S(2)}) copy-start(bf16[128,2048]{0,1:T(8,128)(2,1)S(1)} %copy.309) | copy-start | bytes 1572868
  19.4 2.4 %copy-start.12 = (bf16[128,2048]{0,1:T(8,128)(2,1)}, bf16[128,2048]{0,1:T(8,128)(2,1)S(1)}, u32[]{:S(2)}) copy-start(bf16[128,2048]{0,1:T(8,128)(2,1)S(1)} %copy.312) | copy-start | bytes 1572868
  19.7 3.3 %copy-start.13 = (bf16[128,2048]{0,1:T(8,128)(2,1)}, bf16[128,2048]{0,1:T(8,128)(2,1)S(1)}, u32[]{:S(2)}) copy-start(bf16[128,2048]{0,1:T(8,128)(2,1)S(1)} %copy.311) | copy-start | bytes 1572868
  21.3 1.8 %copy-start.21 = (s32[2]{0:T(128)S(1)}, s32[2]{0:T(128)}, u32[]{:S(2)}) copy-start(s32[2]{0:T(128)} %param.19) | copy-start | bytes 28
  21.3 3.7 %copy-start.22 = (s32[2,5]{1,0:T(2,128)S(1)}, s32[2,5]{1,0:T(2,128)}, u32[]{:S(2)}) copy-start(s32[2,5]{1,0:T(2,128)} %param.18) | copy-start | bytes 124
  23.0 40.8 %collective-permute-start = (f32[16,136,128]{2,1,0:T(8,128)}, f32[16,136,128]{2,1,0:T(8,128)}, u32[]{:S(2)}, u32[]{:S(2)}) collective-permute-start(f32[16,136,128]{2,1,0:T(8,128)} %pad_maximum_fusion), channel_id=1, source_target_pairs={{0,4},{4,0},{1,5},{5,1},{2,6},{6,2},{3,7},{7,3},{8,12},{12,8},{9,1... | collective-permute-start | bytes 3342344 | tf_op jit(solution)/shard_map/ppermute | solution.py:101
  31.0 9.4 %copy-start.3 = (bf16[256,2048]{1,0:T(8,128)(2,1)S(1)}, bf16[256,2048]{1,0:T(8,128)(2,1)}, u32[]{:S(2)}) copy-start(bf16[256,2048]{1,0:T(8,128)(2,1)} %param.16) | copy-start | bytes 3145732
  40.4 20.4 %copy-start.4 = (bf16[256,2048]{1,0:T(8,128)(2,1)S(1)}, bf16[256,2048]{1,0:T(8,128)(2,1)}, u32[]{:S(2)}) copy-start(bf16[256,2048]{1,0:T(8,128)(2,1)} %param.17) | copy-start | bytes 3145732
  43.5 24.8 %collective-permute-start.7 = (bf16[256,2048]{1,0:T(8,128)(2,1)}, bf16[256,2048]{1,0:T(8,128)(2,1)}, u32[]{:S(2)}, u32[]{:S(2)}) collective-permute-start(bf16[256,2048]{1,0:T(8,128)(2,1)} %get-tuple-element.30), channel_id=1, source_target_pairs={{0,4},{4,0},{1,5},{5,1},{2,6},{6,2},{3,7},{7,3},{8,12},{12,8},{9,1... | collective-permute-start | bytes 3145736 | tf_op jit(solution)/shard_map/ppermute | solution.py:101
  63.8 11.7 %collective-permute-start.5 = (bf16[256,2048]{1,0:T(8,128)(2,1)}, bf16[256,2048]{1,0:T(8,128)(2,1)}, u32[]{:S(2)}, u32[]{:S(2)}) collective-permute-start(bf16[256,2048]{1,0:T(8,128)(2,1)} %get-tuple-element.28), channel_id=1, source_target_pairs={{0,4},{4,0},{1,5},{5,1},{2,6},{6,2},{3,7},{7,3},{8,12},{12,8},{9,1... | collective-permute-start | bytes 3145736 | tf_op jit(solution)/shard_map/ppermute | solution.py:101
  71.7 3.8 %copy-start.2 = (bf16[768,2048]{1,0:T(8,128)(2,1)S(1)}, bf16[768,2048]{1,0:T(8,128)(2,1)}, u32[]{:S(2)}) copy-start(bf16[768,2048]{1,0:T(8,128)(2,1)} %get-tuple-element.29) | copy-start | bytes 9437188
  71.7 5.2 %copy-start.5 = (bf16[256,2048]{1,0:T(8,128)(2,1)S(1)}, bf16[256,2048]{1,0:T(8,128)(2,1)}, u32[]{:S(2)}) copy-start(bf16[256,2048]{1,0:T(8,128)(2,1)} %param.17) | copy-start | bytes 3145732
  82.3 1.3 copy-start.18
  95.0 32.0 %all-to-all-start = ((bf16[4,64,2048]{2,1,0:T(8,128)(2,1)}), bf16[4,64,2048]{2,1,0:T(8,128)(2,1)S(1)}, u32[]{:S(2)}, u32[]{:S(2)}) async-start(bf16[4,64,2048]{2,1,0:T(8,128)(2,1)} %all_to_all.28), calls=%async_computation | async-start | bytes 2097152 | tf_op jit(solution)/shard_map/all_to_all | solution.py:258
  112.7 9.8 %copy-start.9 = (bf16[128,2048]{0,1:T(8,128)(2,1)S(1)}, bf16[128,2048]{0,1:T(8,128)(2,1)}, u32[]{:S(2)}) copy-start(bf16[128,2048]{0,1:T(8,128)(2,1)} %copy.307) | copy-start | bytes 1572868
  112.7 9.8 %copy-start.16 = (f32[128,16,128]{2,0,1:T(8,128)S(1)}, f32[128,16,128]{2,0,1:T(8,128)}, u32[]{:S(2)}) copy-start(f32[128,16,128]{2,0,1:T(8,128)} %convolution_bitcast_fusion.3) | copy-start | bytes 3145732
  113.4 10.5 %copy-start.8 = (bf16[128,2048]{0,1:T(8,128)(2,1)S(1)}, bf16[128,2048]{0,1:T(8,128)(2,1)}, u32[]{:S(2)}) copy-start(bf16[128,2048]{0,1:T(8,128)(2,1)} %copy.310) | copy-start | bytes 1572868
  114.3 13.6 %collective-permute-start.1 = (f32[8,136,128]{2,1,0:T(8,128)}, f32[8,136,128]{2,1,0:T(8,128)}, u32[]{:S(2)}, u32[]{:S(2)}) collective-permute-start(f32[8,136,128]{2,1,0:T(8,128)} %pad_maximum_fusion.2), channel_id=1, source_target_pairs={{0,192},{1,193},{2,194},{3,195},{4,196},{5,197},{6,198},{7,199},{8... | collective-permute-start | bytes 1671176 | tf_op jit(solution)/shard_map/ppermute | solution.py:133
  115.8 13.1 %collective-permute-start.2 = (f32[8,136,128]{2,1,0:T(8,128)}, f32[8,136,128]{2,1,0:T(8,128)}, u32[]{:S(2)}, u32[]{:S(2)}) collective-permute-start(f32[8,136,128]{2,1,0:T(8,128)} %pad_maximum_fusion.2), channel_id=1, source_target_pairs={{0,128},{64,192},{1,129},{65,193},{2,130},{66,194},{3,131},{67,195... | collective-permute-start | bytes 1671176 | tf_op jit(solution)/shard_map/ppermute | solution.py:133
  120.6 22.7 %collective-permute-start.3 = (f32[8,136,128]{2,1,0:T(8,128)}, f32[8,136,128]{2,1,0:T(8,128)}, u32[]{:S(2)}, u32[]{:S(2)}) collective-permute-start(f32[8,136,128]{2,1,0:T(8,128)} %pad_maximum_fusion.2), channel_id=1, source_target_pairs={{0,64},{64,128},{128,192},{1,65},{65,129},{129,193},{2,66},{66,130... | collective-permute-start | bytes 1671176 | tf_op jit(solution)/shard_map/ppermute | solution.py:133
  126.9 21.2 %copy-start.14 = (f32[128,16,128]{2,0,1:T(8,128)S(1)}, f32[128,16,128]{2,0,1:T(8,128)}, u32[]{:S(2)}) copy-start(f32[128,16,128]{2,0,1:T(8,128)} %convolution_bitcast_fusion.1) | copy-start | bytes 3145732
  146.2 3.7 %copy-start.7 = (f32[16,128,128]{2,1,0:T(8,128)S(1)}, f32[16,128,128]{2,1,0:T(8,128)}, u32[]{:S(2)}) copy-start(f32[16,128,128]{2,1,0:T(8,128)} %copy-done.6) | copy-start | bytes 3145732
  146.2 3.7 %copy-start.15 = (bf16[256,2048]{1,0:T(8,128)(2,1)S(1)}, bf16[256,2048]{1,0:T(8,128)(2,1)}, u32[]{:S(2)}) copy-start(bf16[256,2048]{1,0:T(8,128)(2,1)} %param.10) | copy-start | bytes 3145732
  146.2 3.7 %copy-start.17 = (f32[128,16,128]{2,0,1:T(8,128)S(1)}, f32[128,16,128]{2,0,1:T(8,128)}, u32[]{:S(2)}) copy-start(f32[128,16,128]{2,0,1:T(8,128)} %fusion.22) | copy-start | bytes 3145732
  147.9 2.0 %collective-permute-start.8 = (f32[8,128,128]{2,1,0:T(8,128)S(1)}, f32[8,128,128]{2,1,0:T(8,128)S(1)}, u32[]{:S(2)}, u32[]{:S(2)}) collective-permute-start(f32[8,128,128]{2,1,0:T(8,128)S(1)} %multiply_add_fusion), channel_id=1, source_target_pairs={{0,4},{4,0},{1,5},{5,1},{2,6},{6,2},{3,7},{7,3},{8,12},{12,8},{9,1... | collective-permute-start | bytes 1572872 | tf_op jit(solution)/shard_map/ppermute | solution.py:101
  149.9 1.6 copy-start.20
  152.3 21.7 %copy-start.1 = (f32[16,256]{1,0:T(8,128)S(1)}, f32[16,256]{1,0:T(8,128)}, u32[]{:S(2)}) copy-start(f32[16,256]{1,0:T(8,128)} %param.13) | copy-start | bytes 49156
  (2 other events, 2.0 us)
Sparse Core Ops, SparseCore 0:
  68.4 41.8 all-gather.2

commit v12 on v11

--- a/solution.py
+++ b/solution.py
@@ -65,19 +65,6 @@
 
 def unpacked(both, width):
     return both[..., :width, :], both[..., width, 0]
-
-
-def narrow(state, factor):
-    heads, width, _ = state.shape
-    high = factor.astype(jnp.bfloat16)
-    low = (factor - high.astype(jnp.float32)).astype(jnp.bfloat16)
-    rows = lambda part: jnp.broadcast_to(part[:, None, None], (heads, 8, width))
-    return jnp.concatenate([state.astype(jnp.bfloat16), rows(high), rows(low)], axis=1)
-
-
-def widened(both, width):
-    wide = both.astype(jnp.float32)
-    return wide[..., :width, :], wide[..., width, 0] + wide[..., width + 8, 0]
 
 
 def folding_weights(factors, upto):
@@ -119,8 +106,8 @@
     second_factor = lax.dynamic_slice_in_dim(second_all, low, half, 0)
     chip_state = second_factor[:, None, None] * first + second
     chip_factor = first_factor * second_factor
-    row_states, row_factors = widened(
-        lax.all_gather(narrow(chip_state, chip_factor), "cz"), width
+    row_states, row_factors = unpacked(
+        lax.all_gather(packed(chip_state, chip_factor), "cz"), width
     )
     count = row_states.shape[0]
     before = folded(row_states, row_factors, row)

time: 182 us -> 179 us (0.984)
  local copies, waits for them, and re-layouts: 39.7 us -> 31.2 us
  waiting for transfers between devices: 44.6 us -> 52.4 us
    ppermute x2, waiting for transfers between devices: 16.8 us -> 28.7 us  [passed_along(): return lax.ppermute(block, axis, route)]
    all_gather x1, waiting for transfers between devices: 11 us -> 2.8 us  [carry_in(): lax.all_gather(packed(chip_state, chip_factor), 'cz')]
    unnamed x62, local copies, waits for them, and re-layouts: 21.9 us -> 15.2 us
    ppermute x3, waiting for transfers between devices: 15.3 us -> 19.5 us  [carry_in(): lax.ppermute(mine, 'cy', [(i, i + d) for i in range(columns) if i + d < c...]
    reduce_sum x1, other arithmetic: 0.68 us -> 3.09 us  [folded(): return jnp.sum(weights[:, :, None, None] * states, axis=0)]
    convert_element_type x3 -> x0, other arithmetic: 2.3 us -> none  [the longest x1 2.07 us: widened(): wide = both.astype(jnp.float32)]
    slice x3 -> x4, local copies, waits for them, and re-layouts: 2.7 us -> 3.83 us  [unpacked(): return (both[..., :width, :], both[..., width, 0])]
  transfers between devices with their start and end apart: 11 -> 11, of which waited for: 5 -> 6; matrix products, arithmetic and copies ran while one was open for 39% -> 33% of each run, Pallas kernels for 0% -> 0%
where the time goes in v12:
time: 179 us; the launch traced here: 178 us
  waiting for transfers between devices  52.4 us (29%)
  local copies, waits for them, and re-layouts  31.2 us (17%)
  other arithmetic  22 us (12%)
  blocking collectives  19.5 us (11%)
  starting transfers between devices  19.2 us (11%)
  matrix products  18.9 us (11%)
  between operations  14.7 us (8%)
    ppermute x2, waiting for transfers between devices, passed_along(): return lax.ppermute(block, axis, route)  28.7 us
    all_to_all x1, blocking collectives, local(): lax.all_to_all(linear_heads, 'head', split_axis=0, concat_axis=1, tiled=T...  19.5 us
    ppermute x3, waiting for transfers between devices, carry_in(): lax.ppermute(mine, 'cy', [(i, i + d) for i in range(columns) if i + d < c...  19.5 us
    unnamed x62, local copies, waits for them, and re-layouts  15.2 us
    ppermute x2, starting transfers between devices, passed_along(): return lax.ppermute(block, axis, route)  7.66 us
    ppermute x3, starting transfers between devices, carry_in(): lax.ppermute(mine, 'cy', [(i, i + d) for i in range(columns) if i + d < c...  6.81 us
    dot_general x2, matrix products, block_output(): jnp.einsum('htj,jhd->thd', mixing, values_blk, preferred_element_type=jnp...  6.28 us
    dot_general x2, matrix products, attend(): jnp.einsum('htkj,kjhd->thd', weights, values_sel, preferred_element_type=...  5.81 us
  transfers between devices with their start and end apart: 11, of which 6 were waited for; matrix products, arithmetic and copies ran while one was open for 33% of the time, Pallas kernels for 0%

profile of v12, /device:TPU:8, one launch (start us, length us, event | category | flops | bytes accessed | tf_op | source)
XLA Modules:
  0.0 178.0 jit_solution(1423772739056430813)
XLA Ops:
  7.2 3.8 %collective-permute-start.6 = (bf16[256,2048]{1,0:T(8,128)(2,1)}, bf16[256,2048]{1,0:T(8,128)(2,1)}, u32[]{:S(2)}, u32[]{:S(2)}) collective-permute-start(bf16[256,2048]{1,0:T(8,128)(2,1)} %param.16), channel_id=1, source_target_pairs={{0,8},{4,12},{8,16},{12,20},{16,24},{20,28},{24,32},{28,36},{32,40... | collective-permute-start | bytes 3145736 | tf_op jit(solution)/shard_map/ppermute | solution.py:21
  11.1 3.8 %collective-permute-start.4 = (bf16[256,2048]{1,0:T(8,128)(2,1)}, bf16[256,2048]{1,0:T(8,128)(2,1)}, u32[]{:S(2)}, u32[]{:S(2)}) collective-permute-start(bf16[256,2048]{1,0:T(8,128)(2,1)} %param.17), channel_id=1, source_target_pairs={{0,8},{4,12},{8,16},{12,20},{16,24},{20,28},{24,32},{28,36},{32,40... | collective-permute-start | bytes 3145736 | tf_op jit(solution)/shard_map/ppermute | solution.py:21
  15.8 1.3 fusion.81
  17.4 1.5 fusion.82
  26.4 1.3 fusion.79
  30.1 1.4 fusion.78
  37.6 1.6 collective-permute-done.6
  39.2 3.0 %broadcast_select_fusion = (bf16[256,2048]{1,0:T(8,128)(2,1)}, bf16[768,2048]{1,0:T(8,128)(2,1)S(1)}) fusion(bf16[256,2048]{1,0:T(8,128)(2,1)} %param.16, bf16[256,2048]{1,0:T(8,128)(2,1)} %collective-permute-done.6, pred[]{:T(512)S(6)} %eq.34), kind=kLoop, calls=%fused_computation.67 | loop fusion | flops 524287 | bytes 4194305 | tf_op jit(solution)/shard_map/jit(_where)/select_n | solution.py:195
  42.2 3.1 %convolution_bitcast_fusion.3 = f32[128,16,128]{2,0,1:T(8,128)} fusion(bf16[128,16,128]{0,2,1:T(8,128)(2,1)} %bitcast.191, bf16[128,16,128]{0,2,1:T(8,128)(2,1)} %bitcast.192, bf16[128,16,128]{0,2,1:T(8,128)(2,1)} %bitcast.189, f32[16,128]{1,0:T(8,128)S(1)} %get-tuple-element.50, pred[128,128]{1,0:T(8,128)(4,1)S(1)} %iota_compare_fusion), kind=kOutput, calls=%fused_computation.42 | convolution fusion | flops 135528448 | bytes 2646016 | tf_op jit(solution)/shard_map/htj,jhd->thd/dot_general | solution.py:48
  45.4 27.1 %collective-permute-done.4 = bf16[256,2048]{1,0:T(8,128)(2,1)} collective-permute-done((bf16[256,2048]{1,0:T(8,128)(2,1)}, bf16[256,2048]{1,0:T(8,128)(2,1)}, u32[]{:S(2)}, u32[]{:S(2)}) %collective-permute-start.4) | collective-permute-done | bytes 1048608 | tf_op jit(solution)/shard_map/ppermute | solution.py:21
  72.5 2.1 %broadcast_select_fusion.1 = (bf16[256,2048]{1,0:T(8,128)(2,1)S(1)}, bf16[768,2048]{1,0:T(8,128)(2,1)S(1)}) fusion(bf16[256,2048]{1,0:T(8,128)(2,1)} %param.17, bf16[256,2048]{1,0:T(8,128)(2,1)} %collective-permute-done.4, pred[]{:T(512)S(6)} %eq.34), kind=kLoop, calls=%fused_computation.68 | loop fusion | flops 524287 | bytes 4194305 | tf_op jit(solution)/shard_map/jit(_where)/select_n | solution.py:195
  74.9 1.3 constant_dynamic-update-slice_fusion.4
  78.9 1.8 %slice_bitcast_fusion.3 = (bf16[80,8,16,128]{3,1,2,0:T(8,128)(2,1)S(1)}, bf16[80,8,16,128]{3,1,2,0:T(8,128)(2,1)S(1)}) fusion(bf16[768,2048]{1,0:T(8,128)(2,1)S(1)} %constant_dynamic-update-slice_fusion), kind=kLoop, calls=%fused_computation.15 | loop fusion | bytes 10485760
  83.4 1.3 fusion.2
  84.7 1.3 fusion.3
  88.2 2.8 %fusion.31 = bf16[128,16,128]{2,0,1:T(8,128)(2,1)S(1)} fusion(f32[16,5,128,128]{3,2,1,0:T(8,128)S(1)} %get-tuple-element.66, f32[16,128]{1,0:T(8,128)S(1)} %fusion, f32[16,128]{1,0:T(8,128)S(1)} %get-tuple-element.65, pred[128,5,128]{0,2,1:T(8,128)(4,1)S(1)} %get-tuple-element.40, bf16[5,128,16,128]{3,2,1,0:T(8,128)(2,1)S(1)} %bitcast.183), kind=kOutput, calls=%fused_computation.48 | convolution fusion | flops 342360064 | bytes 8486912 | tf_op jit(solution)/shard_map/htkj,kjhd->thd/dot_general | solution.py:184
  91.0 3.0 %fusion.34 = bf16[128,16,128]{2,0,1:T(8,128)(2,1)S(1)} fusion(f32[16,5,128,128]{3,2,1,0:T(8,128)S(1)} %get-tuple-element.64, f32[16,128]{1,0:T(8,128)S(1)} %fusion.1, f32[16,128]{1,0:T(8,128)S(1)} %get-tuple-element.63, pred[128,5,128]{0,2,1:T(8,128)(4,1)S(1)} %get-tuple-element.41, bf16[5,128,16,128]{3,2,1,0:T(8,128)(2,1)S(1)} %bitcast.184), kind=kOutput, calls=%fused_computation.49 | convolution fusion | flops 342360064 | bytes 8486912 | tf_op jit(solution)/shard_map/htkj,kjhd->thd/dot_general | solution.py:184
  94.8 1.3 all_to_all.28
  96.1 4.3 %all-to-all-start = ((bf16[4,64,2048]{2,1,0:T(8,128)(2,1)}), bf16[4,64,2048]{2,1,0:T(8,128)(2,1)S(1)}, u32[]{:S(2)}, u32[]{:S(2)}) async-start(bf16[4,64,2048]{2,1,0:T(8,128)(2,1)} %all_to_all.28), calls=%async_computation | async-start | bytes 2097152 | tf_op jit(solution)/shard_map/all_to_all | solution.py:245
  100.4 2.8 %all-gather.3.cloned.1.call-done = f32[64,136,128]{2,1,0:T(8,128)} async-done(((f32[8,136,128]{2,1,0:T(8,128)}), f32[64,136,128]{2,1,0:T(8,128)}) %all-gather.3.cloned.1.call-update) | async-done | bytes 4456464 | tf_op jit(solution)/shard_map/all_gather | solution.py:110
  104.6 3.1 %multiply_reduce_fusion.1 = (f32[8,128,128]{2,1,0:T(8,128)S(1)}, f32[8,128,128]{2,1,0:T(8,128)S(1)}) fusion(f32[8,8,136,128]{3,2,1,0:T(8,128)} %bitcast.181, f32[8,8]{1,0:T(8,128)S(1)} %get-tuple-element.61, f32[8,8]{1,0:T(8,128)S(1)} %get-tuple-element.62), kind=kLoop, calls=%fused_computation.9 | loop fusion | flops 3932160 | bytes 5243392 | tf_op jit(solution)/shard_map/reduce_sum | solution.py:79
  108.6 1.5 collective-permute-start.1
  110.1 3.4 %collective-permute-start.2 = (f32[8,136,128]{2,1,0:T(8,128)}, f32[8,136,128]{2,1,0:T(8,128)}, u32[]{:S(2)}, u32[]{:S(2)}) collective-permute-start(f32[8,136,128]{2,1,0:T(8,128)} %pad_maximum_fusion.3), channel_id=1, source_target_pairs={{0,128},{64,192},{1,129},{65,193},{2,130},{66,194},{3,131},{67,195... | collective-permute-start | bytes 1671176 | tf_op jit(solution)/shard_map/ppermute | solution.py:120
  113.5 1.9 %collective-permute-start.3 = (f32[8,136,128]{2,1,0:T(8,128)}, f32[8,136,128]{2,1,0:T(8,128)}, u32[]{:S(2)}, u32[]{:S(2)}) collective-permute-start(f32[8,136,128]{2,1,0:T(8,128)} %pad_maximum_fusion.3), channel_id=1, source_target_pairs={{0,64},{64,128},{128,192},{1,65},{65,129},{129,193},{2,66},{66,130... | collective-permute-start | bytes 1671176 | tf_op jit(solution)/shard_map/ppermute | solution.py:120
  115.4 1.3 fusion.22
  116.8 3.1 %convolution_bitcast_fusion.1 = f32[128,16,128]{2,0,1:T(8,128)} fusion(bf16[128,16,128]{0,2,1:T(8,128)(2,1)} %bitcast.195, bf16[128,16,128]{0,2,1:T(8,128)(2,1)S(1)} %bitcast.186, bf16[128,16,128]{0,2,1:T(8,128)(2,1)} %bitcast.197, f32[16,128]{1,0:T(8,128)S(1)} %get-tuple-element.51, pred[128,128]{1,0:T(8,128)(4,1)S(1)} %iota_compare_fusion), kind=kOutput, calls=%fused_computation.38 | convolution fusion | flops 135528448 | bytes 2646016 | tf_op jit(solution)/shard_map/htj,jhd->thd/dot_general | solution.py:48
  121.0 3.8 %collective-permute-done.2 = f32[8,136,128]{2,1,0:T(8,128)} collective-permute-done((f32[8,136,128]{2,1,0:T(8,128)}, f32[8,136,128]{2,1,0:T(8,128)}, u32[]{:S(2)}, u32[]{:S(2)}) %collective-permute-start.2) | collective-permute-done | bytes 557088 | tf_op jit(solution)/shard_map/ppermute | solution.py:120
  124.8 15.7 %collective-permute-done.3 = f32[8,136,128]{2,1,0:T(8,128)} collective-permute-done((f32[8,136,128]{2,1,0:T(8,128)}, f32[8,136,128]{2,1,0:T(8,128)}, u32[]{:S(2)}, u32[]{:S(2)}) %collective-permute-start.3) | collective-permute-done | bytes 557088 | tf_op jit(solution)/shard_map/ppermute | solution.py:120
  143.3 1.7 multiply_add_fusion
  145.6 1.4 collective-permute-done.8
  147.1 1.5 multiply_reduce_fusion.2
  150.6 19.5 %all_to_all.38 = bf16[4,64,2048]{2,1,0:T(8,128)(2,1)S(1)} all-to-all(bf16[4,64,2048]{2,1,0:T(8,128)(2,1)S(1)} %all_to_all.32), channel_id=1, replica_groups=mesh['cy'=4,'cz'=8,'cc'=2,'head'=4] {'head'}, dimensions={0} | all-to-all | bytes 2097152 | tf_op jit(solution)/shard_map/all_to_all | solution.py:249
  (137 shorter events, 35.2 us)
Async XLA Ops:
  7.2 7.7 %copy-start = (f32[16,256]{1,0:T(8,128)S(1)}, f32[16,256]{1,0:T(8,128)}, u32[]{:S(2)}) copy-start(f32[16,256]{1,0:T(8,128)} %param.13) | copy-start | bytes 49156
  7.2 96.1 %all-gather.3.cloned.1.call-start = ((), (), s32[]{:S(2)}) async-start(), calls=%async_computation.2 | async-start | bytes 5013504 | tf_op jit(solution)/shard_map/all_gather | solution.py:110
  7.2 31.9 %collective-permute-start.6 = (bf16[256,2048]{1,0:T(8,128)(2,1)}, bf16[256,2048]{1,0:T(8,128)(2,1)}, u32[]{:S(2)}, u32[]{:S(2)}) collective-permute-start(bf16[256,2048]{1,0:T(8,128)(2,1)} %param.16), channel_id=1, source_target_pairs={{0,8},{4,12},{8,16},{12,20},{16,24},{20,28},{24,32},{28,36},{32,40... | collective-permute-start | bytes 3145736 | tf_op jit(solution)/shard_map/ppermute | solution.py:21
  11.1 61.4 %collective-permute-start.4 = (bf16[256,2048]{1,0:T(8,128)(2,1)}, bf16[256,2048]{1,0:T(8,128)(2,1)}, u32[]{:S(2)}, u32[]{:S(2)}) collective-permute-start(bf16[256,2048]{1,0:T(8,128)(2,1)} %param.17), channel_id=1, source_target_pairs={{0,8},{4,12},{8,16},{12,20},{16,24},{20,28},{24,32},{28,36},{32,40... | collective-permute-start | bytes 3145736 | tf_op jit(solution)/shard_map/ppermute | solution.py:21
  17.4 3.9 %copy-start.9 = (bf16[128,2048]{0,1:T(8,128)(2,1)}, bf16[128,2048]{0,1:T(8,128)(2,1)S(1)}, u32[]{:S(2)}) copy-start(bf16[128,2048]{0,1:T(8,128)(2,1)S(1)} %copy.304) | copy-start | bytes 1572868
  19.1 2.2 %copy-start.10 = (bf16[128,2048]{0,1:T(8,128)(2,1)}, bf16[128,2048]{0,1:T(8,128)(2,1)S(1)}, u32[]{:S(2)}) copy-start(bf16[128,2048]{0,1:T(8,128)(2,1)S(1)} %copy.305) | copy-start | bytes 1572868
  19.4 3.3 %copy-start.12 = (bf16[128,2048]{0,1:T(8,128)(2,1)}, bf16[128,2048]{0,1:T(8,128)(2,1)S(1)}, u32[]{:S(2)}) copy-start(bf16[128,2048]{0,1:T(8,128)(2,1)S(1)} %copy.308) | copy-start | bytes 1572868
  19.7 4.2 %copy-start.13 = (bf16[128,2048]{0,1:T(8,128)(2,1)}, bf16[128,2048]{0,1:T(8,128)(2,1)S(1)}, u32[]{:S(2)}) copy-start(bf16[128,2048]{0,1:T(8,128)(2,1)S(1)} %copy.307) | copy-start | bytes 1572868
  21.3 2.7 %copy-start.21 = (s32[2]{0:T(128)S(1)}, s32[2]{0:T(128)}, u32[]{:S(2)}) copy-start(s32[2]{0:T(128)} %param.19) | copy-start | bytes 28
  21.3 4.6 %copy-start.22 = (s32[2,5]{1,0:T(2,128)S(1)}, s32[2,5]{1,0:T(2,128)}, u32[]{:S(2)}) copy-start(s32[2,5]{1,0:T(2,128)} %param.18) | copy-start | bytes 124
  23.9 5.1 %collective-permute-start = (f32[16,136,128]{2,1,0:T(8,128)}, f32[16,136,128]{2,1,0:T(8,128)}, u32[]{:S(2)}, u32[]{:S(2)}) collective-permute-start(f32[16,136,128]{2,1,0:T(8,128)} %pad_maximum_fusion), channel_id=1, source_target_pairs={{0,4},{4,0},{1,5},{5,1},{2,6},{6,2},{3,7},{7,3},{8,12},{12,8},{9,1... | collective-permute-start | bytes 3342344 | tf_op jit(solution)/shard_map/ppermute | solution.py:88
  42.2 32.7 %collective-permute-start.7 = (bf16[256,2048]{1,0:T(8,128)(2,1)}, bf16[256,2048]{1,0:T(8,128)(2,1)}, u32[]{:S(2)}, u32[]{:S(2)}) collective-permute-start(bf16[256,2048]{1,0:T(8,128)(2,1)} %get-tuple-element.32), channel_id=1, source_target_pairs={{0,4},{4,0},{1,5},{5,1},{2,6},{6,2},{3,7},{7,3},{8,12},{12,8},{9,1... | collective-permute-start | bytes 3145736 | tf_op jit(solution)/shard_map/ppermute | solution.py:88
  45.4 30.9 %copy-start.4 = (bf16[256,2048]{1,0:T(8,128)(2,1)S(1)}, bf16[256,2048]{1,0:T(8,128)(2,1)}, u32[]{:S(2)}) copy-start(bf16[256,2048]{1,0:T(8,128)(2,1)} %param.16) | copy-start | bytes 3145732
  74.6 3.8 %collective-permute-start.5 = (bf16[256,2048]{1,0:T(8,128)(2,1)S(1)}, bf16[256,2048]{1,0:T(8,128)(2,1)S(1)}, u32[]{:S(2)}, u32[]{:S(2)}) collective-permute-start(bf16[256,2048]{1,0:T(8,128)(2,1)S(1)} %get-tuple-element.30), channel_id=1, source_target_pairs={{0,4},{4,0},{1,5},{5,1},{2,6},{6,2},{3,7},{7,3},{8,12},{12,8},{9,1... | collective-permute-start | bytes 3145736 | tf_op jit(solution)/shard_map/ppermute | solution.py:88
  77.5 1.2 copy-start.5
  82.3 1.1 copy-start.19
  83.4 1.3 copy-start.18
  96.1 23.8 %all-to-all-start = ((bf16[4,64,2048]{2,1,0:T(8,128)(2,1)}), bf16[4,64,2048]{2,1,0:T(8,128)(2,1)S(1)}, u32[]{:S(2)}, u32[]{:S(2)}) async-start(bf16[4,64,2048]{2,1,0:T(8,128)(2,1)} %all_to_all.28), calls=%async_computation | async-start | bytes 2097152 | tf_op jit(solution)/shard_map/all_to_all | solution.py:245
  104.6 10.9 %copy-start.11 = (bf16[128,2048]{0,1:T(8,128)(2,1)S(1)}, bf16[128,2048]{0,1:T(8,128)(2,1)}, u32[]{:S(2)}) copy-start(bf16[128,2048]{0,1:T(8,128)(2,1)} %copy.303) | copy-start | bytes 1572868
  104.6 10.9 %copy-start.16 = (f32[128,16,128]{2,0,1:T(8,128)S(1)}, f32[128,16,128]{2,0,1:T(8,128)}, u32[]{:S(2)}) copy-start(f32[128,16,128]{2,0,1:T(8,128)} %convolution_bitcast_fusion.3) | copy-start | bytes 3145732
  107.7 9.1 %copy-start.8 = (bf16[128,2048]{0,1:T(8,128)(2,1)S(1)}, bf16[128,2048]{0,1:T(8,128)(2,1)}, u32[]{:S(2)}) copy-start(bf16[128,2048]{0,1:T(8,128)(2,1)} %copy.306) | copy-start | bytes 1572868
  108.6 12.4 %collective-permute-start.1 = (f32[8,136,128]{2,1,0:T(8,128)}, f32[8,136,128]{2,1,0:T(8,128)}, u32[]{:S(2)}, u32[]{:S(2)}) collective-permute-start(f32[8,136,128]{2,1,0:T(8,128)} %pad_maximum_fusion.3), channel_id=1, source_target_pairs={{0,192},{1,193},{2,194},{3,195},{4,196},{5,197},{6,198},{7,199},{8... | collective-permute-start | bytes 1671176 | tf_op jit(solution)/shard_map/ppermute | solution.py:120
  110.1 14.7 %collective-permute-start.2 = (f32[8,136,128]{2,1,0:T(8,128)}, f32[8,136,128]{2,1,0:T(8,128)}, u32[]{:S(2)}, u32[]{:S(2)}) collective-permute-start(f32[8,136,128]{2,1,0:T(8,128)} %pad_maximum_fusion.3), channel_id=1, source_target_pairs={{0,128},{64,192},{1,129},{65,193},{2,130},{66,194},{3,131},{67,195... | collective-permute-start | bytes 1671176 | tf_op jit(solution)/shard_map/ppermute | solution.py:120
  113.5 26.9 %collective-permute-start.3 = (f32[8,136,128]{2,1,0:T(8,128)}, f32[8,136,128]{2,1,0:T(8,128)}, u32[]{:S(2)}, u32[]{:S(2)}) collective-permute-start(f32[8,136,128]{2,1,0:T(8,128)} %pad_maximum_fusion.3), channel_id=1, source_target_pairs={{0,64},{64,128},{128,192},{1,65},{65,129},{129,193},{2,66},{66,130... | collective-permute-start | bytes 1671176 | tf_op jit(solution)/shard_map/ppermute | solution.py:120
  116.8 28.5 %copy-start.3 = (f32[16,128,128]{2,1,0:T(8,128)S(1)}, f32[16,128,128]{2,1,0:T(8,128)}, u32[]{:S(2)}) copy-start(f32[16,128,128]{2,1,0:T(8,128)} %copy-done.2) | copy-start | bytes 3145732
  119.9 25.3 %copy-start.14 = (f32[128,16,128]{2,0,1:T(8,128)S(1)}, f32[128,16,128]{2,0,1:T(8,128)}, u32[]{:S(2)}) copy-start(f32[128,16,128]{2,0,1:T(8,128)} %convolution_bitcast_fusion.1) | copy-start | bytes 3145732
  143.3 3.7 %copy-start.7 = (f32[16,128,128]{2,1,0:T(8,128)S(1)}, f32[16,128,128]{2,1,0:T(8,128)}, u32[]{:S(2)}) copy-start(f32[16,128,128]{2,1,0:T(8,128)} %copy-done.6) | copy-start | bytes 3145732
  143.3 3.7 %copy-start.15 = (bf16[256,2048]{1,0:T(8,128)(2,1)S(1)}, bf16[256,2048]{1,0:T(8,128)(2,1)}, u32[]{:S(2)}) copy-start(bf16[256,2048]{1,0:T(8,128)(2,1)} %param.10) | copy-start | bytes 3145732
  143.3 3.7 %copy-start.17 = (f32[128,16,128]{2,0,1:T(8,128)S(1)}, f32[128,16,128]{2,0,1:T(8,128)}, u32[]{:S(2)}) copy-start(f32[128,16,128]{2,0,1:T(8,128)} %fusion.22) | copy-start | bytes 3145732
  145.1 2.0 %collective-permute-start.8 = (f32[8,128,128]{2,1,0:T(8,128)S(1)}, f32[8,128,128]{2,1,0:T(8,128)S(1)}, u32[]{:S(2)}, u32[]{:S(2)}) collective-permute-start(f32[8,128,128]{2,1,0:T(8,128)S(1)} %multiply_add_fusion), channel_id=1, source_target_pairs={{0,4},{4,0},{1,5},{5,1},{2,6},{6,2},{3,7},{7,3},{8,12},{12,8},{9,1... | collective-permute-start | bytes 1572872 | tf_op jit(solution)/shard_map/ppermute | solution.py:88
  147.1 1.6 copy-start.20
  149.4 21.7 %copy-start.1 = (f32[16,256]{1,0:T(8,128)S(1)}, f32[16,256]{1,0:T(8,128)}, u32[]{:S(2)}) copy-start(f32[16,256]{1,0:T(8,128)} %param.13) | copy-start | bytes 49156
  (2 other events, 1.9 us)
Sparse Core Ops, SparseCore 0:
  33.6 69.5 all-gather.2

commit v13 on v12

--- a/solution.py
+++ b/solution.py
@@ -225,6 +225,18 @@
     return jnp.concatenate(outputs, axis=0).reshape(length, columns)
 
 
+def rows_by_permutes(block):
+    count, mine = (lax.psum(1, "head"), lax.axis_index("head"))
+    length, columns = block.shape
+    share = length // count
+    pieces = [lax.dynamic_slice_in_dim(block, mine * share, share, 0)]
+    for d in range(1, count):
+        outgoing = lax.dynamic_slice_in_dim(block, ((mine + d) % count) * share, share, 0)
+        pieces.append(lax.ppermute(outgoing, "head", [(i, (i + d) % count) for i in range(count)]))
+    ordered = jnp.roll(jnp.stack(pieces[::-1]), mine - (count - 1), axis=0)
+    return ordered.transpose(1, 0, 2).reshape(share, count * columns)
+
+
 def local(
     linear_query,
     linear_key,
@@ -246,7 +258,7 @@
     linear_heads, softmax_rows = linear_layer(
         linear_query, linear_key, linear_value, log_decay, norm_gain, softmax_rows
     )
-    linear_rows = lax.all_to_all(linear_heads, "head", split_axis=0, concat_axis=1, tiled=True)
+    linear_rows = rows_by_permutes(linear_heads)
     return (linear_rows, softmax_rows)
 
 

time: 179 us -> 189 us (1.056)
  waiting for transfers between devices: 52.4 us -> 74 us
  blocking collectives: 19.5 us -> 0 us
  starting transfers between devices: 19.2 us -> 24.3 us
  local copies, waits for them, and re-layouts: 31.2 us -> 34.5 us
    ppermute x0 -> x3, waiting for transfers between devices: none -> 21.6 us  [rows_by_permutes(): lax.ppermute(outgoing, 'head', [(i, (i + d) % count) for i in range(count)])]
    all_to_all x1 -> x0, blocking collectives: 19.5 us -> none  [local(): lax.all_to_all(linear_heads, 'head', split_axis=0, concat_axis=1, tiled=T...]
    ppermute x0 -> x3, starting transfers between devices: none -> 5.04 us  [rows_by_permutes(): lax.ppermute(outgoing, 'head', [(i, (i + d) % count) for i in range(count)])]
    dynamic_slice x0 -> x3, local copies, waits for them, and re-layouts: none -> 2.11 us  [the longest x2 1.96 us: rows_by_permutes(): pieces = [lax.dynamic_slice_in_dim(block, mine * share, share, 0)]]
    unnamed x62 -> x70, local copies, waits for them, and re-layouts: 15.2 us -> 17.3 us
  transfers between devices with their start and end apart: 11 -> 14, of which waited for: 6 -> 9; matrix products, arithmetic and copies ran while one was open for 33% -> 32% of each run, Pallas kernels for 0% -> 0%
where the time goes in v13:
time: 189 us; the launch traced here: 188 us
  waiting for transfers between devices  74 us (39%)
  local copies, waits for them, and re-layouts  34.5 us (18%)
  starting transfers between devices  24.3 us (13%)
  other arithmetic  22 us (12%)
  matrix products  18.9 us (10%)
  between operations  14.9 us (8%)
    ppermute x2, waiting for transfers between devices, passed_along(): return lax.ppermute(block, axis, route)  28.7 us
    ppermute x3, waiting for transfers between devices, rows_by_permutes(): lax.ppermute(outgoing, 'head', [(i, (i + d) % count) for i in range(count)])  21.6 us
    ppermute x3, waiting for transfers between devices, carry_in(): lax.ppermute(mine, 'cy', [(i, i + d) for i in range(columns) if i + d < c...  19.5 us
    unnamed x70, local copies, waits for them, and re-layouts  17.3 us
    ppermute x2, starting transfers between devices, passed_along(): return lax.ppermute(block, axis, route)  7.66 us
    ppermute x3, starting transfers between devices, carry_in(): lax.ppermute(mine, 'cy', [(i, i + d) for i in range(columns) if i + d < c...  6.81 us
    dot_general x2, matrix products, block_output(): jnp.einsum('htj,jhd->thd', mixing, values_blk, preferred_element_type=jnp...  6.28 us
    dot_general x2, matrix products, attend(): jnp.einsum('htkj,kjhd->thd', weights, values_sel, preferred_element_type=...  5.81 us
  transfers between devices with their start and end apart: 14, of which 9 were waited for; matrix products, arithmetic and copies ran while one was open for 32% of the time, Pallas kernels for 0%

profile of v13, /device:TPU:8, one launch (start us, length us, event | category | flops | bytes accessed | tf_op | source)
XLA Modules:
  0.0 188.5 jit_solution(10363624073206063180)
XLA Ops:
  7.2 3.8 %collective-permute-start.6 = (bf16[256,2048]{1,0:T(8,128)(2,1)}, bf16[256,2048]{1,0:T(8,128)(2,1)}, u32[]{:S(2)}, u32[]{:S(2)}) collective-permute-start(bf16[256,2048]{1,0:T(8,128)(2,1)} %param.16), channel_id=1, source_target_pairs={{0,8},{4,12},{8,16},{12,20},{16,24},{20,28},{24,32},{28,36},{32,40... | collective-permute-start | bytes 3145736 | tf_op jit(solution)/shard_map/ppermute | solution.py:21
  11.1 3.8 %collective-permute-start.4 = (bf16[256,2048]{1,0:T(8,128)(2,1)}, bf16[256,2048]{1,0:T(8,128)(2,1)}, u32[]{:S(2)}, u32[]{:S(2)}) collective-permute-start(bf16[256,2048]{1,0:T(8,128)(2,1)} %param.17), channel_id=1, source_target_pairs={{0,8},{4,12},{8,16},{12,20},{16,24},{20,28},{24,32},{28,36},{32,40... | collective-permute-start | bytes 3145736 | tf_op jit(solution)/shard_map/ppermute | solution.py:21
  17.4 1.5 fusion.82
  30.1 1.4 fusion.78
  37.6 1.5 collective-permute-done.6
  39.2 3.0 %broadcast_select_fusion = (bf16[256,2048]{1,0:T(8,128)(2,1)}, bf16[768,2048]{1,0:T(8,128)(2,1)S(1)}) fusion(bf16[256,2048]{1,0:T(8,128)(2,1)} %param.16, bf16[256,2048]{1,0:T(8,128)(2,1)} %collective-permute-done.6, pred[]{:T(512)S(6)} %eq.41), kind=kLoop, calls=%fused_computation.67 | loop fusion | flops 524287 | bytes 4194305 | tf_op jit(solution)/shard_map/jit(_where)/select_n | solution.py:195
  42.2 3.1 %convolution_bitcast_fusion.3 = f32[128,16,128]{2,0,1:T(8,128)} fusion(bf16[128,16,128]{0,2,1:T(8,128)(2,1)} %bitcast.199, bf16[128,16,128]{0,2,1:T(8,128)(2,1)} %bitcast.202, bf16[128,16,128]{0,2,1:T(8,128)(2,1)} %bitcast.197, f32[16,128]{1,0:T(8,128)S(1)} %get-tuple-element.68, pred[128,128]{1,0:T(8,128)(4,1)S(1)} %iota_compare_fusion), kind=kOutput, calls=%fused_computation.42 | convolution fusion | flops 135528448 | bytes 2646016 | tf_op jit(solution)/shard_map/htj,jhd->thd/dot_general | solution.py:48
  45.4 27.1 %collective-permute-done.4 = bf16[256,2048]{1,0:T(8,128)(2,1)} collective-permute-done((bf16[256,2048]{1,0:T(8,128)(2,1)}, bf16[256,2048]{1,0:T(8,128)(2,1)}, u32[]{:S(2)}, u32[]{:S(2)}) %collective-permute-start.4) | collective-permute-done | bytes 1048608 | tf_op jit(solution)/shard_map/ppermute | solution.py:21
  72.5 2.1 %broadcast_select_fusion.1 = (bf16[256,2048]{1,0:T(8,128)(2,1)S(1)}, bf16[768,2048]{1,0:T(8,128)(2,1)S(1)}) fusion(bf16[256,2048]{1,0:T(8,128)(2,1)} %param.17, bf16[256,2048]{1,0:T(8,128)(2,1)} %collective-permute-done.4, pred[]{:T(512)S(6)} %eq.41), kind=kLoop, calls=%fused_computation.68 | loop fusion | flops 524287 | bytes 4194305 | tf_op jit(solution)/shard_map/jit(_where)/select_n | solution.py:195
  78.9 1.8 slice_bitcast_fusion.3
  88.2 2.8 %fusion.31 = bf16[128,16,128]{2,0,1:T(8,128)(2,1)S(1)} fusion(f32[16,5,128,128]{3,2,1,0:T(8,128)S(1)} %get-tuple-element.84, f32[16,128]{1,0:T(8,128)S(1)} %fusion, f32[16,128]{1,0:T(8,128)S(1)} %get-tuple-element.83, pred[128,5,128]{0,2,1:T(8,128)(4,1)S(1)} %get-tuple-element.58, bf16[5,128,16,128]{3,2,1,0:T(8,128)(2,1)S(1)} %bitcast.193), kind=kOutput, calls=%fused_computation.48 | convolution fusion | flops 342360064 | bytes 8486912 | tf_op jit(solution)/shard_map/htkj,kjhd->thd/dot_general | solution.py:184
  91.0 3.0 %fusion.34 = bf16[128,16,128]{2,0,1:T(8,128)(2,1)S(1)} fusion(f32[16,5,128,128]{3,2,1,0:T(8,128)S(1)} %get-tuple-element.82, f32[16,128]{1,0:T(8,128)S(1)} %fusion.1, f32[16,128]{1,0:T(8,128)S(1)} %get-tuple-element.81, pred[128,5,128]{0,2,1:T(8,128)(4,1)S(1)} %get-tuple-element.59, bf16[5,128,16,128]{3,2,1,0:T(8,128)(2,1)S(1)} %bitcast.194), kind=kOutput, calls=%fused_computation.49 | convolution fusion | flops 342360064 | bytes 8486912 | tf_op jit(solution)/shard_map/htkj,kjhd->thd/dot_general | solution.py:184
  96.1 4.3 %all-to-all-start = ((bf16[4,64,2048]{2,1,0:T(8,128)(2,1)}), bf16[4,64,2048]{2,1,0:T(8,128)(2,1)S(1)}, u32[]{:S(2)}, u32[]{:S(2)}) async-start(bf16[4,64,2048]{2,1,0:T(8,128)(2,1)} %all_to_all.14), calls=%async_computation | async-start | bytes 2097152 | tf_op jit(solution)/shard_map/all_to_all | solution.py:257
  100.4 2.8 %all-gather.3.cloned.1.call-done = f32[64,136,128]{2,1,0:T(8,128)} async-done(((f32[8,136,128]{2,1,0:T(8,128)}), f32[64,136,128]{2,1,0:T(8,128)}) %all-gather.3.cloned.1.call-update) | async-done | bytes 4456464 | tf_op jit(solution)/shard_map/all_gather | solution.py:110
  104.6 3.1 %multiply_reduce_fusion.1 = (f32[8,128,128]{2,1,0:T(8,128)S(1)}, f32[8,128,128]{2,1,0:T(8,128)S(1)}) fusion(f32[8,8,136,128]{3,2,1,0:T(8,128)} %bitcast.191, f32[8,8]{1,0:T(8,128)S(1)} %get-tuple-element.79, f32[8,8]{1,0:T(8,128)S(1)} %get-tuple-element.80), kind=kLoop, calls=%fused_computation.9 | loop fusion | flops 3932160 | bytes 5243392 | tf_op jit(solution)/shard_map/reduce_sum | solution.py:79
  108.6 1.5 collective-permute-start.1
  110.1 3.4 %collective-permute-start.2 = (f32[8,136,128]{2,1,0:T(8,128)}, f32[8,136,128]{2,1,0:T(8,128)}, u32[]{:S(2)}, u32[]{:S(2)}) collective-permute-start(f32[8,136,128]{2,1,0:T(8,128)} %pad_maximum_fusion.3), channel_id=1, source_target_pairs={{0,128},{64,192},{1,129},{65,193},{2,130},{66,194},{3,131},{67,195... | collective-permute-start | bytes 1671176 | tf_op jit(solution)/shard_map/ppermute | solution.py:120
  113.5 1.9 %collective-permute-start.3 = (f32[8,136,128]{2,1,0:T(8,128)}, f32[8,136,128]{2,1,0:T(8,128)}, u32[]{:S(2)}, u32[]{:S(2)}) collective-permute-start(f32[8,136,128]{2,1,0:T(8,128)} %pad_maximum_fusion.3), channel_id=1, source_target_pairs={{0,64},{64,128},{128,192},{1,65},{65,129},{129,193},{2,66},{66,130... | collective-permute-start | bytes 1671176 | tf_op jit(solution)/shard_map/ppermute | solution.py:120
  115.4 1.3 fusion.22
  116.8 3.1 %convolution_bitcast_fusion.1 = f32[128,16,128]{2,0,1:T(8,128)} fusion(bf16[128,16,128]{0,2,1:T(8,128)(2,1)} %bitcast.205, bf16[128,16,128]{0,2,1:T(8,128)(2,1)S(1)} %bitcast.200, bf16[128,16,128]{0,2,1:T(8,128)(2,1)} %bitcast.207, f32[16,128]{1,0:T(8,128)S(1)} %get-tuple-element.69, pred[128,128]{1,0:T(8,128)(4,1)S(1)} %iota_compare_fusion), kind=kOutput, calls=%fused_computation.38 | convolution fusion | flops 135528448 | bytes 2646016 | tf_op jit(solution)/shard_map/htj,jhd->thd/dot_general | solution.py:48
  121.0 3.8 %collective-permute-done.2 = f32[8,136,128]{2,1,0:T(8,128)} collective-permute-done((f32[8,136,128]{2,1,0:T(8,128)}, f32[8,136,128]{2,1,0:T(8,128)}, u32[]{:S(2)}, u32[]{:S(2)}) %collective-permute-start.2) | collective-permute-done | bytes 557088 | tf_op jit(solution)/shard_map/ppermute | solution.py:120
  124.8 15.7 %collective-permute-done.3 = f32[8,136,128]{2,1,0:T(8,128)} collective-permute-done((f32[8,136,128]{2,1,0:T(8,128)}, f32[8,136,128]{2,1,0:T(8,128)}, u32[]{:S(2)}, u32[]{:S(2)}) %collective-permute-start.3) | collective-permute-done | bytes 557088 | tf_op jit(solution)/shard_map/ppermute | solution.py:120
  143.4 1.7 multiply_add_fusion
  145.6 1.4 collective-permute-done.8
  147.1 1.5 multiply_reduce_fusion.2
  149.9 1.8 constant_dynamic-slice_fusion
  151.7 1.5 collective-permute-start.11
  153.2 1.7 collective-permute-start.9
  155.0 1.8 collective-permute-start.10
  157.2 9.8 %collective-permute-done.11 = bf16[64,2048]{0,1:T(8,128)(2,1)S(1)} collective-permute-done((bf16[64,2048]{0,1:T(8,128)(2,1)}, bf16[64,2048]{0,1:T(8,128)(2,1)S(1)}, u32[]{:S(2)}, u32[]{:S(2)}) %collective-permute-start.11) | collective-permute-done | bytes 262176 | tf_op jit(solution)/shard_map/ppermute | solution.py:235
  168.3 11.0 %collective-permute-done.10 = bf16[64,2048]{0,1:T(8,128)(2,1)S(1)} collective-permute-done((bf16[64,2048]{0,1:T(8,128)(2,1)}, bf16[64,2048]{0,1:T(8,128)(2,1)S(1)}, u32[]{:S(2)}, u32[]{:S(2)}) %collective-permute-start.10) | collective-permute-done | bytes 262176 | tf_op jit(solution)/shard_map/ppermute | solution.py:235
  180.0 1.6 copy.327
  (155 shorter events, 43.5 us)
Async XLA Ops:
  7.2 7.7 %copy-start = (f32[16,256]{1,0:T(8,128)S(1)}, f32[16,256]{1,0:T(8,128)}, u32[]{:S(2)}) copy-start(f32[16,256]{1,0:T(8,128)} %param.13) | copy-start | bytes 49156
  7.2 96.1 %all-gather.3.cloned.1.call-start = ((), (), s32[]{:S(2)}) async-start(), calls=%async_computation.1 | async-start | bytes 5013504 | tf_op jit(solution)/shard_map/all_gather | solution.py:110
  7.2 31.9 %collective-permute-start.6 = (bf16[256,2048]{1,0:T(8,128)(2,1)}, bf16[256,2048]{1,0:T(8,128)(2,1)}, u32[]{:S(2)}, u32[]{:S(2)}) collective-permute-start(bf16[256,2048]{1,0:T(8,128)(2,1)} %param.16), channel_id=1, source_target_pairs={{0,8},{4,12},{8,16},{12,20},{16,24},{20,28},{24,32},{28,36},{32,40... | collective-permute-start | bytes 3145736 | tf_op jit(solution)/shard_map/ppermute | solution.py:21
  11.1 61.4 %collective-permute-start.4 = (bf16[256,2048]{1,0:T(8,128)(2,1)}, bf16[256,2048]{1,0:T(8,128)(2,1)}, u32[]{:S(2)}, u32[]{:S(2)}) collective-permute-start(bf16[256,2048]{1,0:T(8,128)(2,1)} %param.17), channel_id=1, source_target_pairs={{0,8},{4,12},{8,16},{12,20},{16,24},{20,28},{24,32},{28,36},{32,40... | collective-permute-start | bytes 3145736 | tf_op jit(solution)/shard_map/ppermute | solution.py:21
  17.4 3.9 %copy-start.8 = (bf16[128,2048]{0,1:T(8,128)(2,1)}, bf16[128,2048]{0,1:T(8,128)(2,1)S(1)}, u32[]{:S(2)}) copy-start(bf16[128,2048]{0,1:T(8,128)(2,1)S(1)} %copy.351) | copy-start | bytes 1572868
  19.1 2.2 %copy-start.9 = (bf16[128,2048]{0,1:T(8,128)(2,1)}, bf16[128,2048]{0,1:T(8,128)(2,1)S(1)}, u32[]{:S(2)}) copy-start(bf16[128,2048]{0,1:T(8,128)(2,1)S(1)} %copy.352) | copy-start | bytes 1572868
  19.4 3.3 %copy-start.12 = (bf16[128,2048]{0,1:T(8,128)(2,1)}, bf16[128,2048]{0,1:T(8,128)(2,1)S(1)}, u32[]{:S(2)}) copy-start(bf16[128,2048]{0,1:T(8,128)(2,1)S(1)} %copy.355) | copy-start | bytes 1572868
  19.7 4.2 %copy-start.13 = (bf16[128,2048]{0,1:T(8,128)(2,1)}, bf16[128,2048]{0,1:T(8,128)(2,1)S(1)}, u32[]{:S(2)}) copy-start(bf16[128,2048]{0,1:T(8,128)(2,1)S(1)} %copy.354) | copy-start | bytes 1572868
  21.3 2.7 %copy-start.21 = (s32[2]{0:T(128)S(1)}, s32[2]{0:T(128)}, u32[]{:S(2)}) copy-start(s32[2]{0:T(128)} %param.19) | copy-start | bytes 28
  21.3 4.6 %copy-start.22 = (s32[2,5]{1,0:T(2,128)S(1)}, s32[2,5]{1,0:T(2,128)}, u32[]{:S(2)}) copy-start(s32[2,5]{1,0:T(2,128)} %param.18) | copy-start | bytes 124
  23.9 5.1 %collective-permute-start = (f32[16,136,128]{2,1,0:T(8,128)}, f32[16,136,128]{2,1,0:T(8,128)}, u32[]{:S(2)}, u32[]{:S(2)}) collective-permute-start(f32[16,136,128]{2,1,0:T(8,128)} %pad_maximum_fusion), channel_id=1, source_target_pairs={{0,4},{4,0},{1,5},{5,1},{2,6},{6,2},{3,7},{7,3},{8,12},{12,8},{9,1... | collective-permute-start | bytes 3342344 | tf_op jit(solution)/shard_map/ppermute | solution.py:88
  42.2 32.7 %collective-permute-start.7 = (bf16[256,2048]{1,0:T(8,128)(2,1)}, bf16[256,2048]{1,0:T(8,128)(2,1)}, u32[]{:S(2)}, u32[]{:S(2)}) collective-permute-start(bf16[256,2048]{1,0:T(8,128)(2,1)} %get-tuple-element.50), channel_id=1, source_target_pairs={{0,4},{4,0},{1,5},{5,1},{2,6},{6,2},{3,7},{7,3},{8,12},{12,8},{9,1... | collective-permute-start | bytes 3145736 | tf_op jit(solution)/shard_map/ppermute | solution.py:88
  45.4 30.9 %copy-start.4 = (bf16[256,2048]{1,0:T(8,128)(2,1)S(1)}, bf16[256,2048]{1,0:T(8,128)(2,1)}, u32[]{:S(2)}) copy-start(bf16[256,2048]{1,0:T(8,128)(2,1)} %param.16) | copy-start | bytes 3145732
  74.6 3.8 %collective-permute-start.5 = (bf16[256,2048]{1,0:T(8,128)(2,1)S(1)}, bf16[256,2048]{1,0:T(8,128)(2,1)S(1)}, u32[]{:S(2)}, u32[]{:S(2)}) collective-permute-start(bf16[256,2048]{1,0:T(8,128)(2,1)S(1)} %get-tuple-element.48), channel_id=1, source_target_pairs={{0,4},{4,0},{1,5},{5,1},{2,6},{6,2},{3,7},{7,3},{8,12},{12,8},{9,1... | collective-permute-start | bytes 3145736 | tf_op jit(solution)/shard_map/ppermute | solution.py:88
  96.1 23.8 %all-to-all-start = ((bf16[4,64,2048]{2,1,0:T(8,128)(2,1)}), bf16[4,64,2048]{2,1,0:T(8,128)(2,1)S(1)}, u32[]{:S(2)}, u32[]{:S(2)}) async-start(bf16[4,64,2048]{2,1,0:T(8,128)(2,1)} %all_to_all.14), calls=%async_computation | async-start | bytes 2097152 | tf_op jit(solution)/shard_map/all_to_all | solution.py:257
  104.6 10.9 %copy-start.11 = (bf16[128,2048]{0,1:T(8,128)(2,1)S(1)}, bf16[128,2048]{0,1:T(8,128)(2,1)}, u32[]{:S(2)}) copy-start(bf16[128,2048]{0,1:T(8,128)(2,1)} %copy.350) | copy-start | bytes 1572868
  104.6 10.9 %copy-start.16 = (f32[128,16,128]{2,0,1:T(8,128)S(1)}, f32[128,16,128]{2,0,1:T(8,128)}, u32[]{:S(2)}) copy-start(f32[128,16,128]{2,0,1:T(8,128)} %convolution_bitcast_fusion.3) | copy-start | bytes 3145732
  107.7 9.1 %copy-start.10 = (bf16[128,2048]{0,1:T(8,128)(2,1)S(1)}, bf16[128,2048]{0,1:T(8,128)(2,1)}, u32[]{:S(2)}) copy-start(bf16[128,2048]{0,1:T(8,128)(2,1)} %copy.353) | copy-start | bytes 1572868
  108.6 12.4 %collective-permute-start.1 = (f32[8,136,128]{2,1,0:T(8,128)}, f32[8,136,128]{2,1,0:T(8,128)}, u32[]{:S(2)}, u32[]{:S(2)}) collective-permute-start(f32[8,136,128]{2,1,0:T(8,128)} %pad_maximum_fusion.3), channel_id=1, source_target_pairs={{0,192},{1,193},{2,194},{3,195},{4,196},{5,197},{6,198},{7,199},{8... | collective-permute-start | bytes 1671176 | tf_op jit(solution)/shard_map/ppermute | solution.py:120
  110.1 14.7 %collective-permute-start.2 = (f32[8,136,128]{2,1,0:T(8,128)}, f32[8,136,128]{2,1,0:T(8,128)}, u32[]{:S(2)}, u32[]{:S(2)}) collective-permute-start(f32[8,136,128]{2,1,0:T(8,128)} %pad_maximum_fusion.3), channel_id=1, source_target_pairs={{0,128},{64,192},{1,129},{65,193},{2,130},{66,194},{3,131},{67,195... | collective-permute-start | bytes 1671176 | tf_op jit(solution)/shard_map/ppermute | solution.py:120
  113.5 26.9 %collective-permute-start.3 = (f32[8,136,128]{2,1,0:T(8,128)}, f32[8,136,128]{2,1,0:T(8,128)}, u32[]{:S(2)}, u32[]{:S(2)}) collective-permute-start(f32[8,136,128]{2,1,0:T(8,128)} %pad_maximum_fusion.3), channel_id=1, source_target_pairs={{0,64},{64,128},{128,192},{1,65},{65,129},{129,193},{2,66},{66,130... | collective-permute-start | bytes 1671176 | tf_op jit(solution)/shard_map/ppermute | solution.py:120
  116.8 28.5 %copy-start.3 = (f32[16,128,128]{2,1,0:T(8,128)S(1)}, f32[16,128,128]{2,1,0:T(8,128)}, u32[]{:S(2)}) copy-start(f32[16,128,128]{2,1,0:T(8,128)} %copy-done.2) | copy-start | bytes 3145732
  119.9 25.3 %copy-start.14 = (f32[128,16,128]{2,0,1:T(8,128)S(1)}, f32[128,16,128]{2,0,1:T(8,128)}, u32[]{:S(2)}) copy-start(f32[128,16,128]{2,0,1:T(8,128)} %convolution_bitcast_fusion.1) | copy-start | bytes 3145732
  143.3 3.7 %copy-start.7 = (f32[16,128,128]{2,1,0:T(8,128)S(1)}, f32[16,128,128]{2,1,0:T(8,128)}, u32[]{:S(2)}) copy-start(f32[16,128,128]{2,1,0:T(8,128)} %copy-done.6) | copy-start | bytes 3145732
  143.3 3.7 %copy-start.15 = (bf16[256,2048]{1,0:T(8,128)(2,1)S(1)}, bf16[256,2048]{1,0:T(8,128)(2,1)}, u32[]{:S(2)}) copy-start(bf16[256,2048]{1,0:T(8,128)(2,1)} %param.10) | copy-start | bytes 3145732
  143.3 3.7 %copy-start.17 = (f32[128,16,128]{2,0,1:T(8,128)S(1)}, f32[128,16,128]{2,0,1:T(8,128)}, u32[]{:S(2)}) copy-start(f32[128,16,128]{2,0,1:T(8,128)} %fusion.22) | copy-start | bytes 3145732
  145.1 2.0 %collective-permute-start.8 = (f32[8,128,128]{2,1,0:T(8,128)S(1)}, f32[8,128,128]{2,1,0:T(8,128)S(1)}, u32[]{:S(2)}, u32[]{:S(2)}) collective-permute-start(f32[8,128,128]{2,1,0:T(8,128)S(1)} %multiply_add_fusion), channel_id=1, source_target_pairs={{0,4},{4,0},{1,5},{5,1},{2,6},{6,2},{3,7},{7,3},{8,12},{12,8},{9,1... | collective-permute-start | bytes 1572872 | tf_op jit(solution)/shard_map/ppermute | solution.py:88
  147.1 1.6 copy-start.20
  151.7 15.4 %collective-permute-start.11 = (bf16[64,2048]{0,1:T(8,128)(2,1)}, bf16[64,2048]{0,1:T(8,128)(2,1)S(1)}, u32[]{:S(2)}, u32[]{:S(2)}) collective-permute-start(bf16[64,2048]{0,1:T(8,128)(2,1)} %get-tuple-element.43), channel_id=1, source_target_pairs={{0,1},{1,2},{2,3},{3,0},{4,5},{5,6},{6,7},{7,4},{8,9},{9,10},{10,1... | collective-permute-start | bytes 786440 | tf_op jit(solution)/shard_map/ppermute | solution.py:235
  153.2 15.0 %collective-permute-start.9 = (bf16[64,2048]{0,1:T(8,128)(2,1)}, bf16[64,2048]{0,1:T(8,128)(2,1)S(1)}, u32[]{:S(2)}, u32[]{:S(2)}) collective-permute-start(bf16[64,2048]{0,1:T(8,128)(2,1)} %get-tuple-element.45), channel_id=1, source_target_pairs={{0,3},{1,0},{2,1},{3,2},{4,7},{5,4},{6,5},{7,6},{8,11},{9,8},{10,9... | collective-permute-start | bytes 786440 | tf_op jit(solution)/shard_map/ppermute | solution.py:235
  155.0 24.4 %collective-permute-start.10 = (bf16[64,2048]{0,1:T(8,128)(2,1)}, bf16[64,2048]{0,1:T(8,128)(2,1)S(1)}, u32[]{:S(2)}, u32[]{:S(2)}) collective-permute-start(bf16[64,2048]{0,1:T(8,128)(2,1)} %get-tuple-element.44), channel_id=1, source_target_pairs={{0,2},{1,3},{2,0},{3,1},{4,6},{5,7},{6,4},{7,5},{8,10},{9,11},{10,... | collective-permute-start | bytes 786440 | tf_op jit(solution)/shard_map/ppermute | solution.py:235
  179.8 1.9 copy-start.1
  (5 other events, 5.6 us)
Sparse Core Ops, SparseCore 0:
  33.6 69.5 all-gather.2
